TPU v7x, 128 devices: a whole 4x4x4 slice. The times are simulated.
128 devices in a mesh: row: 8 (over z, x_hi), col: 16 (over x_lo, y, core).
Axes of the slice: x: 4 (x_hi: 2, x_lo: 2; x = x_hi * 2 + x_lo), y: 4, z: 4, core: 2. Of those that a mesh axis runs over, the one named last changes fastest.
Arguments:
- tokens: bfloat16 [512, 8192], P('row', 'col'), may hold values from -6 to 6
- gate_weight: bfloat16 [8192, 28672], P('col', 'row'), may hold values from -0.09375 to 0.09375
- up_weight: bfloat16 [8192, 28672], P('col', 'row'), may hold values from -0.09375 to 0.09375
- down_weight: bfloat16 [28672, 8192], P('row', 'col'), may hold values from -0.046875 to 0.046875
- gate_keep: int32 [64, 224], P('col', 'row'), may hold values from 0 to 1, as said below
- up_keep: int32 [64, 224], P('col', 'row'), may hold values from 0 to 1, as said below
- down_keep: int32 [224, 64], P('row', 'col'), may hold values from 0 to 1, as said below
Outputs:
- mixed: bfloat16 [512, 8192], P('row', 'col')
Inputs may be any that keep to these rules, and one draw needn't show every extreme that they name: `gate_keep`: 1 keeps the block, 0 drops it; the kept share differs between regions of blocks. `up_keep`: 1 keeps the block, 0 drops it; the kept share differs between regions of blocks. `down_keep`: 1 keeps the block, 0 drops it; the kept share differs between regions of blocks.
All inputs are finite; a program needn't handle non-finite values.
Results may differ from a plain program's by a relative error of at most 0.0049.
Values may be sent and summed in bfloat16 or wider, within the bound.
No kernel may reach another device: no remote copies, remote signals or barrier semaphores. Data moves between devices by JAX's collectives and lax.ppermute only.
A program may use at most 128 MiB of HBM per device.

v0:
```python
import jax
import jax.numpy as jnp
from jax import lax
from jax.sharding import PartitionSpec as P


def expand(weight, keep):
    nrow, ncol = keep.shape
    rows, cols = weight.shape
    masked = (
        weight.reshape(nrow, rows // nrow, ncol, cols // ncol)
        * keep.astype(jnp.bfloat16)[:, None, :, None]
    )
    return masked.reshape(rows, cols)


def on_device(tokens, gate_weight, up_weight, down_weight, gate_keep, up_keep, down_keep):
    paired = jnp.concatenate([expand(gate_weight, gate_keep), expand(up_weight, up_keep)], axis=1)
    down_mat = expand(down_weight, down_keep)
    hidden_cols = gate_weight.shape[1]
    features = lax.all_gather(tokens, "row", axis=0, tiled=True)
    partial_pair = jnp.dot(features, paired, preferred_element_type=jnp.float32)
    summed = lax.psum(partial_pair, "col")
    hidden = (jax.nn.silu(summed[:, :hidden_cols]) * summed[:, hidden_cols:]).astype(jnp.bfloat16)
    partial_out = jnp.dot(hidden, down_mat, preferred_element_type=jnp.float32)
    return lax.psum_scatter(partial_out, "row", scatter_dimension=0, tiled=True).astype(
        jnp.bfloat16
    )


def solution(mesh):
    placed = (
        P("row", "col"),
        P("col", "row"),
        P("col", "row"),
        P("row", "col"),
        P("col", "row"),
        P("col", "row"),
        P("row", "col"),
    )
    return jax.shard_map(
        on_device, mesh=mesh, in_specs=placed, out_specs=P("row", "col"), check_vma=False
    )
```

profile of v0, /device:TPU:0, one launch (start us, length us, event | category | flops | bytes accessed | tf_op | source)
XLA Modules:
  0.0 342.2 jit_solution(5104603052554754354)
XLA Ops:
  6.5 0.0 all-reduce.2.cloned.1.call-start
  6.5 0.7 convert_element_type.15
  7.2 0.1 copy.9
  7.3 0.7 convert_element_type.16
  8.0 0.1 copy.11
  8.1 5.9 %copy.10 = bf16[512,3584]{0,1:T(8,128)(2,1)} copy(bf16[512,3584]{1,0:T(8,128)(2,1)} %param.8) | data formatting | bytes 7340032 | tf_op args[1]
  14.1 0.0 copy-start.2
  14.1 6.0 %copy.12 = bf16[512,3584]{0,1:T(8,128)(2,1)} copy(bf16[512,3584]{1,0:T(8,128)(2,1)} %param.9) | data formatting | bytes 7340032 | tf_op args[2]
  20.0 0.0 copy-done.2
  20.0 37.0 %all_gather.3 = bf16[512,512]{1,0:T(8,128)(2,1)S(1)} all-gather(bf16[64,512]{1,0:T(8,128)(2,1)S(1)} %copy-done.2), channel_id=1, replica_groups=mesh['row'=8,'col'=16] {'row'}, dimensions={0}, use_global_device_ids=true | all-gather | bytes 589824 | tf_op jit(solution)/shard_map/all_gather | solution.py:21
  57.1 0.0 copy-start
  57.1 0.0 copy-start.1
  57.1 1.0 mul.40
  58.1 1.0 mul.43
  59.1 0.0 copy-done
  59.1 1.1 copy-done.1
  60.2 1.5 bitcast_multiply_fusion.2
  61.8 12.7 %convolution_bitcast_fusion = f32[512,7168]{0,1:T(8,128)} fusion(bf16[512,512]{1,0:T(8,128)(2,1)S(1)} %all_gather.3, bf16[512,3584]{0,1:T(8,128)(2,1)S(1)} %get-tuple-element.5, bf16[512,3584]{0,1:T(8,128)(2,1)S(1)} %get-tuple-element.6), kind=kOutput, calls=%fused_computation | convolution fusion | flops 3772776448 | bytes 22544384 | tf_op jit(solution)/shard_map/dot_general | solution.py:22
  74.4 0.0 copy-start.3
  74.4 0.0 all-reduce.2.cloned.1.call-update
  74.5 0.0 reduce-scatter.2.cloned.1.call-start
  74.5 0.6 copy-done.3
  75.1 0.1 copy.13
  75.2 177.1 %all-reduce.2.cloned.1.call-done = f32[512,7168]{0,1:T(8,128)} async-done(((f32[512,7168]{0,1:T(8,128)}), f32[512,7168]{0,1:T(8,128)}) %all-reduce.2.cloned.1.call-update) | async-done | bytes 14680080 | tf_op jit(solution)/shard_map/psum | solution.py:23
  252.3 0.0 copy-start.4
  252.3 1.0 mul.48
  253.3 1.0 copy-done.4
  254.4 7.6 %fusion.4 = f32[512,512]{1,0:T(8,128)} fusion(bf16[3584,512]{1,0:T(8,128)(2,1)S(1)} %copy-done.4, bf16[448,8,4,128]{3,2,1,0:T(4,128)(2,1)S(1)} %bitcast.22, f32[512,7168]{0,1:T(8,128)} %all-reduce.2.cloned.1.call-done), kind=kOutput, calls=%fused_computation.7 | convolution fusion | flops 1891893248 | bytes 23068672 | tf_op jit(solution)/shard_map/dot_general | solution.py:25
  262.0 0.0 reduce-scatter.2.cloned.1.call-update
  262.0 71.8 %reduce-scatter.2.cloned.1.call-done = f32[64,512]{1,0:T(8,128)} async-done(((f32[512,512]{1,0:T(8,128)}), f32[64,512]{1,0:T(8,128)}) %reduce-scatter.2.cloned.1.call-update) | async-done | bytes 131088 | tf_op jit(solution)/shard_map/reduce_scatter | solution.py:26
  333.8 1.5 convert_element_type.19
  (1 shorter events, 0.0 us)
Async XLA Ops:
  6.5 245.8 %all-reduce.2.cloned.1.call-start = ((), (), s32[]{:S(2)}) async-start(), calls=%async_computation.1 | async-start | bytes 29360128 | tf_op jit(solution)/shard_map/psum | solution.py:23
  14.1 6.0 %copy-start.2 = (bf16[64,512]{1,0:T(8,128)(2,1)S(1)}, bf16[64,512]{1,0:T(8,128)(2,1)}, u32[]{:S(2)}) copy-start(bf16[64,512]{1,0:T(8,128)(2,1)} %param.7) | copy-start | bytes 196612
  57.1 2.0 copy-start
  57.1 3.2 copy-start.1
  74.4 0.7 copy-start.3
  74.5 259.3 %reduce-scatter.2.cloned.1.call-start = ((), (), s32[]{:S(2)}) async-start(), calls=%async_computation.2 | async-start | bytes 1179648 | tf_op jit(solution)/shard_map/reduce_scatter | solution.py:26
  252.3 2.0 copy-start.4
Sparse Core Ops, SparseCore 0:
  74.6 177.6 all-reduce.1
  262.1 71.6 reduce-scatter.1
where the time goes:
time: 343 us; the launch traced here: 342 us
  waiting for transfers between devices  249 us (73%)
  blocking collectives  37 us (11%)
  matrix products  20.3 us (6%)
  local copies, waits for them, and re-layouts  18 us (5%)
  between operations  13.4 us (4%)
  other arithmetic  4.45 us (1%)
    psum x1, waiting for transfers between devices, on_device(): summed = lax.psum(partial_pair, 'col')  177 us
    reduce_scatter x1, waiting for transfers between devices, on_device(): lax.psum_scatter(partial_out, 'row', scatter_dimension=0, tiled=True)  71.8 us
    all_gather x1, blocking collectives, on_device(): features = lax.all_gather(tokens, 'row', axis=0, tiled=True)  37 us
    unnamed x12, local copies, waits for them, and re-layouts  14.6 us
    dot_general x1, matrix products, on_device(): partial_pair = jnp.dot(features, paired, preferred_element_type=jnp.float32)  12.7 us
    dot_general x1, matrix products, on_device(): partial_out = jnp.dot(hidden, down_mat, preferred_element_type=jnp.float32)  7.61 us
  transfers between devices with their start and end apart: 2, of which 2 were waited for; matrix products, arithmetic and copies ran while one was open for 0% of the time, Pallas kernels for 0%

commit v1 on v0

--- a/solution.py
+++ b/solution.py
@@ -15,14 +15,17 @@
 
 
 def on_device(tokens, gate_weight, up_weight, down_weight, gate_keep, up_keep, down_keep):
-    paired = jnp.concatenate([expand(gate_weight, gate_keep), expand(up_weight, up_keep)], axis=1)
-    down_mat = expand(down_weight, down_keep)
     hidden_cols = gate_weight.shape[1]
     features = lax.all_gather(tokens, "row", axis=0, tiled=True)
-    partial_pair = jnp.dot(features, paired, preferred_element_type=jnp.float32)
-    summed = lax.psum(partial_pair, "col")
+    pg = jnp.dot(features, expand(gate_weight, gate_keep), preferred_element_type=jnp.float32)
+    pu = jnp.dot(features, expand(up_weight, up_keep), preferred_element_type=jnp.float32)
+    pair = jnp.concatenate([pg, pu], axis=1)
+    summed = lax.psum_scatter(pair, "col", scatter_dimension=0, tiled=True)
     hidden = (jax.nn.silu(summed[:, :hidden_cols]) * summed[:, hidden_cols:]).astype(jnp.bfloat16)
-    partial_out = jnp.dot(hidden, down_mat, preferred_element_type=jnp.float32)
+    hidden_all = lax.all_gather(hidden, "col", axis=0, tiled=True)
+    partial_out = jnp.dot(
+        hidden_all, expand(down_weight, down_keep), preferred_element_type=jnp.float32
+    )
     return lax.psum_scatter(partial_out, "row", scatter_dimension=0, tiled=True).astype(
         jnp.bfloat16
     )

time: 343 us -> 303 us (0.88)
  waiting for transfers between devices: 249 us -> 199 us
  local copies, waits for them, and re-layouts: 18 us -> 32.7 us
  matrix products: 20.3 us -> 9.38 us
  other arithmetic: 4.45 us -> 10.3 us
    psum x1 -> x0, waiting for transfers between devices: 177 us -> none  [on_device(): summed = lax.psum(partial_pair, 'col')]
    reduce_scatter x0 -> x1, waiting for transfers between devices: none -> 90.5 us  [on_device(): summed = lax.psum_scatter(pair, 'col', scatter_dimension=0, tiled=True)]
    all_gather x0 -> x1, waiting for transfers between devices: none -> 35.6 us  [on_device(): hidden_all = lax.all_gather(hidden, 'col', axis=0, tiled=True)]
    unnamed x12 -> x13, local copies, waits for them, and re-layouts: 14.6 us -> 29.3 us
    dot_general x2 -> x3, matrix products: 20.3 us -> 9.38 us  [the longest x1 5.17 us: on_device(): jnp.dot(hidden_all, expand(down_weight, down_keep), preferred_element_typ...]
    concatenate x0 -> x1, other arithmetic: none -> 6.11 us  [on_device(): pair = jnp.concatenate([pg, pu], axis=1)]
  transfers between devices with their start and end apart: 2 -> 3, of which waited for: 2 -> 3; matrix products, arithmetic and copies ran while one was open for 0% -> 0% of each run, Pallas kernels for 0% -> 0%
where the time goes in v1:
time: 303 us; the launch traced here: 302 us
  waiting for transfers between devices  199 us (66%)
  blocking collectives  37.3 us (12%)
  local copies, waits for them, and re-layouts  32.7 us (11%)
  between operations  13.2 us (4%)
  other arithmetic  10.3 us (3%)
  matrix products  9.38 us (3%)
    reduce_scatter x1, waiting for transfers between devices, on_device(): summed = lax.psum_scatter(pair, 'col', scatter_dimension=0, tiled=True)  90.5 us
    reduce_scatter x1, waiting for transfers between devices, on_device(): lax.psum_scatter(partial_out, 'row', scatter_dimension=0, tiled=True)  72.8 us
    all_gather x1, blocking collectives, on_device(): features = lax.all_gather(tokens, 'row', axis=0, tiled=True)  37.3 us
    all_gather x1, waiting for transfers between devices, on_device(): hidden_all = lax.all_gather(hidden, 'col', axis=0, tiled=True)  35.6 us
    unnamed x13, local copies, waits for them, and re-layouts  29.3 us
    concatenate x1, other arithmetic, on_device(): pair = jnp.concatenate([pg, pu], axis=1)  6.11 us
  transfers between devices with their start and end apart: 3, of which 3 were waited for; matrix products, arithmetic and copies ran while one was open for 0% of the time, Pallas kernels for 0%

profile of v1, /device:TPU:0, one launch (start us, length us, event | category | flops | bytes accessed | tf_op | source)
XLA Modules:
  0.0 301.8 jit_solution(1548711705113994141)
XLA Ops:
  6.5 0.0 reduce-scatter.7.cloned.1.call-start
  6.5 37.3 %all_gather.6 = bf16[512,512]{1,0:T(8,128)(2,1)S(1)} all-gather(bf16[64,512]{1,0:T(8,128)(2,1)} %param.7), channel_id=1, replica_groups=mesh['row'=8,'col'=16] {'row'}, dimensions={0}, use_global_device_ids=true | all-gather | bytes 589824 | tf_op jit(solution)/shard_map/all_gather | solution.py:19
  43.8 0.7 convert_element_type.16
  44.5 0.1 copy.22
  44.6 0.0 copy-start.2
  44.6 5.9 %copy.23 = bf16[512,3584]{0,1:T(8,128)(2,1)} copy(bf16[512,3584]{1,0:T(8,128)(2,1)} %param.9) | data formatting | bytes 7340032 | tf_op args[2]
  50.5 0.0 copy-done.2
  50.5 0.1 copy.20
  50.7 5.9 %copy.21 = bf16[512,3584]{0,1:T(8,128)(2,1)} copy(bf16[512,3584]{1,0:T(8,128)(2,1)} %param.8) | data formatting | bytes 7340032 | tf_op args[1]
  56.6 0.0 copy-start.1
  56.6 1.0 mul.43
  57.6 1.0 copy-done.1
  58.6 2.1 convolution_bitcast_fusion
  60.7 0.0 copy-start
  60.8 1.0 mul.40
  61.8 1.0 copy-done
  62.8 2.1 convolution_bitcast_fusion.1
  64.9 6.1 %pad_maximum_fusion = f32[512,7168]{0,1:T(8,128)} fusion(f32[512,3584]{0,1:T(8,128)S(1)} %convolution_bitcast_fusion, f32[512,3584]{0,1:T(8,128)S(1)} %convolution_bitcast_fusion.1), kind=kLoop, calls=%fused_computation | loop fusion | flops 3670016 | bytes 29360128 | tf_op jit(solution)/shard_map/concatenate | solution.py:22
  71.0 14.3 %copy.27 = f32[512,7168]{1,0:T(8,128)} copy(f32[512,7168]{0,1:T(8,128)} %pad_maximum_fusion) | data formatting | bytes 29360128
  85.4 0.0 copy-start.3
  85.4 0.0 reduce-scatter.7.cloned.1.call-update
  85.4 0.0 all-gather.2.cloned.1.call-start
  85.4 90.5 %reduce-scatter.7.cloned.1.call-done = f32[32,7168]{1,0:T(8,128)} async-done(((f32[512,7168]{1,0:T(8,128)}), f32[32,7168]{1,0:T(8,128)}) %reduce-scatter.7.cloned.1.call-update) | async-done | bytes 917520 | tf_op jit(solution)/shard_map/reduce_scatter | solution.py:23
  175.9 2.0 fusion.4
  177.9 0.0 all-gather.2.cloned.1.call-update
  177.9 0.0 reduce-scatter.5.cloned.1.call-start
  178.0 0.0 copy-done.3
  178.0 0.1 copy.26
  178.1 35.6 %all-gather.2.cloned.1.call-done = bf16[512,3584]{1,0:T(8,128)(2,1)} async-done(((bf16[32,3584]{1,0:T(8,128)(2,1)}), bf16[512,3584]{1,0:T(8,128)(2,1)}) %all-gather.2.cloned.1.call-update) | async-done | bytes 3670032 | tf_op jit(solution)/shard_map/all_gather | solution.py:25
  213.7 0.0 copy-start.4
  213.7 1.0 mul.48
  214.7 1.0 copy-done.4
  215.8 5.2 %fusion = f32[512,512]{1,0:T(8,128)} fusion(bf16[512,3584]{1,0:T(8,128)(2,1)} %all-gather.2.cloned.1.call-done, bf16[3584,512]{1,0:T(8,128)(2,1)S(1)} %copy-done.4, bf16[448,8,4,128]{3,2,1,0:T(4,128)(2,1)S(1)} %bitcast.29), kind=kOutput, calls=%fused_computation.4 | convolution fusion | flops 1880883200 | bytes 12058624 | tf_op jit(solution)/shard_map/dot_general | solution.py:26
  220.9 0.0 reduce-scatter.5.cloned.1.call-update
  220.9 72.8 %reduce-scatter.5.cloned.1.call-done = f32[64,512]{1,0:T(8,128)} async-done(((f32[512,512]{1,0:T(8,128)}), f32[64,512]{1,0:T(8,128)}) %reduce-scatter.5.cloned.1.call-update) | async-done | bytes 131088 | tf_op jit(solution)/shard_map/reduce_scatter | solution.py:29
  293.7 1.5 convert_element_type.19
  (2 shorter events, 0.0 us)
Async XLA Ops:
  6.5 169.4 %reduce-scatter.7.cloned.1.call-start = ((), (), s32[]{:S(2)}) async-start(), calls=%async_computation.4 | async-start | bytes 15597568 | tf_op jit(solution)/shard_map/reduce_scatter | solution.py:23
  44.6 5.9 %copy-start.2 = (s32[4,28]{1,0:T(4,128)S(1)}, s32[4,28]{1,0:T(4,128)}, u32[]{:S(2)}) copy-start(s32[4,28]{1,0:T(4,128)} %param.11) | copy-start | bytes 1348
  56.6 2.0 copy-start.1
  60.7 2.0 copy-start
  85.4 92.6 %copy-start.3 = (s32[28,4]{0,1:T(4,128)S(1)}, s32[28,4]{0,1:T(4,128)}, u32[]{:S(2)}) copy-start(s32[28,4]{0,1:T(4,128)} %param.13) | copy-start | bytes 1348
  85.4 128.3 %all-gather.2.cloned.1.call-start = ((), (), s32[]{:S(2)}) async-start(), calls=%async_computation.2 | async-start | bytes 3899392 | tf_op jit(solution)/shard_map/all_gather | solution.py:25
  177.9 115.8 %reduce-scatter.5.cloned.1.call-start = ((), (), s32[]{:S(2)}) async-start(), calls=%async_computation.3 | async-start | bytes 1179648 | tf_op jit(solution)/shard_map/reduce_scatter | solution.py:29
  213.7 2.0 copy-start.4
Sparse Core Ops, SparseCore 0:
  85.5 90.3 reduce-scatter.6
  178.1 35.6 all-gather.1
  221.1 72.6 reduce-scatter.4

commit v2 on v1

v2 whole, which is shorter than its diff:
```python
import jax
import jax.numpy as jnp
from jax import lax
from jax.sharding import Mesh
from jax.sharding import PartitionSpec as P

ROW = ("z", "x_hi")
COL = ("x_lo", "y", "core")
CHIPS = ("x_lo", "y")


def expand(weight, keep):
    nrow, ncol = keep.shape
    rows, cols = weight.shape
    masked = (
        weight.reshape(nrow, rows // nrow, ncol, cols // ncol)
        * keep.astype(jnp.bfloat16)[:, None, :, None]
    )
    return masked.reshape(rows, cols)


def on_device(tokens, gate_weight, up_weight, down_weight, gate_keep, up_keep, down_keep):
    hidden_cols = gate_weight.shape[1]
    features = lax.all_gather(tokens, ROW, axis=0, tiled=True)
    pg = jnp.dot(features, expand(gate_weight, gate_keep), preferred_element_type=jnp.float32)
    pu = jnp.dot(features, expand(up_weight, up_keep), preferred_element_type=jnp.float32)
    pair = jnp.concatenate([pg, pu], axis=1)
    on_chip = lax.psum_scatter(pair, "core", scatter_dimension=0, tiled=True)
    summed = lax.psum_scatter(on_chip, CHIPS, scatter_dimension=0, tiled=True)
    hidden = (jax.nn.silu(summed[:, :hidden_cols]) * summed[:, hidden_cols:]).astype(jnp.bfloat16)
    hidden_chip = lax.all_gather(hidden, CHIPS, axis=0, tiled=True)
    hidden_all = lax.all_gather(hidden_chip, "core", axis=0, tiled=True)
    partial_out = jnp.dot(
        hidden_all, expand(down_weight, down_keep), preferred_element_type=jnp.float32
    )
    n_row = partial_out.shape[0] // tokens.shape[0]
    pieces = partial_out.reshape(n_row, tokens.shape[0], partial_out.shape[1])
    pieces = lax.all_to_all(pieces, ROW, 0, 0, tiled=True)
    return jnp.sum(pieces, axis=0).astype(jnp.bfloat16)


def solution(mesh):
    fine = Mesh(mesh.devices.reshape(4, 2, 2, 4, 2), ROW + COL)
    placed = (
        P(ROW, COL),
        P(COL, ROW),
        P(COL, ROW),
        P(ROW, COL),
        P(COL, ROW),
        P(COL, ROW),
        P(ROW, COL),
    )
    return jax.shard_map(
        on_device, mesh=fine, in_specs=placed, out_specs=P(ROW, COL), check_vma=False
    )
```

time: 303 us -> 286 us (0.944)
  waiting for transfers between devices: 199 us -> 166 us
  blocking collectives: 37.3 us -> 61.6 us
  local copies, waits for them, and re-layouts: 32.7 us -> 26.7 us
    reduce_scatter x2, waiting for transfers between devices: 163 us -> 110 us  [the longest x1 84.3 us: on_device(): summed = lax.psum_scatter(on_chip, CHIPS, scatter_dimension=0, tiled=True)]
    all_to_all x0 -> x1, blocking collectives: none -> 24.4 us  [on_device(): pieces = lax.all_to_all(pieces, ROW, 0, 0, tiled=True)]
    all_gather x1 -> x2, waiting for transfers between devices: 35.6 us -> 56 us  [the longest x1 39.7 us: on_device(): hidden_chip = lax.all_gather(hidden, CHIPS, axis=0, tiled=True)]
    unnamed x13, local copies, waits for them, and re-layouts: 29.3 us -> 23.3 us
  transfers between devices with their start and end apart: 3 -> 4, of which waited for: 3 -> 4; matrix products, arithmetic and copies ran while one was open for 0% -> 0% of each run, Pallas kernels for 0% -> 0%
where the time goes in v2:
time: 286 us; the launch traced here: 285 us
  waiting for transfers between devices  166 us (58%)
  blocking collectives  61.6 us (22%)
  local copies, waits for them, and re-layouts  26.7 us (9%)
  between operations  13.2 us (5%)
  other arithmetic  9.49 us (3%)
  matrix products  8.37 us (3%)
    reduce_scatter x1, waiting for transfers between devices, on_device(): summed = lax.psum_scatter(on_chip, CHIPS, scatter_dimension=0, tiled=True)  84.3 us
    all_gather x1, waiting for transfers between devices, on_device(): hidden_chip = lax.all_gather(hidden, CHIPS, axis=0, tiled=True)  39.7 us
    all_gather x1, blocking collectives, on_device(): features = lax.all_gather(tokens, ROW, axis=0, tiled=True)  37.3 us
    reduce_scatter x1, waiting for transfers between devices, on_device(): on_chip = lax.psum_scatter(pair, 'core', scatter_dimension=0, tiled=True)  25.3 us
    all_to_all x1, blocking collectives, on_device(): pieces = lax.all_to_all(pieces, ROW, 0, 0, tiled=True)  24.4 us
    unnamed x13, local copies, waits for them, and re-layouts  23.3 us
    all_gather x1, waiting for transfers between devices, on_device(): hidden_all = lax.all_gather(hidden_chip, 'core', axis=0, tiled=True)  16.3 us
    concatenate x1, other arithmetic, on_device(): pair = jnp.concatenate([pg, pu], axis=1)  6.12 us
  transfers between devices with their start and end apart: 4, of which 4 were waited for; matrix products, arithmetic and copies ran while one was open for 0% of the time, Pallas kernels for 0%

profile of v2, /device:TPU:0, one launch (start us, length us, event | category | flops | bytes accessed | tf_op | source)
XLA Modules:
  0.0 285.2 jit_solution(11566388527710110565)
XLA Ops:
  6.5 0.0 reduce-scatter.5.cloned.1.call-start
  6.5 37.3 %all_gather.9 = bf16[512,512]{1,0:T(8,128)(2,1)S(1)} all-gather(bf16[64,512]{1,0:T(8,128)(2,1)} %param.7), channel_id=1, replica_groups=mesh['z'=4,'x_hi'=2,'x_lo'=2,'y'=4,'core'=2] {'z','x_hi'}, dimensions={0}, use_global_device_ids=true | all-gather | bytes 589824 | tf_op jit(solution)/shard_map/all_gather | solution.py:24
  43.8 0.7 convert_element_type.16
  44.5 0.1 copy.24
  44.6 0.0 copy-start.2
  44.6 5.9 %copy.25 = bf16[512,3584]{0,1:T(8,128)(2,1)} copy(bf16[512,3584]{1,0:T(8,128)(2,1)} %param.9) | data formatting | bytes 7340032 | tf_op args[2]
  50.5 0.0 copy-done.2
  50.5 0.1 copy.22
  50.7 5.9 %copy.23 = bf16[512,3584]{0,1:T(8,128)(2,1)} copy(bf16[512,3584]{1,0:T(8,128)(2,1)} %param.8) | data formatting | bytes 7340032 | tf_op args[1]
  56.6 0.0 copy-start.1
  56.6 1.0 mul.43
  57.6 1.0 copy-done.1
  58.6 2.1 convolution_bitcast_fusion
  60.7 0.0 copy-start
  60.8 1.0 mul.40
  61.8 1.0 copy-done
  62.8 2.1 convolution_bitcast_fusion.1
  64.9 6.1 %pad_maximum_fusion = f32[512,7168]{0,1:T(8,128)} fusion(f32[512,3584]{0,1:T(8,128)S(1)} %convolution_bitcast_fusion, f32[512,3584]{0,1:T(8,128)S(1)} %convolution_bitcast_fusion.1), kind=kLoop, calls=%fused_computation | loop fusion | flops 3670016 | bytes 29360128 | tf_op jit(solution)/shard_map/concatenate | solution.py:27
  71.0 0.0 reduce-scatter.5.cloned.1.call-update
  71.0 0.0 reduce-scatter.7.cloned.1.call-start
  71.1 25.3 %reduce-scatter.5.cloned.1.call-done = f32[256,7168]{0,1:T(8,128)} async-done(((f32[512,7168]{0,1:T(8,128)}), f32[256,7168]{0,1:T(8,128)}) %reduce-scatter.5.cloned.1.call-update) | async-done | bytes 7340048 | tf_op jit(solution)/shard_map/reduce_scatter | solution.py:28
  96.4 8.4 %copy.29 = f32[256,7168]{1,0:T(8,128)} copy(f32[256,7168]{0,1:T(8,128)} %reduce-scatter.5.cloned.1.call-done) | data formatting | bytes 14680064
  104.8 0.0 copy-start.3
  104.8 0.0 reduce-scatter.7.cloned.1.call-update
  104.8 0.0 all-gather.3.cloned.1.call-start
  104.8 84.3 %reduce-scatter.7.cloned.1.call-done = f32[32,7168]{1,0:T(8,128)} async-done(((f32[256,7168]{1,0:T(8,128)}), f32[32,7168]{1,0:T(8,128)}) %reduce-scatter.7.cloned.1.call-update) | async-done | bytes 917520 | tf_op jit(solution)/shard_map/reduce_scatter | solution.py:29
  189.1 2.0 fusion.6
  191.1 0.0 all-gather.3.cloned.1.call-update
  191.1 0.0 all-gather.5.cloned.1.call-start
  191.2 39.7 %all-gather.3.cloned.1.call-done = bf16[256,3584]{1,0:T(8,128)(2,1)} async-done(((bf16[32,3584]{1,0:T(8,128)(2,1)}), bf16[256,3584]{1,0:T(8,128)(2,1)}) %all-gather.3.cloned.1.call-update) | async-done | bytes 1835024 | tf_op jit(solution)/shard_map/all_gather | solution.py:31
  230.9 0.0 all-gather.5.cloned.1.call-update
  231.0 0.0 copy-done.3
  231.0 0.1 copy.28
  231.1 16.3 %all-gather.5.cloned.1.call-done = bf16[512,3584]{1,0:T(8,128)(2,1)} async-done(((bf16[256,3584]{1,0:T(8,128)(2,1)}), bf16[512,3584]{1,0:T(8,128)(2,1)}) %all-gather.5.cloned.1.call-update) | async-done | bytes 3670032 | tf_op jit(solution)/shard_map/all_gather | solution.py:32
  247.4 0.0 copy-start.4
  247.4 1.0 mul.48
  248.4 1.0 copy-done.4
  249.4 4.2 %fusion.1 = f32[8,64,512]{2,1,0:T(8,128)S(1)} fusion(bf16[8,64,3584]{2,1,0:T(8,128)(2,1)} %bitcast.36, bf16[3584,512]{1,0:T(8,128)(2,1)S(1)} %copy-done.4, bf16[448,8,4,128]{3,2,1,0:T(4,128)(2,1)S(1)} %bitcast.35), kind=kOutput, calls=%fused_computation.5 | convolution fusion | flops 1880883200 | bytes 12058624 | tf_op jit(solution)/shard_map/dot_general | solution.py:33
  253.6 24.4 %all_to_all.5 = f32[8,64,512]{2,1,0:T(8,128)S(1)} all-to-all(f32[8,64,512]{2,1,0:T(8,128)S(1)} %fusion.1), channel_id=1, replica_groups=mesh['z'=4,'x_hi'=2,'x_lo'=2,'y'=4,'core'=2] {'z','x_hi'}, dimensions={0} | all-to-all | bytes 2097152 | tf_op jit(solution)/shard_map/all_to_all | solution.py:38
  278.0 0.7 reduce_sum.9
  (2 shorter events, 0.0 us)
Async XLA Ops:
  6.5 89.8 %reduce-scatter.5.cloned.1.call-start = ((), (), s32[]{:S(2)}) async-start(), calls=%async_computation.3 | async-start | bytes 22020096 | tf_op jit(solution)/shard_map/reduce_scatter | solution.py:28
  44.6 5.9 %copy-start.2 = (s32[4,28]{1,0:T(4,128)S(1)}, s32[4,28]{1,0:T(4,128)}, u32[]{:S(2)}) copy-start(s32[4,28]{1,0:T(4,128)} %param.11) | copy-start | bytes 1348
  56.6 2.0 copy-start.1
  60.7 2.0 copy-start
  71.0 118.1 %reduce-scatter.7.cloned.1.call-start = ((), (), s32[]{:S(2)}) async-start(), calls=%async_computation.6 | async-start | bytes 8257536 | tf_op jit(solution)/shard_map/reduce_scatter | solution.py:29
  104.8 126.2 %copy-start.3 = (s32[28,4]{0,1:T(4,128)S(1)}, s32[28,4]{0,1:T(4,128)}, u32[]{:S(2)}) copy-start(s32[28,4]{0,1:T(4,128)} %param.13) | copy-start | bytes 1348
  104.8 126.1 %all-gather.3.cloned.1.call-start = ((), (), s32[]{:S(2)}) async-start(), calls=%async_computation.4 | async-start | bytes 2064384 | tf_op jit(solution)/shard_map/all_gather | solution.py:31
  191.1 56.2 %all-gather.5.cloned.1.call-start = ((), (), s32[]{:S(2)}) async-start(), calls=%async_computation.5 | async-start | bytes 5505024 | tf_op jit(solution)/shard_map/all_gather | solution.py:32
  247.4 2.0 copy-start.4
Sparse Core Ops, SparseCore 0:
  71.2 25.1 reduce-scatter.4
  104.9 84.1 reduce-scatter.6
  191.3 39.6 all-gather.2
  232.4 14.9 all-gather.4

commit v3 on v2

v3 whole, which is shorter than its diff:
```python
import jax
import jax.numpy as jnp
from jax import lax
from jax.sharding import Mesh
from jax.sharding import PartitionSpec as P

ROW = ("z", "x_hi")
COL = ("x_lo", "y", "core")


def expand(weight, keep):
    nrow, ncol = keep.shape
    rows, cols = weight.shape
    masked = (
        weight.reshape(nrow, rows // nrow, ncol, cols // ncol)
        * keep.astype(jnp.bfloat16)[:, None, :, None]
    )
    return masked.reshape(rows, cols)


def shift(x, k, n):
    return lax.ppermute(x, ROW, [(i, (i + k) % n) for i in range(n)])


def on_device(tokens, gate_weight, up_weight, down_weight, gate_keep, up_keep, down_keep):
    n = lax.axis_size(ROW)
    hidden_cols = gate_weight.shape[1]
    features = jnp.concatenate([tokens] + [shift(tokens, k, n) for k in range(1, n)], axis=0)
    pg = jnp.dot(features, expand(gate_weight, gate_keep), preferred_element_type=jnp.float32)
    pu = jnp.dot(features, expand(up_weight, up_keep), preferred_element_type=jnp.float32)
    pair = jnp.concatenate([pg, pu], axis=1)
    summed = lax.psum_scatter(pair, COL, scatter_dimension=0, tiled=True)
    hidden = (jax.nn.silu(summed[:, :hidden_cols]) * summed[:, hidden_cols:]).astype(jnp.bfloat16)
    hidden_all = lax.all_gather(hidden, COL, axis=0, tiled=True)
    partial_out = jnp.dot(
        hidden_all, expand(down_weight, down_keep), preferred_element_type=jnp.float32
    )
    t = tokens.shape[0]
    total = partial_out[:t]
    for k in range(1, n):
        total = total + shift(partial_out[k * t:(k + 1) * t], -k, n)
    return total.astype(jnp.bfloat16)


def solution(mesh):
    fine = Mesh(mesh.devices.reshape(4, 2, 2, 4, 2), ROW + COL)
    placed = (
        P(ROW, COL),
        P(COL, ROW),
        P(COL, ROW),
        P(ROW, COL),
        P(COL, ROW),
        P(COL, ROW),
        P(ROW, COL),
    )
    return jax.shard_map(
        on_device, mesh=fine, in_specs=placed, out_specs=P(ROW, COL), check_vma=False
    )
```

time: 286 us -> 215 us (0.75)
  blocking collectives: 61.6 us -> 0 us
  waiting for transfers between devices: 166 us -> 134 us
  starting transfers between devices: 0.13 us -> 31.8 us
  local copies, waits for them, and re-layouts: 26.7 us -> 17.5 us
    all_gather x1 -> x0, blocking collectives: 37.3 us -> none  [on_device(): features = lax.all_gather(tokens, ROW, axis=0, tiled=True)]
    ppermute x0 -> x14, starting transfers between devices: none -> 31.6 us  [shift(): return lax.ppermute(x, ROW, [(i, (i + k) % n) for i in range(n)])]
    all_to_all x1 -> x0, blocking collectives: 24.4 us -> none  [on_device(): pieces = lax.all_to_all(pieces, ROW, 0, 0, tiled=True)]
    reduce_scatter x2 -> x1, waiting for transfers between devices: 110 us -> 87.5 us  [on_device(): summed = lax.psum_scatter(pair, COL, scatter_dimension=0, tiled=True)]
    all_gather x2 -> x1, waiting for transfers between devices: 56 us -> 35.7 us  [on_device(): hidden_all = lax.all_gather(hidden, COL, axis=0, tiled=True)]
    ppermute x0 -> x14, waiting for transfers between devices: none -> 10.9 us  [shift(): return lax.ppermute(x, ROW, [(i, (i + k) % n) for i in range(n)])]
    unnamed x13 -> x21, local copies, waits for them, and re-layouts: 23.3 us -> 14 us
  transfers between devices with their start and end apart: 4 -> 16, of which waited for: 4 -> 6; matrix products, arithmetic and copies ran while one was open for 0% -> 6% of each run, Pallas kernels for 0% -> 0%
where the time goes in v3:
time: 215 us; the launch traced here: 214 us
  waiting for transfers between devices  134 us (62%)
  starting transfers between devices  31.8 us (15%)
  local copies, waits for them, and re-layouts  17.5 us (8%)
  between operations  13.6 us (6%)
  other arithmetic  8.86 us (4%)
  matrix products  8.38 us (4%)
    reduce_scatter x1, waiting for transfers between devices, on_device(): summed = lax.psum_scatter(pair, COL, scatter_dimension=0, tiled=True)  87.5 us
    all_gather x1, waiting for transfers between devices, on_device(): hidden_all = lax.all_gather(hidden, COL, axis=0, tiled=True)  35.7 us
    ppermute x14, starting transfers between devices, shift(): return lax.ppermute(x, ROW, [(i, (i + k) % n) for i in range(n)])  31.6 us
    unnamed x21, local copies, waits for them, and re-layouts  14 us
    ppermute x14, waiting for transfers between devices, shift(): return lax.ppermute(x, ROW, [(i, (i + k) % n) for i in range(n)])  10.9 us
    concatenate x1, other arithmetic, on_device(): pair = jnp.concatenate([pg, pu], axis=1)  5.5 us
  transfers between devices with their start and end apart: 16, of which 6 were waited for; matrix products, arithmetic and copies ran while one was open for 6% of the time, Pallas kernels for 0%

profile of v3, /device:TPU:0, one launch (start us, length us, event | category | flops | bytes accessed | tf_op | source)
XLA Modules:
  0.0 214.2 jit_solution(13571002036243783006)
XLA Ops:
  6.5 0.0 reduce-scatter.2.cloned.1.call-start
  6.5 3.1 %collective-permute-start = (bf16[64,512]{1,0:T(8,128)(2,1)}, bf16[64,512]{1,0:T(8,128)(2,1)S(1)}, u32[]{:S(2)}, u32[]{:S(2)}) collective-permute-start(bf16[64,512]{1,0:T(8,128)(2,1)} %param.7), channel_id=1, source_target_pairs={{0,16},{16,32},{32,48},{48,64},{64,80},{80,96},{96,112},{112,0},{1... | collective-permute-start | bytes 196616 | tf_op jit(solution)/shard_map/ppermute | solution.py:22
  9.7 1.9 collective-permute-start.1
  11.6 2.9 %collective-permute-start.2 = (bf16[64,512]{1,0:T(8,128)(2,1)}, bf16[64,512]{1,0:T(8,128)(2,1)S(1)}, u32[]{:S(2)}, u32[]{:S(2)}) collective-permute-start(bf16[64,512]{1,0:T(8,128)(2,1)} %param.7), channel_id=1, source_target_pairs={{0,48},{16,64},{32,80},{48,96},{64,112},{80,0},{96,16},{112,32},{1... | collective-permute-start | bytes 196616 | tf_op jit(solution)/shard_map/ppermute | solution.py:22
  14.5 1.2 collective-permute-start.3
  15.7 5.4 %collective-permute-start.4 = (bf16[64,512]{1,0:T(8,128)(2,1)}, bf16[64,512]{1,0:T(8,128)(2,1)S(1)}, u32[]{:S(2)}, u32[]{:S(2)}) collective-permute-start(bf16[64,512]{1,0:T(8,128)(2,1)} %param.7), channel_id=1, source_target_pairs={{0,80},{16,96},{32,112},{48,0},{64,16},{80,32},{96,48},{112,64},{1... | collective-permute-start | bytes 196616 | tf_op jit(solution)/shard_map/ppermute | solution.py:22
  21.1 0.7 convert_element_type.16
  21.8 0.1 copy.11
  21.9 0.0 copy-start.3
  21.9 5.9 %copy.12 = bf16[512,3584]{0,1:T(8,128)(2,1)} copy(bf16[512,3584]{1,0:T(8,128)(2,1)} %param.9) | data formatting | bytes 7340032 | tf_op args[2]
  27.9 0.0 copy-done.3
  27.9 0.1 copy.9
  28.0 0.0 copy-start.2
  28.0 6.0 %copy.10 = bf16[512,3584]{0,1:T(8,128)(2,1)} copy(bf16[512,3584]{1,0:T(8,128)(2,1)} %param.8) | data formatting | bytes 7340032 | tf_op args[1]
  34.0 0.0 copy-done.2
  34.0 0.0 copy-start.1
  34.0 0.0 collective-permute-done
  34.0 1.1 collective-permute-start.5
  35.1 0.0 collective-permute-done.1
  35.1 0.1 collective-permute-start.6
  35.2 0.0 collective-permute-done.2
  35.2 0.0 collective-permute-done.3
  35.2 0.0 collective-permute-done.4
  35.2 3.1 %collective-permute-done.5 = bf16[64,512]{1,0:T(8,128)(2,1)S(1)} collective-permute-done((bf16[64,512]{1,0:T(8,128)(2,1)S(1)}, bf16[64,512]{1,0:T(8,128)(2,1)S(1)}, u32[]{:S(2)}, u32[]{:S(2)}) %collective-permute-start.5) | collective-permute-done | bytes 65568 | tf_op jit(solution)/shard_map/ppermute | solution.py:22
  38.3 2.6 %collective-permute-done.6 = bf16[64,512]{1,0:T(8,128)(2,1)S(1)} collective-permute-done((bf16[64,512]{1,0:T(8,128)(2,1)S(1)}, bf16[64,512]{1,0:T(8,128)(2,1)S(1)}, u32[]{:S(2)}, u32[]{:S(2)}) %collective-permute-start.6) | collective-permute-done | bytes 65568 | tf_op jit(solution)/shard_map/ppermute | solution.py:22
  40.9 1.0 mul.43
  41.9 0.0 copy-done.1
  41.9 2.1 fusion.2
  44.1 0.0 copy-start
  44.1 1.0 mul.40
  45.1 1.0 copy-done
  46.1 2.1 fusion.4
  48.2 5.5 %pad_maximum_fusion = f32[512,7168]{1,0:T(8,128)} fusion(f32[512,3584]{1,0:T(8,128)S(1)} %fusion.2, f32[512,3584]{1,0:T(8,128)S(1)} %fusion.4), kind=kLoop, calls=%fused_computation | loop fusion | flops 3670016 | bytes 29360128 | tf_op jit(solution)/shard_map/concatenate | solution.py:31
  53.7 0.0 copy-start.4
  53.7 0.0 reduce-scatter.2.cloned.1.call-update
  53.7 0.2 all-gather.2.cloned.1.call-start
  54.0 87.5 %reduce-scatter.2.cloned.1.call-done = f32[32,7168]{1,0:T(8,128)} async-done(((f32[512,7168]{1,0:T(8,128)}), f32[32,7168]{1,0:T(8,128)}) %reduce-scatter.2.cloned.1.call-update) | async-done | bytes 917520 | tf_op jit(solution)/shard_map/reduce_scatter | solution.py:32
  141.5 2.0 fusion.6
  143.4 0.0 all-gather.2.cloned.1.call-update
  143.5 0.0 copy-done.4
  143.5 0.1 copy.13
  143.6 35.7 %all-gather.2.cloned.1.call-done = bf16[512,3584]{1,0:T(8,128)(2,1)} async-done(((bf16[32,3584]{1,0:T(8,128)(2,1)}), bf16[512,3584]{1,0:T(8,128)(2,1)}) %all-gather.2.cloned.1.call-update) | async-done | bytes 3670032 | tf_op jit(solution)/shard_map/all_gather | solution.py:34
  179.3 0.0 copy-start.5
  179.3 1.0 mul.48
  180.3 1.0 copy-done.5
  181.3 4.2 %fusion = f32[512,512]{1,0:T(8,128)S(1)} fusion(bf16[512,3584]{1,0:T(8,128)(2,1)} %all-gather.2.cloned.1.call-done, bf16[3584,512]{1,0:T(8,128)(2,1)S(1)} %copy-done.5, bf16[448,8,4,128]{3,2,1,0:T(4,128)(2,1)S(1)} %bitcast.24), kind=kOutput, calls=%fused_computation.2 | convolution fusion | flops 1880883200 | bytes 12058624 | tf_op jit(solution)/shard_map/dot_general | solution.py:35
  185.5 0.1 fusion.14
  185.6 3.2 %collective-permute-start.10 = (f32[64,512]{1,0:T(8,128)S(1)}, f32[64,512]{1,0:T(8,128)S(1)}, u32[]{:S(2)}, u32[]{:S(2)}) collective-permute-start(f32[64,512]{1,0:T(8,128)S(1)} %get-tuple-element.9), channel_id=1, source_target_pairs={{0,64},{16,80},{32,96},{48,112},{64,0},{80,16},{96,32},{112,48},{1... | collective-permute-start | bytes 393224 | tf_op jit(solution)/shard_map/ppermute | solution.py:22
  188.8 2.8 %collective-permute-start.11 = (f32[64,512]{1,0:T(8,128)S(1)}, f32[64,512]{1,0:T(8,128)S(1)}, u32[]{:S(2)}, u32[]{:S(2)}) collective-permute-start(f32[64,512]{1,0:T(8,128)S(1)} %get-tuple-element.8), channel_id=1, source_target_pairs={{0,48},{16,64},{32,80},{48,96},{64,112},{80,0},{96,16},{112,32},{1... | collective-permute-start | bytes 393224 | tf_op jit(solution)/shard_map/ppermute | solution.py:22
  191.6 0.0 collective-permute-start.12
  191.6 2.1 collective-permute-start.13
  193.7 3.5 %collective-permute-start.7 = (f32[64,512]{1,0:T(8,128)S(1)}, f32[64,512]{1,0:T(8,128)S(1)}, u32[]{:S(2)}, u32[]{:S(2)}) collective-permute-start(f32[64,512]{1,0:T(8,128)S(1)} %get-tuple-element.5), channel_id=1, source_target_pairs={{0,112},{16,0},{32,16},{48,32},{64,48},{80,64},{96,80},{112,96},{1... | collective-permute-start | bytes 393224 | tf_op jit(solution)/shard_map/ppermute | solution.py:22
  197.2 0.0 collective-permute-done.10
  197.2 2.0 collective-permute-start.8
  199.3 0.0 collective-permute-done.11
  199.3 2.2 %collective-permute-start.9 = (f32[64,512]{1,0:T(8,128)S(1)}, f32[64,512]{1,0:T(8,128)S(1)}, u32[]{:S(2)}, u32[]{:S(2)}) collective-permute-start(f32[64,512]{1,0:T(8,128)S(1)} %get-tuple-element.10), channel_id=1, source_target_pairs={{0,80},{16,96},{32,112},{48,0},{64,16},{80,32},{96,48},{112,64},{1... | collective-permute-start | bytes 393224 | tf_op jit(solution)/shard_map/ppermute | solution.py:22
  201.5 2.0 collective-permute-done.12
  203.5 0.0 collective-permute-done.13
  203.5 0.0 collective-permute-done.7
  203.5 0.0 collective-permute-done.8
  203.5 3.1 %collective-permute-done.9 = f32[64,512]{1,0:T(8,128)S(1)} collective-permute-done((f32[64,512]{1,0:T(8,128)S(1)}, f32[64,512]{1,0:T(8,128)S(1)}, u32[]{:S(2)}, u32[]{:S(2)}) %collective-permute-start.9) | collective-permute-done | bytes 131104 | tf_op jit(solution)/shard_map/ppermute | solution.py:22
  206.6 0.7 fusion.13
  (10 shorter events, 0.1 us)
Async XLA Ops:
  6.5 134.9 %reduce-scatter.2.cloned.1.call-start = ((), (), s32[]{:S(2)}) async-start(), calls=%async_computation.1 | async-start | bytes 15597568 | tf_op jit(solution)/shard_map/reduce_scatter | solution.py:32
  6.5 27.4 %collective-permute-start = (bf16[64,512]{1,0:T(8,128)(2,1)}, bf16[64,512]{1,0:T(8,128)(2,1)S(1)}, u32[]{:S(2)}, u32[]{:S(2)}) collective-permute-start(bf16[64,512]{1,0:T(8,128)(2,1)} %param.7), channel_id=1, source_target_pairs={{0,16},{16,32},{32,48},{48,64},{64,80},{80,96},{96,112},{112,0},{1... | collective-permute-start | bytes 196616 | tf_op jit(solution)/shard_map/ppermute | solution.py:22
  9.7 25.4 %collective-permute-start.1 = (bf16[64,512]{1,0:T(8,128)(2,1)}, bf16[64,512]{1,0:T(8,128)(2,1)S(1)}, u32[]{:S(2)}, u32[]{:S(2)}) collective-permute-start(bf16[64,512]{1,0:T(8,128)(2,1)} %param.7), channel_id=1, source_target_pairs={{0,32},{16,48},{32,64},{48,80},{64,96},{80,112},{96,0},{112,16},{1... | collective-permute-start | bytes 196616 | tf_op jit(solution)/shard_map/ppermute | solution.py:22
  11.6 23.6 %collective-permute-start.2 = (bf16[64,512]{1,0:T(8,128)(2,1)}, bf16[64,512]{1,0:T(8,128)(2,1)S(1)}, u32[]{:S(2)}, u32[]{:S(2)}) collective-permute-start(bf16[64,512]{1,0:T(8,128)(2,1)} %param.7), channel_id=1, source_target_pairs={{0,48},{16,64},{32,80},{48,96},{64,112},{80,0},{96,16},{112,32},{1... | collective-permute-start | bytes 196616 | tf_op jit(solution)/shard_map/ppermute | solution.py:22
  14.5 20.7 %collective-permute-start.3 = (bf16[64,512]{1,0:T(8,128)(2,1)}, bf16[64,512]{1,0:T(8,128)(2,1)S(1)}, u32[]{:S(2)}, u32[]{:S(2)}) collective-permute-start(bf16[64,512]{1,0:T(8,128)(2,1)} %param.7), channel_id=1, source_target_pairs={{0,64},{16,80},{32,96},{48,112},{64,0},{80,16},{96,32},{112,48},{1... | collective-permute-start | bytes 196616 | tf_op jit(solution)/shard_map/ppermute | solution.py:22
  15.7 19.5 %collective-permute-start.4 = (bf16[64,512]{1,0:T(8,128)(2,1)}, bf16[64,512]{1,0:T(8,128)(2,1)S(1)}, u32[]{:S(2)}, u32[]{:S(2)}) collective-permute-start(bf16[64,512]{1,0:T(8,128)(2,1)} %param.7), channel_id=1, source_target_pairs={{0,80},{16,96},{32,112},{48,0},{64,16},{80,32},{96,48},{112,64},{1... | collective-permute-start | bytes 196616 | tf_op jit(solution)/shard_map/ppermute | solution.py:22
  21.9 5.9 %copy-start.3 = (s32[4,28]{1,0:T(4,128)S(1)}, s32[4,28]{1,0:T(4,128)}, u32[]{:S(2)}) copy-start(s32[4,28]{1,0:T(4,128)} %param.11) | copy-start | bytes 1348
  28.0 6.0 %copy-start.2 = (bf16[64,512]{1,0:T(8,128)(2,1)S(1)}, bf16[64,512]{1,0:T(8,128)(2,1)}, u32[]{:S(2)}) copy-start(bf16[64,512]{1,0:T(8,128)(2,1)} %param.7) | copy-start | bytes 196612
  34.0 8.0 %copy-start.1 = (bf16[512,3584]{0,1:T(8,128)(2,1)S(1)}, bf16[512,3584]{0,1:T(8,128)(2,1)}, u32[]{:S(2)}) copy-start(bf16[512,3584]{0,1:T(8,128)(2,1)} %copy.12) | copy-start | bytes 11010052
  34.0 4.3 %collective-permute-start.5 = (bf16[64,512]{1,0:T(8,128)(2,1)S(1)}, bf16[64,512]{1,0:T(8,128)(2,1)S(1)}, u32[]{:S(2)}, u32[]{:S(2)}) collective-permute-start(bf16[64,512]{1,0:T(8,128)(2,1)S(1)} %copy-done.2), channel_id=1, source_target_pairs={{0,96},{16,112},{32,0},{48,16},{64,32},{80,48},{96,64},{112,80},{1... | collective-permute-start | bytes 196616 | tf_op jit(solution)/shard_map/ppermute | solution.py:22
  35.1 5.8 %collective-permute-start.6 = (bf16[64,512]{1,0:T(8,128)(2,1)S(1)}, bf16[64,512]{1,0:T(8,128)(2,1)S(1)}, u32[]{:S(2)}, u32[]{:S(2)}) collective-permute-start(bf16[64,512]{1,0:T(8,128)(2,1)S(1)} %copy-done.2), channel_id=1, source_target_pairs={{0,112},{16,0},{32,16},{48,32},{64,48},{80,64},{96,80},{112,96},{1... | collective-permute-start | bytes 196616 | tf_op jit(solution)/shard_map/ppermute | solution.py:22
  44.1 2.0 copy-start
  53.7 89.7 %copy-start.4 = (s32[28,4]{0,1:T(4,128)S(1)}, s32[28,4]{0,1:T(4,128)}, u32[]{:S(2)}) copy-start(s32[28,4]{0,1:T(4,128)} %param.13) | copy-start | bytes 1348
  53.7 125.6 %all-gather.2.cloned.1.call-start = ((), (), s32[]{:S(2)}) async-start(), calls=%async_computation.2 | async-start | bytes 3899392 | tf_op jit(solution)/shard_map/all_gather | solution.py:34
  179.3 2.0 copy-start.5
  185.6 11.7 %collective-permute-start.10 = (f32[64,512]{1,0:T(8,128)S(1)}, f32[64,512]{1,0:T(8,128)S(1)}, u32[]{:S(2)}, u32[]{:S(2)}) collective-permute-start(f32[64,512]{1,0:T(8,128)S(1)} %get-tuple-element.9), channel_id=1, source_target_pairs={{0,64},{16,80},{32,96},{48,112},{64,0},{80,16},{96,32},{112,48},{1... | collective-permute-start | bytes 393224 | tf_op jit(solution)/shard_map/ppermute | solution.py:22
  188.8 10.5 %collective-permute-start.11 = (f32[64,512]{1,0:T(8,128)S(1)}, f32[64,512]{1,0:T(8,128)S(1)}, u32[]{:S(2)}, u32[]{:S(2)}) collective-permute-start(f32[64,512]{1,0:T(8,128)S(1)} %get-tuple-element.8), channel_id=1, source_target_pairs={{0,48},{16,64},{32,80},{48,96},{64,112},{80,0},{96,16},{112,32},{1... | collective-permute-start | bytes 393224 | tf_op jit(solution)/shard_map/ppermute | solution.py:22
  191.6 11.9 %collective-permute-start.12 = (f32[64,512]{1,0:T(8,128)S(1)}, f32[64,512]{1,0:T(8,128)S(1)}, u32[]{:S(2)}, u32[]{:S(2)}) collective-permute-start(f32[64,512]{1,0:T(8,128)S(1)} %get-tuple-element.7), channel_id=1, source_target_pairs={{0,32},{16,48},{32,64},{48,80},{64,96},{80,112},{96,0},{112,16},{1... | collective-permute-start | bytes 393224 | tf_op jit(solution)/shard_map/ppermute | solution.py:22
  191.6 11.9 %collective-permute-start.13 = (f32[64,512]{1,0:T(8,128)S(1)}, f32[64,512]{1,0:T(8,128)S(1)}, u32[]{:S(2)}, u32[]{:S(2)}) collective-permute-start(f32[64,512]{1,0:T(8,128)S(1)} %get-tuple-element.6), channel_id=1, source_target_pairs={{0,16},{16,32},{32,48},{48,64},{64,80},{80,96},{96,112},{112,0},{1... | collective-permute-start | bytes 393224 | tf_op jit(solution)/shard_map/ppermute | solution.py:22
  193.7 9.8 %collective-permute-start.7 = (f32[64,512]{1,0:T(8,128)S(1)}, f32[64,512]{1,0:T(8,128)S(1)}, u32[]{:S(2)}, u32[]{:S(2)}) collective-permute-start(f32[64,512]{1,0:T(8,128)S(1)} %get-tuple-element.5), channel_id=1, source_target_pairs={{0,112},{16,0},{32,16},{48,32},{64,48},{80,64},{96,80},{112,96},{1... | collective-permute-start | bytes 393224 | tf_op jit(solution)/shard_map/ppermute | solution.py:22
  197.2 6.3 %collective-permute-start.8 = (f32[64,512]{1,0:T(8,128)S(1)}, f32[64,512]{1,0:T(8,128)S(1)}, u32[]{:S(2)}, u32[]{:S(2)}) collective-permute-start(f32[64,512]{1,0:T(8,128)S(1)} %get-tuple-element.11), channel_id=1, source_target_pairs={{0,96},{16,112},{32,0},{48,16},{64,32},{80,48},{96,64},{112,80},{1... | collective-permute-start | bytes 393224 | tf_op jit(solution)/shard_map/ppermute | solution.py:22
  199.3 7.4 %collective-permute-start.9 = (f32[64,512]{1,0:T(8,128)S(1)}, f32[64,512]{1,0:T(8,128)S(1)}, u32[]{:S(2)}, u32[]{:S(2)}) collective-permute-start(f32[64,512]{1,0:T(8,128)S(1)} %get-tuple-element.10), channel_id=1, source_target_pairs={{0,80},{16,96},{32,112},{48,0},{64,16},{80,32},{96,48},{112,64},{1... | collective-permute-start | bytes 393224 | tf_op jit(solution)/shard_map/ppermute | solution.py:22
Sparse Core Ops, SparseCore 0:
  53.9 87.5 reduce-scatter.1
  143.6 35.6 all-gather.1

commit v4 on v3

--- a/solution.py
+++ b/solution.py
@@ -1,8 +1,66 @@
+import functools
+
 import jax
 import jax.numpy as jnp
 from jax import lax
+from jax.experimental import pallas as pl
+from jax.experimental.pallas import tpu as pltpu
 from jax.sharding import Mesh
 from jax.sharding import PartitionSpec as P
+
+BLOCK = 128
+TILE = 256
+
+
+def _gate_up_kernel(n_half, n_feat, gk_ref, uk_ref, x_ref, gw_ref, uw_ref, o_ref, w_scr):
+    j = pl.program_id(0)
+
+    def build(w_ref, k_ref, jj):
+        for kb in range(n_feat):
+            for hb in range(TILE // BLOCK):
+                k = k_ref[kb, jj * (TILE // BLOCK) + hb]
+                rows = slice(kb * BLOCK, (kb + 1) * BLOCK)
+                cols = slice(hb * BLOCK, (hb + 1) * BLOCK)
+                sub = w_ref[rows, cols]
+                w_scr[rows, cols] = jnp.where(k == 0, jnp.zeros_like(sub), sub)
+
+    @pl.when(j < n_half)
+    def _():
+        build(gw_ref, gk_ref, j)
+
+    @pl.when(j >= n_half)
+    def _():
+        build(uw_ref, uk_ref, j - n_half)
+
+    o_ref[...] = jnp.dot(x_ref[...], w_scr[...], preferred_element_type=jnp.float32)
+
+
+def gate_up(x, gw, uw, gk, uk):
+    t, f = x.shape
+    h = gw.shape[1]
+    n_half = h // TILE
+    n_feat = f // BLOCK
+    grid_spec = pltpu.PrefetchScalarGridSpec(
+        num_scalar_prefetch=2,
+        grid=(2 * n_half,),
+        in_specs=[
+            pl.BlockSpec((t, f), lambda j, gk, uk: (0, 0)),
+            pl.BlockSpec((f, TILE), lambda j, gk, uk: (0, jnp.minimum(j, n_half - 1))),
+            pl.BlockSpec((f, TILE), lambda j, gk, uk: (0, jnp.maximum(j - n_half, 0))),
+        ],
+        out_specs=pl.BlockSpec((t, TILE), lambda j, gk, uk: (0, j)),
+        scratch_shapes=[pltpu.VMEM((f, TILE), x.dtype)],
+    )
+    return pl.pallas_call(
+        functools.partial(_gate_up_kernel, n_half, n_feat),
+        grid_spec=grid_spec,
+        out_shape=jax.ShapeDtypeStruct((t, 2 * h), jnp.float32),
+        compiler_params=pltpu.CompilerParams(dimension_semantics=("arbitrary",)),
+        cost_estimate=pl.CostEstimate(
+            flops=2 * t * f * 2 * h, transcendentals=0,
+            bytes_accessed=2 * (t * f + 2 * f * h) + 4 * t * 2 * h,
+        ),
+    )(gk, uk, x, gw, uw)
 
 ROW = ("z", "x_hi")
 COL = ("x_lo", "y", "core")
@@ -26,9 +84,7 @@
     n = lax.axis_size(ROW)
     hidden_cols = gate_weight.shape[1]
     features = jnp.concatenate([tokens] + [shift(tokens, k, n) for k in range(1, n)], axis=0)
-    pg = jnp.dot(features, expand(gate_weight, gate_keep), preferred_element_type=jnp.float32)
-    pu = jnp.dot(features, expand(up_weight, up_keep), preferred_element_type=jnp.float32)
-    pair = jnp.concatenate([pg, pu], axis=1)
+    pair = gate_up(features, gate_weight, up_weight, gate_keep, up_keep)
     summed = lax.psum_scatter(pair, COL, scatter_dimension=0, tiled=True)
     hidden = (jax.nn.silu(summed[:, :hidden_cols]) * summed[:, hidden_cols:]).astype(jnp.bfloat16)
     hidden_all = lax.all_gather(hidden, COL, axis=0, tiled=True)

time: 215 us -> 215 us (level)
  Pallas kernels: 0 us -> 23.7 us
  local copies, waits for them, and re-layouts: 17.5 us -> 3.93 us
  other arithmetic: 8.86 us -> 2.69 us
  matrix products: 8.38 us -> 4.16 us
    pallas_call x0 -> x1, Pallas kernels: none -> 23.7 us  [gate_up(): pl.pallas_call(functools.partial(_gate_up_kernel, n_half, n_feat), grid_s...]
    unnamed x21 -> x13, local copies, waits for them, and re-layouts: 14 us -> 2.74 us
    concatenate x1 -> x0, other arithmetic: 5.5 us -> none  [on_device(): pair = jnp.concatenate([pg, pu], axis=1)]
    dot_general x2 -> x0, matrix products: 4.22 us -> none  [the longest x1 2.11 us: on_device(): jnp.dot(features, expand(up_weight, up_keep), preferred_element_type=jnp....]
  transfers between devices with their start and end apart: 16 -> 16, of which waited for: 6 -> 7; matrix products, arithmetic and copies ran while one was open for 6% -> 0% of each run, Pallas kernels for 0% -> 0%
where the time goes in v4:
time: 215 us; the launch traced here: 214 us
  waiting for transfers between devices  134 us (62%)
  starting transfers between devices  31.6 us (15%)
  Pallas kernels  23.7 us (11%)
  between operations  13.5 us (6%)
  matrix products  4.16 us (2%)
  local copies, waits for them, and re-layouts  3.93 us (2%)
  other arithmetic  2.69 us (1%)
    reduce_scatter x1, waiting for transfers between devices, on_device(): summed = lax.psum_scatter(pair, COL, scatter_dimension=0, tiled=True)  87.5 us
    all_gather x1, waiting for transfers between devices, on_device(): hidden_all = lax.all_gather(hidden, COL, axis=0, tiled=True)  35.8 us
    ppermute x14, starting transfers between devices, shift(): return lax.ppermute(x, ROW, [(i, (i + k) % n) for i in range(n)])  31.5 us
    pallas_call x1, Pallas kernels, gate_up(): pl.pallas_call(functools.partial(_gate_up_kernel, n_half, n_feat), grid_s...  23.7 us
    ppermute x14, waiting for transfers between devices, shift(): return lax.ppermute(x, ROW, [(i, (i + k) % n) for i in range(n)])  11.1 us
  transfers between devices with their start and end apart: 16, of which 7 were waited for; matrix products, arithmetic and copies ran while one was open for 0% of the time, Pallas kernels for 0%

profile of v4, /device:TPU:0, one launch (start us, length us, event | category | flops | bytes accessed | tf_op | source)
XLA Modules:
  0.0 214.0 jit_solution(4095411930372446212)
XLA Ops:
  6.5 0.0 reduce-scatter.2.cloned.1.call-start
  6.5 3.1 %collective-permute-start = (bf16[64,512]{1,0:T(8,128)(2,1)}, bf16[64,512]{1,0:T(8,128)(2,1)S(1)}, u32[]{:S(2)}, u32[]{:S(2)}) collective-permute-start(bf16[64,512]{1,0:T(8,128)(2,1)} %param.7), channel_id=1, source_target_pairs={{0,16},{16,32},{32,48},{48,64},{64,80},{80,96},{96,112},{112,0},{1... | collective-permute-start | bytes 196616 | tf_op jit(solution)/shard_map/ppermute | solution.py:80
  9.7 1.9 collective-permute-start.1
  11.6 2.9 %collective-permute-start.2 = (bf16[64,512]{1,0:T(8,128)(2,1)}, bf16[64,512]{1,0:T(8,128)(2,1)S(1)}, u32[]{:S(2)}, u32[]{:S(2)}) collective-permute-start(bf16[64,512]{1,0:T(8,128)(2,1)} %param.7), channel_id=1, source_target_pairs={{0,48},{16,64},{32,80},{48,96},{64,112},{80,0},{96,16},{112,32},{1... | collective-permute-start | bytes 196616 | tf_op jit(solution)/shard_map/ppermute | solution.py:80
  14.5 1.2 collective-permute-start.3
  15.7 5.4 %collective-permute-start.4 = (bf16[64,512]{1,0:T(8,128)(2,1)}, bf16[64,512]{1,0:T(8,128)(2,1)S(1)}, u32[]{:S(2)}, u32[]{:S(2)}) collective-permute-start(bf16[64,512]{1,0:T(8,128)(2,1)} %param.7), channel_id=1, source_target_pairs={{0,80},{16,96},{32,112},{48,0},{64,16},{80,32},{96,48},{112,64},{1... | collective-permute-start | bytes 196616 | tf_op jit(solution)/shard_map/ppermute | solution.py:80
  21.1 0.9 constant_dynamic-update-slice_fusion.7
  22.0 0.0 collective-permute-done
  22.0 1.0 collective-permute-start.5
  23.0 0.0 collective-permute-done.1
  23.0 0.1 collective-permute-start.6
  23.1 0.0 collective-permute-done.2
  23.1 0.0 collective-permute-done.3
  23.2 0.2 collective-permute-done.4
  23.4 3.1 %collective-permute-done.5 = bf16[64,512]{1,0:T(8,128)(2,1)S(1)} collective-permute-done((bf16[64,512]{1,0:T(8,128)(2,1)}, bf16[64,512]{1,0:T(8,128)(2,1)S(1)}, u32[]{:S(2)}, u32[]{:S(2)}) %collective-permute-start.5) | collective-permute-done | bytes 65568 | tf_op jit(solution)/shard_map/ppermute | solution.py:80
  26.5 2.6 %collective-permute-done.6 = bf16[64,512]{1,0:T(8,128)(2,1)S(1)} collective-permute-done((bf16[64,512]{1,0:T(8,128)(2,1)}, bf16[64,512]{1,0:T(8,128)(2,1)S(1)}, u32[]{:S(2)}, u32[]{:S(2)}) %collective-permute-start.6) | collective-permute-done | bytes 65568 | tf_op jit(solution)/shard_map/ppermute | solution.py:80
  29.1 0.0 copy-start
  29.1 0.8 copy-done
  29.9 23.7 %shard_map.73 = f32[512,7168]{1,0:T(8,128)} custom-call(s32[4,28]{1,0:T(4,128)} %gk_ref.1, s32[4,28]{1,0:T(4,128)} %uk_ref.1, bf16[512,512]{1,0:T(8,128)(2,1)} %copy-done, bf16[512,3584]{1,0:T(8,128)(2,1)} %gw_ref.1, bf16[512,3584]{1,0:T(8,128)(2,1)} %uw_ref.1), custom_call_target="tpu_custom_call" | custom-call | flops 3758096384 | bytes 22544384 | tf_op jit(solution)/shard_map/pallas_call | solution.py:54
  53.6 0.0 copy-start.1
  53.6 0.0 reduce-scatter.2.cloned.1.call-update
  53.6 0.0 all-gather.2.cloned.1.call-start
  53.7 87.5 %reduce-scatter.2.cloned.1.call-done = f32[32,7168]{1,0:T(8,128)} async-done(((f32[512,7168]{1,0:T(8,128)}), f32[32,7168]{1,0:T(8,128)}) %reduce-scatter.2.cloned.1.call-update) | async-done | bytes 917520 | tf_op jit(solution)/shard_map/reduce_scatter | solution.py:88
  141.2 2.0 fusion.2
  143.2 0.0 all-gather.2.cloned.1.call-update
  143.2 0.0 copy-done.1
  143.2 0.1 copy.8
  143.3 35.8 %all-gather.2.cloned.1.call-done = bf16[512,3584]{1,0:T(8,128)(2,1)} async-done(((bf16[32,3584]{1,0:T(8,128)(2,1)}), bf16[512,3584]{1,0:T(8,128)(2,1)}) %all-gather.2.cloned.1.call-update) | async-done | bytes 3670032 | tf_op jit(solution)/shard_map/all_gather | solution.py:90
  179.1 0.0 copy-start.2
  179.1 1.0 mul.20
  180.1 1.0 copy-done.2
  181.1 4.2 %fusion = f32[512,512]{1,0:T(8,128)S(1)} fusion(bf16[512,3584]{1,0:T(8,128)(2,1)} %all-gather.2.cloned.1.call-done, bf16[3584,512]{1,0:T(8,128)(2,1)S(1)} %copy-done.2, bf16[448,8,4,128]{3,2,1,0:T(4,128)(2,1)S(1)} %bitcast.6), kind=kOutput, calls=%fused_computation.1 | convolution fusion | flops 1880883200 | bytes 12058624 | tf_op jit(solution)/shard_map/dot_general | solution.py:91
  185.3 0.1 fusion.10
  185.4 3.2 %collective-permute-start.10 = (f32[64,512]{1,0:T(8,128)S(1)}, f32[64,512]{1,0:T(8,128)S(1)}, u32[]{:S(2)}, u32[]{:S(2)}) collective-permute-start(f32[64,512]{1,0:T(8,128)S(1)} %get-tuple-element.9), channel_id=1, source_target_pairs={{0,64},{16,80},{32,96},{48,112},{64,0},{80,16},{96,32},{112,48},{1... | collective-permute-start | bytes 393224 | tf_op jit(solution)/shard_map/ppermute | solution.py:80
  188.6 2.8 %collective-permute-start.11 = (f32[64,512]{1,0:T(8,128)S(1)}, f32[64,512]{1,0:T(8,128)S(1)}, u32[]{:S(2)}, u32[]{:S(2)}) collective-permute-start(f32[64,512]{1,0:T(8,128)S(1)} %get-tuple-element.8), channel_id=1, source_target_pairs={{0,48},{16,64},{32,80},{48,96},{64,112},{80,0},{96,16},{112,32},{1... | collective-permute-start | bytes 393224 | tf_op jit(solution)/shard_map/ppermute | solution.py:80
  191.4 0.0 collective-permute-start.12
  191.4 2.1 collective-permute-start.13
  193.5 3.5 %collective-permute-start.7 = (f32[64,512]{1,0:T(8,128)S(1)}, f32[64,512]{1,0:T(8,128)S(1)}, u32[]{:S(2)}, u32[]{:S(2)}) collective-permute-start(f32[64,512]{1,0:T(8,128)S(1)} %get-tuple-element.5), channel_id=1, source_target_pairs={{0,112},{16,0},{32,16},{48,32},{64,48},{80,64},{96,80},{112,96},{1... | collective-permute-start | bytes 393224 | tf_op jit(solution)/shard_map/ppermute | solution.py:80
  197.0 0.0 collective-permute-done.10
  197.0 2.0 collective-permute-start.8
  199.1 0.0 collective-permute-done.11
  199.1 2.2 %collective-permute-start.9 = (f32[64,512]{1,0:T(8,128)S(1)}, f32[64,512]{1,0:T(8,128)S(1)}, u32[]{:S(2)}, u32[]{:S(2)}) collective-permute-start(f32[64,512]{1,0:T(8,128)S(1)} %get-tuple-element.10), channel_id=1, source_target_pairs={{0,80},{16,96},{32,112},{48,0},{64,16},{80,32},{96,48},{112,64},{1... | collective-permute-start | bytes 393224 | tf_op jit(solution)/shard_map/ppermute | solution.py:80
  201.2 2.0 collective-permute-done.12
  203.3 0.0 collective-permute-done.13
  203.3 0.0 collective-permute-done.7
  203.3 0.0 collective-permute-done.8
  203.3 3.1 %collective-permute-done.9 = f32[64,512]{1,0:T(8,128)S(1)} collective-permute-done((f32[64,512]{1,0:T(8,128)S(1)}, f32[64,512]{1,0:T(8,128)S(1)}, u32[]{:S(2)}, u32[]{:S(2)}) %collective-permute-start.9) | collective-permute-done | bytes 131104 | tf_op jit(solution)/shard_map/ppermute | solution.py:80
  206.4 0.7 fusion.9
  (8 shorter events, 0.0 us)
Async XLA Ops:
  6.5 134.6 %reduce-scatter.2.cloned.1.call-start = ((), (), s32[]{:S(2)}) async-start(), calls=%async_computation.1 | async-start | bytes 15597568 | tf_op jit(solution)/shard_map/reduce_scatter | solution.py:88
  6.5 15.5 %collective-permute-start = (bf16[64,512]{1,0:T(8,128)(2,1)}, bf16[64,512]{1,0:T(8,128)(2,1)S(1)}, u32[]{:S(2)}, u32[]{:S(2)}) collective-permute-start(bf16[64,512]{1,0:T(8,128)(2,1)} %param.7), channel_id=1, source_target_pairs={{0,16},{16,32},{32,48},{48,64},{64,80},{80,96},{96,112},{112,0},{1... | collective-permute-start | bytes 196616 | tf_op jit(solution)/shard_map/ppermute | solution.py:80
  9.7 13.3 %collective-permute-start.1 = (bf16[64,512]{1,0:T(8,128)(2,1)}, bf16[64,512]{1,0:T(8,128)(2,1)S(1)}, u32[]{:S(2)}, u32[]{:S(2)}) collective-permute-start(bf16[64,512]{1,0:T(8,128)(2,1)} %param.7), channel_id=1, source_target_pairs={{0,32},{16,48},{32,64},{48,80},{64,96},{80,112},{96,0},{112,16},{1... | collective-permute-start | bytes 196616 | tf_op jit(solution)/shard_map/ppermute | solution.py:80
  11.6 11.5 %collective-permute-start.2 = (bf16[64,512]{1,0:T(8,128)(2,1)}, bf16[64,512]{1,0:T(8,128)(2,1)S(1)}, u32[]{:S(2)}, u32[]{:S(2)}) collective-permute-start(bf16[64,512]{1,0:T(8,128)(2,1)} %param.7), channel_id=1, source_target_pairs={{0,48},{16,64},{32,80},{48,96},{64,112},{80,0},{96,16},{112,32},{1... | collective-permute-start | bytes 196616 | tf_op jit(solution)/shard_map/ppermute | solution.py:80
  14.5 8.6 %collective-permute-start.3 = (bf16[64,512]{1,0:T(8,128)(2,1)}, bf16[64,512]{1,0:T(8,128)(2,1)S(1)}, u32[]{:S(2)}, u32[]{:S(2)}) collective-permute-start(bf16[64,512]{1,0:T(8,128)(2,1)} %param.7), channel_id=1, source_target_pairs={{0,64},{16,80},{32,96},{48,112},{64,0},{80,16},{96,32},{112,48},{1... | collective-permute-start | bytes 196616 | tf_op jit(solution)/shard_map/ppermute | solution.py:80
  15.7 7.7 %collective-permute-start.4 = (bf16[64,512]{1,0:T(8,128)(2,1)}, bf16[64,512]{1,0:T(8,128)(2,1)S(1)}, u32[]{:S(2)}, u32[]{:S(2)}) collective-permute-start(bf16[64,512]{1,0:T(8,128)(2,1)} %param.7), channel_id=1, source_target_pairs={{0,80},{16,96},{32,112},{48,0},{64,16},{80,32},{96,48},{112,64},{1... | collective-permute-start | bytes 196616 | tf_op jit(solution)/shard_map/ppermute | solution.py:80
  22.0 4.5 %collective-permute-start.5 = (bf16[64,512]{1,0:T(8,128)(2,1)}, bf16[64,512]{1,0:T(8,128)(2,1)S(1)}, u32[]{:S(2)}, u32[]{:S(2)}) collective-permute-start(bf16[64,512]{1,0:T(8,128)(2,1)} %param.7), channel_id=1, source_target_pairs={{0,96},{16,112},{32,0},{48,16},{64,32},{80,48},{96,64},{112,80},{1... | collective-permute-start | bytes 196616 | tf_op jit(solution)/shard_map/ppermute | solution.py:80
  23.0 6.0 %collective-permute-start.6 = (bf16[64,512]{1,0:T(8,128)(2,1)}, bf16[64,512]{1,0:T(8,128)(2,1)S(1)}, u32[]{:S(2)}, u32[]{:S(2)}) collective-permute-start(bf16[64,512]{1,0:T(8,128)(2,1)} %param.7), channel_id=1, source_target_pairs={{0,112},{16,0},{32,16},{48,32},{64,48},{80,64},{96,80},{112,96},{1... | collective-permute-start | bytes 196616 | tf_op jit(solution)/shard_map/ppermute | solution.py:80
  29.1 0.8 copy-start
  53.6 89.6 %copy-start.1 = (s32[28,4]{0,1:T(4,128)S(1)}, s32[28,4]{0,1:T(4,128)}, u32[]{:S(2)}) copy-start(s32[28,4]{0,1:T(4,128)} %param.13) | copy-start | bytes 1348
  53.6 125.5 %all-gather.2.cloned.1.call-start = ((), (), s32[]{:S(2)}) async-start(), calls=%async_computation.2 | async-start | bytes 3899392 | tf_op jit(solution)/shard_map/all_gather | solution.py:90
  179.1 2.0 copy-start.2
  185.4 11.7 %collective-permute-start.10 = (f32[64,512]{1,0:T(8,128)S(1)}, f32[64,512]{1,0:T(8,128)S(1)}, u32[]{:S(2)}, u32[]{:S(2)}) collective-permute-start(f32[64,512]{1,0:T(8,128)S(1)} %get-tuple-element.9), channel_id=1, source_target_pairs={{0,64},{16,80},{32,96},{48,112},{64,0},{80,16},{96,32},{112,48},{1... | collective-permute-start | bytes 393224 | tf_op jit(solution)/shard_map/ppermute | solution.py:80
  188.6 10.5 %collective-permute-start.11 = (f32[64,512]{1,0:T(8,128)S(1)}, f32[64,512]{1,0:T(8,128)S(1)}, u32[]{:S(2)}, u32[]{:S(2)}) collective-permute-start(f32[64,512]{1,0:T(8,128)S(1)} %get-tuple-element.8), channel_id=1, source_target_pairs={{0,48},{16,64},{32,80},{48,96},{64,112},{80,0},{96,16},{112,32},{1... | collective-permute-start | bytes 393224 | tf_op jit(solution)/shard_map/ppermute | solution.py:80
  191.4 11.9 %collective-permute-start.12 = (f32[64,512]{1,0:T(8,128)S(1)}, f32[64,512]{1,0:T(8,128)S(1)}, u32[]{:S(2)}, u32[]{:S(2)}) collective-permute-start(f32[64,512]{1,0:T(8,128)S(1)} %get-tuple-element.7), channel_id=1, source_target_pairs={{0,32},{16,48},{32,64},{48,80},{64,96},{80,112},{96,0},{112,16},{1... | collective-permute-start | bytes 393224 | tf_op jit(solution)/shard_map/ppermute | solution.py:80
  191.4 11.9 %collective-permute-start.13 = (f32[64,512]{1,0:T(8,128)S(1)}, f32[64,512]{1,0:T(8,128)S(1)}, u32[]{:S(2)}, u32[]{:S(2)}) collective-permute-start(f32[64,512]{1,0:T(8,128)S(1)} %get-tuple-element.6), channel_id=1, source_target_pairs={{0,16},{16,32},{32,48},{48,64},{64,80},{80,96},{96,112},{112,0},{1... | collective-permute-start | bytes 393224 | tf_op jit(solution)/shard_map/ppermute | solution.py:80
  193.5 9.8 %collective-permute-start.7 = (f32[64,512]{1,0:T(8,128)S(1)}, f32[64,512]{1,0:T(8,128)S(1)}, u32[]{:S(2)}, u32[]{:S(2)}) collective-permute-start(f32[64,512]{1,0:T(8,128)S(1)} %get-tuple-element.5), channel_id=1, source_target_pairs={{0,112},{16,0},{32,16},{48,32},{64,48},{80,64},{96,80},{112,96},{1... | collective-permute-start | bytes 393224 | tf_op jit(solution)/shard_map/ppermute | solution.py:80
  197.0 6.3 %collective-permute-start.8 = (f32[64,512]{1,0:T(8,128)S(1)}, f32[64,512]{1,0:T(8,128)S(1)}, u32[]{:S(2)}, u32[]{:S(2)}) collective-permute-start(f32[64,512]{1,0:T(8,128)S(1)} %get-tuple-element.11), channel_id=1, source_target_pairs={{0,96},{16,112},{32,0},{48,16},{64,32},{80,48},{96,64},{112,80},{1... | collective-permute-start | bytes 393224 | tf_op jit(solution)/shard_map/ppermute | solution.py:80
  199.1 7.4 %collective-permute-start.9 = (f32[64,512]{1,0:T(8,128)S(1)}, f32[64,512]{1,0:T(8,128)S(1)}, u32[]{:S(2)}, u32[]{:S(2)}) collective-permute-start(f32[64,512]{1,0:T(8,128)S(1)} %get-tuple-element.10), channel_id=1, source_target_pairs={{0,80},{16,96},{32,112},{48,0},{64,16},{80,32},{96,48},{112,64},{1... | collective-permute-start | bytes 393224 | tf_op jit(solution)/shard_map/ppermute | solution.py:80
Sparse Core Ops, SparseCore 0:
  53.7 87.3 reduce-scatter.1
  143.3 35.7 all-gather.1

commit v5 on v4

--- a/solution.py
+++ b/solution.py
@@ -9,7 +9,7 @@
 from jax.sharding import PartitionSpec as P
 
 BLOCK = 128
-TILE = 256
+TILE = 1792
 
 
 def _gate_up_kernel(n_half, n_feat, gk_ref, uk_ref, x_ref, gw_ref, uw_ref, o_ref, w_scr):

time: 215 us -> 204 us (0.949)
  Pallas kernels: 23.7 us -> 12.3 us
    pallas_call x1, Pallas kernels: 23.7 us -> 12.3 us  [gate_up(): pl.pallas_call(functools.partial(_gate_up_kernel, n_half, n_feat), grid_s...]
  transfers between devices with their start and end apart: 16 -> 16, of which waited for: 7 -> 7; matrix products, arithmetic and copies ran while one was open for 0% -> 1% of each run, Pallas kernels for 0% -> 0%
where the time goes in v5:
time: 204 us; the launch traced here: 203 us
  waiting for transfers between devices  135 us (66%)
  starting transfers between devices  31.6 us (15%)
  between operations  13.5 us (7%)
  Pallas kernels  12.3 us (6%)
  matrix products  4.16 us (2%)
  local copies, waits for them, and re-layouts  3.93 us (2%)
  other arithmetic  2.69 us (1%)
    reduce_scatter x1, waiting for transfers between devices, on_device(): summed = lax.psum_scatter(pair, COL, scatter_dimension=0, tiled=True)  87.5 us
    all_gather x1, waiting for transfers between devices, on_device(): hidden_all = lax.all_gather(hidden, COL, axis=0, tiled=True)  35.9 us
    ppermute x14, starting transfers between devices, shift(): return lax.ppermute(x, ROW, [(i, (i + k) % n) for i in range(n)])  31.5 us
    pallas_call x1, Pallas kernels, gate_up(): pl.pallas_call(functools.partial(_gate_up_kernel, n_half, n_feat), grid_s...  12.3 us
    ppermute x14, waiting for transfers between devices, shift(): return lax.ppermute(x, ROW, [(i, (i + k) % n) for i in range(n)])  11.1 us
    dot_general x1, matrix products, on_device(): jnp.dot(hidden_all, expand(down_weight, down_keep), preferred_element_typ...  4.16 us
  transfers between devices with their start and end apart: 16, of which 7 were waited for; matrix products, arithmetic and copies ran while one was open for 1% of the time, Pallas kernels for 0%

profile of v5, /device:TPU:0, one launch (start us, length us, event | category | flops | bytes accessed | tf_op | source)
XLA Modules:
  0.0 202.7 jit_solution(4525715739687707080)
XLA Ops:
  6.5 0.0 reduce-scatter.2.cloned.1.call-start
  6.5 3.1 %collective-permute-start = (bf16[64,512]{1,0:T(8,128)(2,1)}, bf16[64,512]{1,0:T(8,128)(2,1)S(1)}, u32[]{:S(2)}, u32[]{:S(2)}) collective-permute-start(bf16[64,512]{1,0:T(8,128)(2,1)} %param.7), channel_id=1, source_target_pairs={{0,16},{16,32},{32,48},{48,64},{64,80},{80,96},{96,112},{112,0},{1... | collective-permute-start | bytes 196616 | tf_op jit(solution)/shard_map/ppermute | solution.py:80
  9.7 1.9 collective-permute-start.1
  11.6 2.9 %collective-permute-start.2 = (bf16[64,512]{1,0:T(8,128)(2,1)}, bf16[64,512]{1,0:T(8,128)(2,1)S(1)}, u32[]{:S(2)}, u32[]{:S(2)}) collective-permute-start(bf16[64,512]{1,0:T(8,128)(2,1)} %param.7), channel_id=1, source_target_pairs={{0,48},{16,64},{32,80},{48,96},{64,112},{80,0},{96,16},{112,32},{1... | collective-permute-start | bytes 196616 | tf_op jit(solution)/shard_map/ppermute | solution.py:80
  14.5 1.2 collective-permute-start.3
  15.7 5.4 %collective-permute-start.4 = (bf16[64,512]{1,0:T(8,128)(2,1)}, bf16[64,512]{1,0:T(8,128)(2,1)S(1)}, u32[]{:S(2)}, u32[]{:S(2)}) collective-permute-start(bf16[64,512]{1,0:T(8,128)(2,1)} %param.7), channel_id=1, source_target_pairs={{0,80},{16,96},{32,112},{48,0},{64,16},{80,32},{96,48},{112,64},{1... | collective-permute-start | bytes 196616 | tf_op jit(solution)/shard_map/ppermute | solution.py:80
  21.1 0.9 constant_dynamic-update-slice_fusion.7
  22.0 0.0 collective-permute-done
  22.0 1.0 collective-permute-start.5
  23.0 0.0 collective-permute-done.1
  23.0 0.1 collective-permute-start.6
  23.1 0.0 collective-permute-done.2
  23.1 0.0 collective-permute-done.3
  23.2 0.2 collective-permute-done.4
  23.4 3.1 %collective-permute-done.5 = bf16[64,512]{1,0:T(8,128)(2,1)S(1)} collective-permute-done((bf16[64,512]{1,0:T(8,128)(2,1)}, bf16[64,512]{1,0:T(8,128)(2,1)S(1)}, u32[]{:S(2)}, u32[]{:S(2)}) %collective-permute-start.5) | collective-permute-done | bytes 65568 | tf_op jit(solution)/shard_map/ppermute | solution.py:80
  26.5 2.6 %collective-permute-done.6 = bf16[64,512]{1,0:T(8,128)(2,1)S(1)} collective-permute-done((bf16[64,512]{1,0:T(8,128)(2,1)}, bf16[64,512]{1,0:T(8,128)(2,1)S(1)}, u32[]{:S(2)}, u32[]{:S(2)}) %collective-permute-start.6) | collective-permute-done | bytes 65568 | tf_op jit(solution)/shard_map/ppermute | solution.py:80
  29.1 0.0 copy-start
  29.1 0.8 copy-done
  29.9 12.3 %shard_map.73 = f32[512,7168]{1,0:T(8,128)} custom-call(s32[4,28]{1,0:T(4,128)} %gk_ref.1, s32[4,28]{1,0:T(4,128)} %uk_ref.1, bf16[512,512]{1,0:T(8,128)(2,1)} %copy-done, bf16[512,3584]{1,0:T(8,128)(2,1)} %gw_ref.1, bf16[512,3584]{1,0:T(8,128)(2,1)} %uw_ref.1), custom_call_target="tpu_custom_call" | custom-call | flops 3758096384 | bytes 22544384 | tf_op jit(solution)/shard_map/pallas_call | solution.py:54
  42.2 0.0 copy-start.1
  42.2 0.0 reduce-scatter.2.cloned.1.call-update
  42.2 0.0 all-gather.2.cloned.1.call-start
  42.3 87.5 %reduce-scatter.2.cloned.1.call-done = f32[32,7168]{1,0:T(8,128)} async-done(((f32[512,7168]{1,0:T(8,128)}), f32[32,7168]{1,0:T(8,128)}) %reduce-scatter.2.cloned.1.call-update) | async-done | bytes 917520 | tf_op jit(solution)/shard_map/reduce_scatter | solution.py:88
  129.7 2.0 fusion.2
  131.7 0.0 all-gather.2.cloned.1.call-update
  131.7 0.0 copy-done.1
  131.8 0.1 copy.8
  131.9 35.9 %all-gather.2.cloned.1.call-done = bf16[512,3584]{1,0:T(8,128)(2,1)} async-done(((bf16[32,3584]{1,0:T(8,128)(2,1)}), bf16[512,3584]{1,0:T(8,128)(2,1)}) %all-gather.2.cloned.1.call-update) | async-done | bytes 3670032 | tf_op jit(solution)/shard_map/all_gather | solution.py:90
  167.8 0.0 copy-start.2
  167.8 1.0 mul.20
  168.8 1.0 copy-done.2
  169.8 4.2 %fusion = f32[512,512]{1,0:T(8,128)S(1)} fusion(bf16[512,3584]{1,0:T(8,128)(2,1)} %all-gather.2.cloned.1.call-done, bf16[3584,512]{1,0:T(8,128)(2,1)S(1)} %copy-done.2, bf16[448,8,4,128]{3,2,1,0:T(4,128)(2,1)S(1)} %bitcast.6), kind=kOutput, calls=%fused_computation.1 | convolution fusion | flops 1880883200 | bytes 12058624 | tf_op jit(solution)/shard_map/dot_general | solution.py:91
  174.0 0.1 fusion.10
  174.1 3.2 %collective-permute-start.10 = (f32[64,512]{1,0:T(8,128)S(1)}, f32[64,512]{1,0:T(8,128)S(1)}, u32[]{:S(2)}, u32[]{:S(2)}) collective-permute-start(f32[64,512]{1,0:T(8,128)S(1)} %get-tuple-element.9), channel_id=1, source_target_pairs={{0,64},{16,80},{32,96},{48,112},{64,0},{80,16},{96,32},{112,48},{1... | collective-permute-start | bytes 393224 | tf_op jit(solution)/shard_map/ppermute | solution.py:80
  177.3 2.8 %collective-permute-start.11 = (f32[64,512]{1,0:T(8,128)S(1)}, f32[64,512]{1,0:T(8,128)S(1)}, u32[]{:S(2)}, u32[]{:S(2)}) collective-permute-start(f32[64,512]{1,0:T(8,128)S(1)} %get-tuple-element.8), channel_id=1, source_target_pairs={{0,48},{16,64},{32,80},{48,96},{64,112},{80,0},{96,16},{112,32},{1... | collective-permute-start | bytes 393224 | tf_op jit(solution)/shard_map/ppermute | solution.py:80
  180.1 0.0 collective-permute-start.12
  180.1 2.1 %collective-permute-start.13 = (f32[64,512]{1,0:T(8,128)S(1)}, f32[64,512]{1,0:T(8,128)S(1)}, u32[]{:S(2)}, u32[]{:S(2)}) collective-permute-start(f32[64,512]{1,0:T(8,128)S(1)} %get-tuple-element.6), channel_id=1, source_target_pairs={{0,16},{16,32},{32,48},{48,64},{64,80},{80,96},{96,112},{112,0},{1... | collective-permute-start | bytes 393224 | tf_op jit(solution)/shard_map/ppermute | solution.py:80
  182.2 3.5 %collective-permute-start.7 = (f32[64,512]{1,0:T(8,128)S(1)}, f32[64,512]{1,0:T(8,128)S(1)}, u32[]{:S(2)}, u32[]{:S(2)}) collective-permute-start(f32[64,512]{1,0:T(8,128)S(1)} %get-tuple-element.5), channel_id=1, source_target_pairs={{0,112},{16,0},{32,16},{48,32},{64,48},{80,64},{96,80},{112,96},{1... | collective-permute-start | bytes 393224 | tf_op jit(solution)/shard_map/ppermute | solution.py:80
  185.8 0.0 collective-permute-done.10
  185.8 2.0 collective-permute-start.8
  187.8 0.0 collective-permute-done.11
  187.8 2.2 %collective-permute-start.9 = (f32[64,512]{1,0:T(8,128)S(1)}, f32[64,512]{1,0:T(8,128)S(1)}, u32[]{:S(2)}, u32[]{:S(2)}) collective-permute-start(f32[64,512]{1,0:T(8,128)S(1)} %get-tuple-element.10), channel_id=1, source_target_pairs={{0,80},{16,96},{32,112},{48,0},{64,16},{80,32},{96,48},{112,64},{1... | collective-permute-start | bytes 393224 | tf_op jit(solution)/shard_map/ppermute | solution.py:80
  190.0 2.0 %collective-permute-done.12 = f32[64,512]{1,0:T(8,128)S(1)} collective-permute-done((f32[64,512]{1,0:T(8,128)S(1)}, f32[64,512]{1,0:T(8,128)S(1)}, u32[]{:S(2)}, u32[]{:S(2)}) %collective-permute-start.12) | collective-permute-done | bytes 131104 | tf_op jit(solution)/shard_map/ppermute | solution.py:80
  192.0 0.0 collective-permute-done.13
  192.0 0.0 collective-permute-done.7
  192.0 0.0 collective-permute-done.8
  192.0 3.1 %collective-permute-done.9 = f32[64,512]{1,0:T(8,128)S(1)} collective-permute-done((f32[64,512]{1,0:T(8,128)S(1)}, f32[64,512]{1,0:T(8,128)S(1)}, u32[]{:S(2)}, u32[]{:S(2)}) %collective-permute-start.9) | collective-permute-done | bytes 131104 | tf_op jit(solution)/shard_map/ppermute | solution.py:80
  195.2 0.7 fusion.9
  (8 shorter events, 0.0 us)
Async XLA Ops:
  6.5 123.2 %reduce-scatter.2.cloned.1.call-start = ((), (), s32[]{:S(2)}) async-start(), calls=%async_computation.1 | async-start | bytes 15597568 | tf_op jit(solution)/shard_map/reduce_scatter | solution.py:88
  6.5 15.5 %collective-permute-start = (bf16[64,512]{1,0:T(8,128)(2,1)}, bf16[64,512]{1,0:T(8,128)(2,1)S(1)}, u32[]{:S(2)}, u32[]{:S(2)}) collective-permute-start(bf16[64,512]{1,0:T(8,128)(2,1)} %param.7), channel_id=1, source_target_pairs={{0,16},{16,32},{32,48},{48,64},{64,80},{80,96},{96,112},{112,0},{1... | collective-permute-start | bytes 196616 | tf_op jit(solution)/shard_map/ppermute | solution.py:80
  9.7 13.3 %collective-permute-start.1 = (bf16[64,512]{1,0:T(8,128)(2,1)}, bf16[64,512]{1,0:T(8,128)(2,1)S(1)}, u32[]{:S(2)}, u32[]{:S(2)}) collective-permute-start(bf16[64,512]{1,0:T(8,128)(2,1)} %param.7), channel_id=1, source_target_pairs={{0,32},{16,48},{32,64},{48,80},{64,96},{80,112},{96,0},{112,16},{1... | collective-permute-start | bytes 196616 | tf_op jit(solution)/shard_map/ppermute | solution.py:80
  11.6 11.5 %collective-permute-start.2 = (bf16[64,512]{1,0:T(8,128)(2,1)}, bf16[64,512]{1,0:T(8,128)(2,1)S(1)}, u32[]{:S(2)}, u32[]{:S(2)}) collective-permute-start(bf16[64,512]{1,0:T(8,128)(2,1)} %param.7), channel_id=1, source_target_pairs={{0,48},{16,64},{32,80},{48,96},{64,112},{80,0},{96,16},{112,32},{1... | collective-permute-start | bytes 196616 | tf_op jit(solution)/shard_map/ppermute | solution.py:80
  14.5 8.6 %collective-permute-start.3 = (bf16[64,512]{1,0:T(8,128)(2,1)}, bf16[64,512]{1,0:T(8,128)(2,1)S(1)}, u32[]{:S(2)}, u32[]{:S(2)}) collective-permute-start(bf16[64,512]{1,0:T(8,128)(2,1)} %param.7), channel_id=1, source_target_pairs={{0,64},{16,80},{32,96},{48,112},{64,0},{80,16},{96,32},{112,48},{1... | collective-permute-start | bytes 196616 | tf_op jit(solution)/shard_map/ppermute | solution.py:80
  15.7 7.7 %collective-permute-start.4 = (bf16[64,512]{1,0:T(8,128)(2,1)}, bf16[64,512]{1,0:T(8,128)(2,1)S(1)}, u32[]{:S(2)}, u32[]{:S(2)}) collective-permute-start(bf16[64,512]{1,0:T(8,128)(2,1)} %param.7), channel_id=1, source_target_pairs={{0,80},{16,96},{32,112},{48,0},{64,16},{80,32},{96,48},{112,64},{1... | collective-permute-start | bytes 196616 | tf_op jit(solution)/shard_map/ppermute | solution.py:80
  22.0 4.5 %collective-permute-start.5 = (bf16[64,512]{1,0:T(8,128)(2,1)}, bf16[64,512]{1,0:T(8,128)(2,1)S(1)}, u32[]{:S(2)}, u32[]{:S(2)}) collective-permute-start(bf16[64,512]{1,0:T(8,128)(2,1)} %param.7), channel_id=1, source_target_pairs={{0,96},{16,112},{32,0},{48,16},{64,32},{80,48},{96,64},{112,80},{1... | collective-permute-start | bytes 196616 | tf_op jit(solution)/shard_map/ppermute | solution.py:80
  23.0 6.0 %collective-permute-start.6 = (bf16[64,512]{1,0:T(8,128)(2,1)}, bf16[64,512]{1,0:T(8,128)(2,1)S(1)}, u32[]{:S(2)}, u32[]{:S(2)}) collective-permute-start(bf16[64,512]{1,0:T(8,128)(2,1)} %param.7), channel_id=1, source_target_pairs={{0,112},{16,0},{32,16},{48,32},{64,48},{80,64},{96,80},{112,96},{1... | collective-permute-start | bytes 196616 | tf_op jit(solution)/shard_map/ppermute | solution.py:80
  29.1 0.8 copy-start
  42.2 89.6 %copy-start.1 = (s32[28,4]{0,1:T(4,128)S(1)}, s32[28,4]{0,1:T(4,128)}, u32[]{:S(2)}) copy-start(s32[28,4]{0,1:T(4,128)} %param.13) | copy-start | bytes 1348
  42.2 125.6 %all-gather.2.cloned.1.call-start = ((), (), s32[]{:S(2)}) async-start(), calls=%async_computation.2 | async-start | bytes 3899392 | tf_op jit(solution)/shard_map/all_gather | solution.py:90
  167.8 2.0 %copy-start.2 = (bf16[3584,512]{1,0:T(8,128)(2,1)S(1)}, bf16[3584,512]{1,0:T(8,128)(2,1)}, u32[]{:S(2)}) copy-start(bf16[3584,512]{1,0:T(8,128)(2,1)} %param.10) | copy-start | bytes 11010052
  174.1 11.7 %collective-permute-start.10 = (f32[64,512]{1,0:T(8,128)S(1)}, f32[64,512]{1,0:T(8,128)S(1)}, u32[]{:S(2)}, u32[]{:S(2)}) collective-permute-start(f32[64,512]{1,0:T(8,128)S(1)} %get-tuple-element.9), channel_id=1, source_target_pairs={{0,64},{16,80},{32,96},{48,112},{64,0},{80,16},{96,32},{112,48},{1... | collective-permute-start | bytes 393224 | tf_op jit(solution)/shard_map/ppermute | solution.py:80
  177.3 10.5 %collective-permute-start.11 = (f32[64,512]{1,0:T(8,128)S(1)}, f32[64,512]{1,0:T(8,128)S(1)}, u32[]{:S(2)}, u32[]{:S(2)}) collective-permute-start(f32[64,512]{1,0:T(8,128)S(1)} %get-tuple-element.8), channel_id=1, source_target_pairs={{0,48},{16,64},{32,80},{48,96},{64,112},{80,0},{96,16},{112,32},{1... | collective-permute-start | bytes 393224 | tf_op jit(solution)/shard_map/ppermute | solution.py:80
  180.1 11.9 %collective-permute-start.12 = (f32[64,512]{1,0:T(8,128)S(1)}, f32[64,512]{1,0:T(8,128)S(1)}, u32[]{:S(2)}, u32[]{:S(2)}) collective-permute-start(f32[64,512]{1,0:T(8,128)S(1)} %get-tuple-element.7), channel_id=1, source_target_pairs={{0,32},{16,48},{32,64},{48,80},{64,96},{80,112},{96,0},{112,16},{1... | collective-permute-start | bytes 393224 | tf_op jit(solution)/shard_map/ppermute | solution.py:80
  180.1 11.9 %collective-permute-start.13 = (f32[64,512]{1,0:T(8,128)S(1)}, f32[64,512]{1,0:T(8,128)S(1)}, u32[]{:S(2)}, u32[]{:S(2)}) collective-permute-start(f32[64,512]{1,0:T(8,128)S(1)} %get-tuple-element.6), channel_id=1, source_target_pairs={{0,16},{16,32},{32,48},{48,64},{64,80},{80,96},{96,112},{112,0},{1... | collective-permute-start | bytes 393224 | tf_op jit(solution)/shard_map/ppermute | solution.py:80
  182.2 9.8 %collective-permute-start.7 = (f32[64,512]{1,0:T(8,128)S(1)}, f32[64,512]{1,0:T(8,128)S(1)}, u32[]{:S(2)}, u32[]{:S(2)}) collective-permute-start(f32[64,512]{1,0:T(8,128)S(1)} %get-tuple-element.5), channel_id=1, source_target_pairs={{0,112},{16,0},{32,16},{48,32},{64,48},{80,64},{96,80},{112,96},{1... | collective-permute-start | bytes 393224 | tf_op jit(solution)/shard_map/ppermute | solution.py:80
  185.8 6.3 %collective-permute-start.8 = (f32[64,512]{1,0:T(8,128)S(1)}, f32[64,512]{1,0:T(8,128)S(1)}, u32[]{:S(2)}, u32[]{:S(2)}) collective-permute-start(f32[64,512]{1,0:T(8,128)S(1)} %get-tuple-element.11), channel_id=1, source_target_pairs={{0,96},{16,112},{32,0},{48,16},{64,32},{80,48},{96,64},{112,80},{1... | collective-permute-start | bytes 393224 | tf_op jit(solution)/shard_map/ppermute | solution.py:80
  187.8 7.4 %collective-permute-start.9 = (f32[64,512]{1,0:T(8,128)S(1)}, f32[64,512]{1,0:T(8,128)S(1)}, u32[]{:S(2)}, u32[]{:S(2)}) collective-permute-start(f32[64,512]{1,0:T(8,128)S(1)} %get-tuple-element.10), channel_id=1, source_target_pairs={{0,80},{16,96},{32,112},{48,0},{64,16},{80,32},{96,48},{112,64},{1... | collective-permute-start | bytes 393224 | tf_op jit(solution)/shard_map/ppermute | solution.py:80
Sparse Core Ops, SparseCore 0:
  42.3 87.3 reduce-scatter.1
  131.9 35.9 all-gather.1

commit v6 on v5

--- a/solution.py
+++ b/solution.py
@@ -76,14 +76,25 @@
     return masked.reshape(rows, cols)
 
 
-def shift(x, k, n):
-    return lax.ppermute(x, ROW, [(i, (i + k) % n) for i in range(n)])
+def partner(x, mask, n):
+    return lax.ppermute(x, ROW, [(i, i ^ mask) for i in range(n)])
+
+
+def row_masks(n):
+    masks = [1 << b for b in range(n.bit_length() - 1)]
+    if 2 in masks:
+        masks.remove(2)
+        masks.append(2)
+    return masks
 
 
 def on_device(tokens, gate_weight, up_weight, down_weight, gate_keep, up_keep, down_keep):
     n = lax.axis_size(ROW)
     hidden_cols = gate_weight.shape[1]
-    features = jnp.concatenate([tokens] + [shift(tokens, k, n) for k in range(1, n)], axis=0)
+    masks = row_masks(n)
+    features = tokens
+    for mask in masks:
+        features = jnp.concatenate([features, partner(features, mask, n)], axis=0)
     pair = gate_up(features, gate_weight, up_weight, gate_keep, up_keep)
     summed = lax.psum_scatter(pair, COL, scatter_dimension=0, tiled=True)
     hidden = (jax.nn.silu(summed[:, :hidden_cols]) * summed[:, hidden_cols:]).astype(jnp.bfloat16)
@@ -91,10 +102,10 @@
     partial_out = jnp.dot(
         hidden_all, expand(down_weight, down_keep), preferred_element_type=jnp.float32
     )
-    t = tokens.shape[0]
-    total = partial_out[:t]
-    for k in range(1, n):
-        total = total + shift(partial_out[k * t:(k + 1) * t], -k, n)
+    total = partial_out
+    for mask in reversed(masks):
+        half = total.shape[0] // 2
+        total = total[:half] + partner(total[half:], mask, n)
     return total.astype(jnp.bfloat16)
 
 

time: 204 us -> 215 us (1.054)
  waiting for transfers between devices: 135 us -> 160 us
  starting transfers between devices: 31.6 us -> 16.5 us
  other arithmetic: 2.69 us -> 6.12 us
    ppermute x14 -> x6, waiting for transfers between devices: 11.1 us -> 32.8 us  [partner(): return lax.ppermute(x, ROW, [(i, i ^ mask) for i in range(n)])]
    ppermute x14 -> x6, starting transfers between devices: 31.5 us -> 16.5 us  [partner(): return lax.ppermute(x, ROW, [(i, i ^ mask) for i in range(n)])]
    reduce_scatter x1, waiting for transfers between devices: 87.5 us -> 91 us  [on_device(): summed = lax.psum_scatter(pair, COL, scatter_dimension=0, tiled=True)]
    concatenate x0 -> x3, other arithmetic: none -> 3.37 us  [on_device(): features = jnp.concatenate([features, partner(features, mask, n)], axis=0)]
  transfers between devices with their start and end apart: 16 -> 8, of which waited for: 7 -> 8; matrix products, arithmetic and copies ran while one was open for 1% -> 0% of each run, Pallas kernels for 0% -> 0%
where the time goes in v6:
time: 215 us
  waiting for transfers between devices  160 us (74%)
  starting transfers between devices  16.5 us (8%)
  between operations  13.5 us (6%)
  Pallas kernels  12.5 us (6%)
  other arithmetic  6.12 us (3%)
  matrix products  4.16 us (2%)
  local copies, waits for them, and re-layouts  2.21 us (1%)
    reduce_scatter x1, waiting for transfers between devices, on_device(): summed = lax.psum_scatter(pair, COL, scatter_dimension=0, tiled=True)  91 us
    all_gather x1, waiting for transfers between devices, on_device(): hidden_all = lax.all_gather(hidden, COL, axis=0, tiled=True)  35.9 us
    ppermute x6, waiting for transfers between devices, partner(): return lax.ppermute(x, ROW, [(i, i ^ mask) for i in range(n)])  32.8 us
    ppermute x6, starting transfers between devices, partner(): return lax.ppermute(x, ROW, [(i, i ^ mask) for i in range(n)])  16.5 us
    pallas_call x1, Pallas kernels, gate_up(): pl.pallas_call(functools.partial(_gate_up_kernel, n_half, n_feat), grid_s...  12.5 us
  transfers between devices with their start and end apart: 8, of which 8 were waited for; matrix products, arithmetic and copies ran while one was open for 0% of the time, Pallas kernels for 0%

profile of v6, /device:TPU:0, one launch (start us, length us, event | category | flops | bytes accessed | tf_op | source)
XLA Modules:
  0.0 214.7 jit_solution(135047386409092582)
XLA Ops:
  6.5 0.0 reduce-scatter.2.cloned.1.call-start
  6.5 3.1 %collective-permute-start = (bf16[64,512]{1,0:T(8,128)(2,1)}, bf16[64,512]{1,0:T(8,128)(2,1)S(1)}, u32[]{:S(2)}, u32[]{:S(2)}) collective-permute-start(bf16[64,512]{1,0:T(8,128)(2,1)} %param.7), channel_id=1, source_target_pairs={{0,16},{16,0},{32,48},{48,32},{64,80},{80,64},{96,112},{112,96},{1... | collective-permute-start | bytes 196616 | tf_op jit(solution)/shard_map/ppermute | solution.py:80
  9.7 2.8 %collective-permute-done = bf16[64,512]{1,0:T(8,128)(2,1)S(1)} collective-permute-done((bf16[64,512]{1,0:T(8,128)(2,1)}, bf16[64,512]{1,0:T(8,128)(2,1)S(1)}, u32[]{:S(2)}, u32[]{:S(2)}) %collective-permute-start) | collective-permute-done | bytes 65568 | tf_op jit(solution)/shard_map/ppermute | solution.py:80
  12.5 0.8 pad_maximum_fusion.2
  13.4 4.1 %collective-permute-start.1 = (bf16[128,512]{1,0:T(8,128)(2,1)S(1)}, bf16[128,512]{1,0:T(8,128)(2,1)S(1)}, u32[]{:S(2)}, u32[]{:S(2)}) collective-permute-start(bf16[128,512]{1,0:T(8,128)(2,1)S(1)} %pad_maximum_fusion.2), channel_id=1, source_target_pairs={{0,64},{16,80},{32,96},{48,112},{64,0},{80,16},{96,32},{112,48},{1... | collective-permute-start | bytes 393224 | tf_op jit(solution)/shard_map/ppermute | solution.py:80
  17.4 2.9 %collective-permute-done.1 = bf16[128,512]{1,0:T(8,128)(2,1)S(1)} collective-permute-done((bf16[128,512]{1,0:T(8,128)(2,1)S(1)}, bf16[128,512]{1,0:T(8,128)(2,1)S(1)}, u32[]{:S(2)}, u32[]{:S(2)}) %collective-permute-start.1) | collective-permute-done | bytes 131104 | tf_op jit(solution)/shard_map/ppermute | solution.py:80
  20.4 0.9 pad_maximum_fusion.1
  21.2 1.6 collective-permute-start.2
  22.9 4.8 %collective-permute-done.2 = bf16[256,512]{1,0:T(8,128)(2,1)S(1)} collective-permute-done((bf16[256,512]{1,0:T(8,128)(2,1)S(1)}, bf16[256,512]{1,0:T(8,128)(2,1)S(1)}, u32[]{:S(2)}, u32[]{:S(2)}) %collective-permute-start.2) | collective-permute-done | bytes 262176 | tf_op jit(solution)/shard_map/ppermute | solution.py:80
  27.7 1.7 pad_maximum_fusion.x_ref
  29.4 12.5 %shard_map.73 = f32[512,7168]{1,0:T(8,128)} custom-call(s32[4,28]{1,0:T(4,128)} %gk_ref.1, s32[4,28]{1,0:T(4,128)} %uk_ref.1, bf16[512,512]{1,0:T(8,128)(2,1)} %pad_maximum_fusion.x_ref, bf16[512,3584]{1,0:T(8,128)(2,1)} %gw_ref.1, bf16[512,3584]{1,0:T(8,128)(2,1)} %uw_ref.1), custom_call_target="tpu_custom_call" | custom-call | flops 3758096384 | bytes 22544384 | tf_op jit(solution)/shard_map/pallas_call | solution.py:54
  41.8 0.0 copy-start
  41.8 0.0 reduce-scatter.2.cloned.1.call-update
  41.9 0.0 all-gather.2.cloned.1.call-start
  41.9 91.0 %reduce-scatter.2.cloned.1.call-done = f32[32,7168]{1,0:T(8,128)} async-done(((f32[512,7168]{1,0:T(8,128)}), f32[32,7168]{1,0:T(8,128)}) %reduce-scatter.2.cloned.1.call-update) | async-done | bytes 917520 | tf_op jit(solution)/shard_map/reduce_scatter | solution.py:99
  132.9 2.0 fusion.2
  134.9 0.0 all-gather.2.cloned.1.call-update
  134.9 0.0 copy-done
  134.9 0.1 copy.8
  135.0 35.9 %all-gather.2.cloned.1.call-done = bf16[512,3584]{1,0:T(8,128)(2,1)} async-done(((bf16[32,3584]{1,0:T(8,128)(2,1)}), bf16[512,3584]{1,0:T(8,128)(2,1)}) %all-gather.2.cloned.1.call-update) | async-done | bytes 3670032 | tf_op jit(solution)/shard_map/all_gather | solution.py:101
  171.0 0.0 copy-start.1
  171.0 1.0 mul.20
  172.0 1.0 copy-done.1
  173.0 4.2 %fusion = f32[512,512]{1,0:T(8,128)S(1)} fusion(bf16[512,3584]{1,0:T(8,128)(2,1)} %all-gather.2.cloned.1.call-done, bf16[3584,512]{1,0:T(8,128)(2,1)S(1)} %copy-done.1, bf16[448,8,4,128]{3,2,1,0:T(4,128)(2,1)S(1)} %bitcast.6), kind=kOutput, calls=%fused_computation.1 | convolution fusion | flops 1880883200 | bytes 12058624 | tf_op jit(solution)/shard_map/dot_general | solution.py:102
  177.2 1.6 collective-permute-start.3
  178.8 12.5 %collective-permute-done.3 = f32[256,512]{1,0:T(8,128)S(1)} collective-permute-done((f32[256,512]{1,0:T(8,128)S(1)}, f32[256,512]{1,0:T(8,128)S(1)}, u32[]{:S(2)}, u32[]{:S(2)}) %collective-permute-start.3) | collective-permute-done | bytes 524320 | tf_op jit(solution)/shard_map/ppermute | solution.py:80
  191.3 0.1 slice_add_fusion
  191.5 3.2 %collective-permute-start.4 = (f32[128,512]{1,0:T(8,128)S(1)}, f32[128,512]{1,0:T(8,128)S(1)}, u32[]{:S(2)}, u32[]{:S(2)}) collective-permute-start(f32[128,512]{1,0:T(8,128)S(1)} %slice.37), channel_id=1, source_target_pairs={{0,64},{16,80},{32,96},{48,112},{64,0},{80,16},{96,32},{112,48},{1... | collective-permute-start | bytes 786440 | tf_op jit(solution)/shard_map/ppermute | solution.py:80
  194.7 5.9 %collective-permute-done.4 = f32[128,512]{1,0:T(8,128)S(1)} collective-permute-done((f32[128,512]{1,0:T(8,128)S(1)}, f32[128,512]{1,0:T(8,128)S(1)}, u32[]{:S(2)}, u32[]{:S(2)}) %collective-permute-start.4) | collective-permute-done | bytes 262176 | tf_op jit(solution)/shard_map/ppermute | solution.py:80
  200.7 2.8 %collective-permute-start.5 = (f32[64,512]{1,0:T(8,128)S(1)}, f32[64,512]{1,0:T(8,128)S(1)}, u32[]{:S(2)}, u32[]{:S(2)}) collective-permute-start(f32[64,512]{1,0:T(8,128)S(1)} %slice.39), channel_id=1, source_target_pairs={{0,16},{16,0},{32,48},{48,32},{64,80},{80,64},{96,112},{112,96},{1... | collective-permute-start | bytes 393224 | tf_op jit(solution)/shard_map/ppermute | solution.py:80
  203.5 3.8 %collective-permute-done.5 = f32[64,512]{1,0:T(8,128)S(1)} collective-permute-done((f32[64,512]{1,0:T(8,128)S(1)}, f32[64,512]{1,0:T(8,128)S(1)}, u32[]{:S(2)}, u32[]{:S(2)}) %collective-permute-start.5) | collective-permute-done | bytes 131104 | tf_op jit(solution)/shard_map/ppermute | solution.py:80
  207.2 0.6 fusion.3
  (5 shorter events, 0.1 us)
Async XLA Ops:
  6.5 126.4 %reduce-scatter.2.cloned.1.call-start = ((), (), s32[]{:S(2)}) async-start(), calls=%async_computation.1 | async-start | bytes 15597568 | tf_op jit(solution)/shard_map/reduce_scatter | solution.py:99
  6.5 6.0 %collective-permute-start = (bf16[64,512]{1,0:T(8,128)(2,1)}, bf16[64,512]{1,0:T(8,128)(2,1)S(1)}, u32[]{:S(2)}, u32[]{:S(2)}) collective-permute-start(bf16[64,512]{1,0:T(8,128)(2,1)} %param.7), channel_id=1, source_target_pairs={{0,16},{16,0},{32,48},{48,32},{64,80},{80,64},{96,112},{112,96},{1... | collective-permute-start | bytes 196616 | tf_op jit(solution)/shard_map/ppermute | solution.py:80
  13.4 7.0 %collective-permute-start.1 = (bf16[128,512]{1,0:T(8,128)(2,1)S(1)}, bf16[128,512]{1,0:T(8,128)(2,1)S(1)}, u32[]{:S(2)}, u32[]{:S(2)}) collective-permute-start(bf16[128,512]{1,0:T(8,128)(2,1)S(1)} %pad_maximum_fusion.2), channel_id=1, source_target_pairs={{0,64},{16,80},{32,96},{48,112},{64,0},{80,16},{96,32},{112,48},{1... | collective-permute-start | bytes 393224 | tf_op jit(solution)/shard_map/ppermute | solution.py:80
  21.2 6.5 %collective-permute-start.2 = (bf16[256,512]{1,0:T(8,128)(2,1)S(1)}, bf16[256,512]{1,0:T(8,128)(2,1)S(1)}, u32[]{:S(2)}, u32[]{:S(2)}) collective-permute-start(bf16[256,512]{1,0:T(8,128)(2,1)S(1)} %pad_maximum_fusion.1), channel_id=1, source_target_pairs={{0,32},{16,48},{32,0},{48,16},{64,96},{80,112},{96,64},{112,80},{1... | collective-permute-start | bytes 786440 | tf_op jit(solution)/shard_map/ppermute | solution.py:80
  41.8 93.1 %copy-start = (s32[28,4]{0,1:T(4,128)S(1)}, s32[28,4]{0,1:T(4,128)}, u32[]{:S(2)}) copy-start(s32[28,4]{0,1:T(4,128)} %param.13) | copy-start | bytes 1348
  41.9 129.1 %all-gather.2.cloned.1.call-start = ((), (), s32[]{:S(2)}) async-start(), calls=%async_computation.2 | async-start | bytes 3899392 | tf_op jit(solution)/shard_map/all_gather | solution.py:101
  171.0 2.0 copy-start.1
  177.2 14.1 %collective-permute-start.3 = (f32[256,512]{1,0:T(8,128)S(1)}, f32[256,512]{1,0:T(8,128)S(1)}, u32[]{:S(2)}, u32[]{:S(2)}) collective-permute-start(f32[256,512]{1,0:T(8,128)S(1)} %slice.35), channel_id=1, source_target_pairs={{0,32},{16,48},{32,0},{48,16},{64,96},{80,112},{96,64},{112,80},{1... | collective-permute-start | bytes 1572872 | tf_op jit(solution)/shard_map/ppermute | solution.py:80
  191.5 9.2 %collective-permute-start.4 = (f32[128,512]{1,0:T(8,128)S(1)}, f32[128,512]{1,0:T(8,128)S(1)}, u32[]{:S(2)}, u32[]{:S(2)}) collective-permute-start(f32[128,512]{1,0:T(8,128)S(1)} %slice.37), channel_id=1, source_target_pairs={{0,64},{16,80},{32,96},{48,112},{64,0},{80,16},{96,32},{112,48},{1... | collective-permute-start | bytes 786440 | tf_op jit(solution)/shard_map/ppermute | solution.py:80
  200.7 6.6 %collective-permute-start.5 = (f32[64,512]{1,0:T(8,128)S(1)}, f32[64,512]{1,0:T(8,128)S(1)}, u32[]{:S(2)}, u32[]{:S(2)}) collective-permute-start(f32[64,512]{1,0:T(8,128)S(1)} %slice.39), channel_id=1, source_target_pairs={{0,16},{16,0},{32,48},{48,32},{64,80},{80,64},{96,112},{112,96},{1... | collective-permute-start | bytes 393224 | tf_op jit(solution)/shard_map/ppermute | solution.py:80
Sparse Core Ops, SparseCore 0:
  42.0 90.8 reduce-scatter.1
  135.0 35.8 all-gather.1

commit v7 on v5

--- a/solution.py
+++ b/solution.py
@@ -12,55 +12,54 @@
 TILE = 1792
 
 
-def _gate_up_kernel(n_half, n_feat, gk_ref, uk_ref, x_ref, gw_ref, uw_ref, o_ref, w_scr):
+def _gate_up_kernel(part, n_feat, gk_ref, uk_ref, x_ref, gw_ref, uw_ref, o_ref, w_scr):
     j = pl.program_id(0)
 
-    def build(w_ref, k_ref, jj):
+    def build(w_ref, k_ref):
         for kb in range(n_feat):
             for hb in range(TILE // BLOCK):
-                k = k_ref[kb, jj * (TILE // BLOCK) + hb]
+                k = k_ref[kb, part * (TILE // BLOCK) + hb]
                 rows = slice(kb * BLOCK, (kb + 1) * BLOCK)
                 cols = slice(hb * BLOCK, (hb + 1) * BLOCK)
                 sub = w_ref[rows, cols]
                 w_scr[rows, cols] = jnp.where(k == 0, jnp.zeros_like(sub), sub)
 
-    @pl.when(j < n_half)
+    @pl.when(j == 0)
     def _():
-        build(gw_ref, gk_ref, j)
+        build(gw_ref, gk_ref)
 
-    @pl.when(j >= n_half)
+    @pl.when(j == 1)
     def _():
-        build(uw_ref, uk_ref, j - n_half)
+        build(uw_ref, uk_ref)
 
     o_ref[...] = jnp.dot(x_ref[...], w_scr[...], preferred_element_type=jnp.float32)
 
 
-def gate_up(x, gw, uw, gk, uk):
+def gate_up(x, gw, uw, gk, uk, part):
     t, f = x.shape
-    h = gw.shape[1]
-    n_half = h // TILE
     n_feat = f // BLOCK
     grid_spec = pltpu.PrefetchScalarGridSpec(
         num_scalar_prefetch=2,
-        grid=(2 * n_half,),
+        grid=(2,),
         in_specs=[
             pl.BlockSpec((t, f), lambda j, gk, uk: (0, 0)),
-            pl.BlockSpec((f, TILE), lambda j, gk, uk: (0, jnp.minimum(j, n_half - 1))),
-            pl.BlockSpec((f, TILE), lambda j, gk, uk: (0, jnp.maximum(j - n_half, 0))),
+            pl.BlockSpec((f, TILE), lambda j, gk, uk: (0, part)),
+            pl.BlockSpec((f, TILE), lambda j, gk, uk: (0, part)),
         ],
         out_specs=pl.BlockSpec((t, TILE), lambda j, gk, uk: (0, j)),
         scratch_shapes=[pltpu.VMEM((f, TILE), x.dtype)],
     )
     return pl.pallas_call(
-        functools.partial(_gate_up_kernel, n_half, n_feat),
+        functools.partial(_gate_up_kernel, part, n_feat),
         grid_spec=grid_spec,
-        out_shape=jax.ShapeDtypeStruct((t, 2 * h), jnp.float32),
+        out_shape=jax.ShapeDtypeStruct((t, 2 * TILE), jnp.float32),
         compiler_params=pltpu.CompilerParams(dimension_semantics=("arbitrary",)),
         cost_estimate=pl.CostEstimate(
-            flops=2 * t * f * 2 * h, transcendentals=0,
-            bytes_accessed=2 * (t * f + 2 * f * h) + 4 * t * 2 * h,
+            flops=2 * t * f * 2 * TILE, transcendentals=0,
+            bytes_accessed=2 * (t * f + 2 * f * TILE) + 4 * t * 2 * TILE,
         ),
     )(gk, uk, x, gw, uw)
+
 
 ROW = ("z", "x_hi")
 COL = ("x_lo", "y", "core")
@@ -84,9 +83,14 @@
     n = lax.axis_size(ROW)
     hidden_cols = gate_weight.shape[1]
     features = jnp.concatenate([tokens] + [shift(tokens, k, n) for k in range(1, n)], axis=0)
-    pair = gate_up(features, gate_weight, up_weight, gate_keep, up_keep)
-    summed = lax.psum_scatter(pair, COL, scatter_dimension=0, tiled=True)
-    hidden = (jax.nn.silu(summed[:, :hidden_cols]) * summed[:, hidden_cols:]).astype(jnp.bfloat16)
+    hidden_parts = []
+    for part in range(hidden_cols // TILE):
+        pair = gate_up(features, gate_weight, up_weight, gate_keep, up_keep, part)
+        summed = lax.psum_scatter(pair, COL, scatter_dimension=0, tiled=True)
+        hidden_parts.append(
+            (jax.nn.silu(summed[:, :TILE]) * summed[:, TILE:]).astype(jnp.bfloat16)
+        )
+    hidden = jnp.concatenate(hidden_parts, axis=1)
     hidden_all = lax.all_gather(hidden, COL, axis=0, tiled=True)
     partial_out = jnp.dot(
         hidden_all, expand(down_weight, down_keep), preferred_element_type=jnp.float32

time: 204 us -> 256 us (1.25)
  waiting for transfers between devices: 135 us -> 183 us
  Pallas kernels: 12.3 us -> 15.9 us
    reduce_scatter x1 -> x2, waiting for transfers between devices: 87.5 us -> 137 us  [on_device(): summed = lax.psum_scatter(pair, COL, scatter_dimension=0, tiled=True)]
    pallas_call x1 -> x2, Pallas kernels: 12.3 us -> 15.9 us  [gate_up(): pl.pallas_call(functools.partial(_gate_up_kernel, part, n_feat), grid_spe...]
  transfers between devices with their start and end apart: 16 -> 17, of which waited for: 7 -> 8; matrix products, arithmetic and copies ran while one was open for 1% -> 1% of each run, Pallas kernels for 0% -> 3%
where the time goes in v7:
time: 256 us; the launch traced here: 255 us
  waiting for transfers between devices  183 us (71%)
  starting transfers between devices  31.6 us (12%)
  Pallas kernels  15.9 us (6%)
  between operations  13.2 us (5%)
  matrix products  4.16 us (2%)
  local copies, waits for them, and re-layouts  3.93 us (2%)
  other arithmetic  3.66 us (1%)
    reduce_scatter x2, waiting for transfers between devices, on_device(): summed = lax.psum_scatter(pair, COL, scatter_dimension=0, tiled=True)  137 us
    all_gather x1, waiting for transfers between devices, on_device(): hidden_all = lax.all_gather(hidden, COL, axis=0, tiled=True)  34.9 us
    ppermute x14, starting transfers between devices, shift(): return lax.ppermute(x, ROW, [(i, (i + k) % n) for i in range(n)])  31.5 us
    pallas_call x2, Pallas kernels, gate_up(): pl.pallas_call(functools.partial(_gate_up_kernel, part, n_feat), grid_spe...  15.9 us
    ppermute x14, waiting for transfers between devices, shift(): return lax.ppermute(x, ROW, [(i, (i + k) % n) for i in range(n)])  11.1 us
  transfers between devices with their start and end apart: 17, of which 8 were waited for; matrix products, arithmetic and copies ran while one was open for 1% of the time, Pallas kernels for 3%

profile of v7, /device:TPU:0, one launch (start us, length us, event | category | flops | bytes accessed | tf_op | source)
XLA Modules:
  0.0 255.0 jit_solution(12884142712097708435)
XLA Ops:
  6.5 0.0 reduce-scatter.5.cloned.1.call-start
  6.5 3.1 %collective-permute-start = (bf16[64,512]{1,0:T(8,128)(2,1)}, bf16[64,512]{1,0:T(8,128)(2,1)S(1)}, u32[]{:S(2)}, u32[]{:S(2)}) collective-permute-start(bf16[64,512]{1,0:T(8,128)(2,1)} %param.7), channel_id=1, source_target_pairs={{0,16},{16,32},{32,48},{48,64},{64,80},{80,96},{96,112},{112,0},{1... | collective-permute-start | bytes 196616 | tf_op jit(solution)/shard_map/ppermute | solution.py:79
  9.7 1.9 collective-permute-start.1
  11.6 2.9 %collective-permute-start.2 = (bf16[64,512]{1,0:T(8,128)(2,1)}, bf16[64,512]{1,0:T(8,128)(2,1)S(1)}, u32[]{:S(2)}, u32[]{:S(2)}) collective-permute-start(bf16[64,512]{1,0:T(8,128)(2,1)} %param.7), channel_id=1, source_target_pairs={{0,48},{16,64},{32,80},{48,96},{64,112},{80,0},{96,16},{112,32},{1... | collective-permute-start | bytes 196616 | tf_op jit(solution)/shard_map/ppermute | solution.py:79
  14.5 1.2 collective-permute-start.3
  15.7 5.4 %collective-permute-start.4 = (bf16[64,512]{1,0:T(8,128)(2,1)}, bf16[64,512]{1,0:T(8,128)(2,1)S(1)}, u32[]{:S(2)}, u32[]{:S(2)}) collective-permute-start(bf16[64,512]{1,0:T(8,128)(2,1)} %param.7), channel_id=1, source_target_pairs={{0,80},{16,96},{32,112},{48,0},{64,16},{80,32},{96,48},{112,64},{1... | collective-permute-start | bytes 196616 | tf_op jit(solution)/shard_map/ppermute | solution.py:79
  21.1 0.9 constant_dynamic-update-slice_fusion.7
  22.0 0.0 collective-permute-done
  22.0 1.0 collective-permute-start.5
  23.0 0.0 collective-permute-done.1
  23.0 0.1 collective-permute-start.6
  23.1 0.0 collective-permute-done.2
  23.1 0.0 collective-permute-done.3
  23.2 0.2 collective-permute-done.4
  23.4 3.1 %collective-permute-done.5 = bf16[64,512]{1,0:T(8,128)(2,1)S(1)} collective-permute-done((bf16[64,512]{1,0:T(8,128)(2,1)}, bf16[64,512]{1,0:T(8,128)(2,1)S(1)}, u32[]{:S(2)}, u32[]{:S(2)}) %collective-permute-start.5) | collective-permute-done | bytes 65568 | tf_op jit(solution)/shard_map/ppermute | solution.py:79
  26.5 2.6 %collective-permute-done.6 = bf16[64,512]{1,0:T(8,128)(2,1)S(1)} collective-permute-done((bf16[64,512]{1,0:T(8,128)(2,1)}, bf16[64,512]{1,0:T(8,128)(2,1)S(1)}, u32[]{:S(2)}, u32[]{:S(2)}) %collective-permute-start.6) | collective-permute-done | bytes 65568 | tf_op jit(solution)/shard_map/ppermute | solution.py:79
  29.1 0.0 copy-start
  29.1 0.8 copy-done
  29.9 7.9 %shard_map.74 = f32[512,3584]{1,0:T(8,128)} custom-call(s32[4,28]{1,0:T(4,128)} %gk_ref.3, s32[4,28]{1,0:T(4,128)} %uk_ref.3, bf16[512,512]{1,0:T(8,128)(2,1)} %copy-done, bf16[512,3584]{1,0:T(8,128)(2,1)} %gw_ref.3, bf16[512,3584]{1,0:T(8,128)(2,1)} %uw_ref.3), custom_call_target="tpu_custom_call" | custom-call | flops 1879048192 | bytes 11534336 | tf_op jit(solution)/shard_map/pallas_call | solution.py:52
  37.8 0.0 reduce-scatter.5.cloned.1.call-update
  37.8 0.0 reduce-scatter.3.cloned.1.call-start
  37.9 7.9 %shard_map.73 = f32[512,3584]{1,0:T(8,128)} custom-call(s32[4,28]{1,0:T(4,128)} %gk_ref.3, s32[4,28]{1,0:T(4,128)} %uk_ref.3, bf16[512,512]{1,0:T(8,128)(2,1)} %copy-done, bf16[512,3584]{1,0:T(8,128)(2,1)} %gw_ref.3, bf16[512,3584]{1,0:T(8,128)(2,1)} %uw_ref.3), custom_call_target="tpu_custom_call" | custom-call | flops 1879048192 | bytes 11534336 | tf_op jit(solution)/shard_map/pallas_call | solution.py:52
  45.8 0.0 copy-start.1
  45.8 0.0 reduce-scatter.3.cloned.1.call-update
  45.8 0.0 all-gather.2.cloned.1.call-start
  45.9 63.7 %reduce-scatter.5.cloned.1.call-done = f32[32,3584]{1,0:T(8,128)} async-done(((f32[512,3584]{1,0:T(8,128)}), f32[32,3584]{1,0:T(8,128)}) %reduce-scatter.5.cloned.1.call-update) | async-done | bytes 458768 | tf_op jit(solution)/shard_map/reduce_scatter | solution.py:89
  109.6 1.1 fusion.2
  110.7 72.8 %reduce-scatter.3.cloned.1.call-done = f32[32,3584]{1,0:T(8,128)} async-done(((f32[512,3584]{1,0:T(8,128)}), f32[32,3584]{1,0:T(8,128)}) %reduce-scatter.3.cloned.1.call-update) | async-done | bytes 458768 | tf_op jit(solution)/shard_map/reduce_scatter | solution.py:89
  183.6 1.1 fusion.3
  184.7 0.7 pad_maximum_fusion
  185.4 0.0 all-gather.2.cloned.1.call-update
  185.4 0.0 copy-done.1
  185.4 0.1 copy.8
  185.5 34.9 %all-gather.2.cloned.1.call-done = bf16[512,3584]{1,0:T(8,128)(2,1)} async-done(((bf16[32,3584]{1,0:T(8,128)(2,1)}), bf16[512,3584]{1,0:T(8,128)(2,1)}) %all-gather.2.cloned.1.call-update) | async-done | bytes 3670032 | tf_op jit(solution)/shard_map/all_gather | solution.py:94
  220.4 0.0 copy-start.2
  220.4 1.0 mul.28
  221.4 1.0 copy-done.2
  222.4 4.2 %fusion = f32[512,512]{1,0:T(8,128)S(1)} fusion(bf16[512,3584]{1,0:T(8,128)(2,1)} %all-gather.2.cloned.1.call-done, bf16[3584,512]{1,0:T(8,128)(2,1)S(1)} %copy-done.2, bf16[448,8,4,128]{3,2,1,0:T(4,128)(2,1)S(1)} %bitcast.6), kind=kOutput, calls=%fused_computation.1 | convolution fusion | flops 1880883200 | bytes 12058624 | tf_op jit(solution)/shard_map/dot_general | solution.py:95
  226.6 0.1 fusion.11
  226.7 3.2 %collective-permute-start.10 = (f32[64,512]{1,0:T(8,128)S(1)}, f32[64,512]{1,0:T(8,128)S(1)}, u32[]{:S(2)}, u32[]{:S(2)}) collective-permute-start(f32[64,512]{1,0:T(8,128)S(1)} %get-tuple-element.9), channel_id=1, source_target_pairs={{0,64},{16,80},{32,96},{48,112},{64,0},{80,16},{96,32},{112,48},{1... | collective-permute-start | bytes 393224 | tf_op jit(solution)/shard_map/ppermute | solution.py:79
  229.9 2.8 %collective-permute-start.11 = (f32[64,512]{1,0:T(8,128)S(1)}, f32[64,512]{1,0:T(8,128)S(1)}, u32[]{:S(2)}, u32[]{:S(2)}) collective-permute-start(f32[64,512]{1,0:T(8,128)S(1)} %get-tuple-element.8), channel_id=1, source_target_pairs={{0,48},{16,64},{32,80},{48,96},{64,112},{80,0},{96,16},{112,32},{1... | collective-permute-start | bytes 393224 | tf_op jit(solution)/shard_map/ppermute | solution.py:79
  232.7 0.0 collective-permute-start.12
  232.7 2.1 collective-permute-start.13
  234.8 3.5 %collective-permute-start.7 = (f32[64,512]{1,0:T(8,128)S(1)}, f32[64,512]{1,0:T(8,128)S(1)}, u32[]{:S(2)}, u32[]{:S(2)}) collective-permute-start(f32[64,512]{1,0:T(8,128)S(1)} %get-tuple-element.5), channel_id=1, source_target_pairs={{0,112},{16,0},{32,16},{48,32},{64,48},{80,64},{96,80},{112,96},{1... | collective-permute-start | bytes 393224 | tf_op jit(solution)/shard_map/ppermute | solution.py:79
  238.4 0.0 collective-permute-done.10
  238.4 2.0 collective-permute-start.8
  240.4 0.0 collective-permute-done.11
  240.4 2.2 collective-permute-start.9
  242.6 2.0 collective-permute-done.12
  244.6 0.0 collective-permute-done.13
  244.6 0.0 collective-permute-done.7
  244.6 0.0 collective-permute-done.8
  244.6 3.1 %collective-permute-done.9 = f32[64,512]{1,0:T(8,128)S(1)} collective-permute-done((f32[64,512]{1,0:T(8,128)S(1)}, f32[64,512]{1,0:T(8,128)S(1)}, u32[]{:S(2)}, u32[]{:S(2)}) %collective-permute-start.9) | collective-permute-done | bytes 131104 | tf_op jit(solution)/shard_map/ppermute | solution.py:79
  247.8 0.7 fusion.10
  (8 shorter events, 0.0 us)
Async XLA Ops:
  6.5 103.1 %reduce-scatter.5.cloned.1.call-start = ((), (), s32[]{:S(2)}) async-start(), calls=%async_computation.3 | async-start | bytes 7798784 | tf_op jit(solution)/shard_map/reduce_scatter | solution.py:89
  6.5 15.5 %collective-permute-start = (bf16[64,512]{1,0:T(8,128)(2,1)}, bf16[64,512]{1,0:T(8,128)(2,1)S(1)}, u32[]{:S(2)}, u32[]{:S(2)}) collective-permute-start(bf16[64,512]{1,0:T(8,128)(2,1)} %param.7), channel_id=1, source_target_pairs={{0,16},{16,32},{32,48},{48,64},{64,80},{80,96},{96,112},{112,0},{1... | collective-permute-start | bytes 196616 | tf_op jit(solution)/shard_map/ppermute | solution.py:79
  9.7 13.3 %collective-permute-start.1 = (bf16[64,512]{1,0:T(8,128)(2,1)}, bf16[64,512]{1,0:T(8,128)(2,1)S(1)}, u32[]{:S(2)}, u32[]{:S(2)}) collective-permute-start(bf16[64,512]{1,0:T(8,128)(2,1)} %param.7), channel_id=1, source_target_pairs={{0,32},{16,48},{32,64},{48,80},{64,96},{80,112},{96,0},{112,16},{1... | collective-permute-start | bytes 196616 | tf_op jit(solution)/shard_map/ppermute | solution.py:79
  11.6 11.5 %collective-permute-start.2 = (bf16[64,512]{1,0:T(8,128)(2,1)}, bf16[64,512]{1,0:T(8,128)(2,1)S(1)}, u32[]{:S(2)}, u32[]{:S(2)}) collective-permute-start(bf16[64,512]{1,0:T(8,128)(2,1)} %param.7), channel_id=1, source_target_pairs={{0,48},{16,64},{32,80},{48,96},{64,112},{80,0},{96,16},{112,32},{1... | collective-permute-start | bytes 196616 | tf_op jit(solution)/shard_map/ppermute | solution.py:79
  14.5 8.6 %collective-permute-start.3 = (bf16[64,512]{1,0:T(8,128)(2,1)}, bf16[64,512]{1,0:T(8,128)(2,1)S(1)}, u32[]{:S(2)}, u32[]{:S(2)}) collective-permute-start(bf16[64,512]{1,0:T(8,128)(2,1)} %param.7), channel_id=1, source_target_pairs={{0,64},{16,80},{32,96},{48,112},{64,0},{80,16},{96,32},{112,48},{1... | collective-permute-start | bytes 196616 | tf_op jit(solution)/shard_map/ppermute | solution.py:79
  15.7 7.7 %collective-permute-start.4 = (bf16[64,512]{1,0:T(8,128)(2,1)}, bf16[64,512]{1,0:T(8,128)(2,1)S(1)}, u32[]{:S(2)}, u32[]{:S(2)}) collective-permute-start(bf16[64,512]{1,0:T(8,128)(2,1)} %param.7), channel_id=1, source_target_pairs={{0,80},{16,96},{32,112},{48,0},{64,16},{80,32},{96,48},{112,64},{1... | collective-permute-start | bytes 196616 | tf_op jit(solution)/shard_map/ppermute | solution.py:79
  22.0 4.5 %collective-permute-start.5 = (bf16[64,512]{1,0:T(8,128)(2,1)}, bf16[64,512]{1,0:T(8,128)(2,1)S(1)}, u32[]{:S(2)}, u32[]{:S(2)}) collective-permute-start(bf16[64,512]{1,0:T(8,128)(2,1)} %param.7), channel_id=1, source_target_pairs={{0,96},{16,112},{32,0},{48,16},{64,32},{80,48},{96,64},{112,80},{1... | collective-permute-start | bytes 196616 | tf_op jit(solution)/shard_map/ppermute | solution.py:79
  23.0 6.0 %collective-permute-start.6 = (bf16[64,512]{1,0:T(8,128)(2,1)}, bf16[64,512]{1,0:T(8,128)(2,1)S(1)}, u32[]{:S(2)}, u32[]{:S(2)}) collective-permute-start(bf16[64,512]{1,0:T(8,128)(2,1)} %param.7), channel_id=1, source_target_pairs={{0,112},{16,0},{32,16},{48,32},{64,48},{80,64},{96,80},{112,96},{1... | collective-permute-start | bytes 196616 | tf_op jit(solution)/shard_map/ppermute | solution.py:79
  29.1 0.8 copy-start
  37.8 145.7 %reduce-scatter.3.cloned.1.call-start = ((), (), s32[]{:S(2)}) async-start(), calls=%async_computation.2 | async-start | bytes 7798784 | tf_op jit(solution)/shard_map/reduce_scatter | solution.py:89
  45.8 139.6 %copy-start.1 = (s32[28,4]{0,1:T(4,128)S(1)}, s32[28,4]{0,1:T(4,128)}, u32[]{:S(2)}) copy-start(s32[28,4]{0,1:T(4,128)} %param.13) | copy-start | bytes 1348
  45.8 174.6 %all-gather.2.cloned.1.call-start = ((), (), s32[]{:S(2)}) async-start(), calls=%async_computation.4 | async-start | bytes 3899392 | tf_op jit(solution)/shard_map/all_gather | solution.py:94
  220.4 2.0 copy-start.2
  226.7 11.7 %collective-permute-start.10 = (f32[64,512]{1,0:T(8,128)S(1)}, f32[64,512]{1,0:T(8,128)S(1)}, u32[]{:S(2)}, u32[]{:S(2)}) collective-permute-start(f32[64,512]{1,0:T(8,128)S(1)} %get-tuple-element.9), channel_id=1, source_target_pairs={{0,64},{16,80},{32,96},{48,112},{64,0},{80,16},{96,32},{112,48},{1... | collective-permute-start | bytes 393224 | tf_op jit(solution)/shard_map/ppermute | solution.py:79
  229.9 10.5 %collective-permute-start.11 = (f32[64,512]{1,0:T(8,128)S(1)}, f32[64,512]{1,0:T(8,128)S(1)}, u32[]{:S(2)}, u32[]{:S(2)}) collective-permute-start(f32[64,512]{1,0:T(8,128)S(1)} %get-tuple-element.8), channel_id=1, source_target_pairs={{0,48},{16,64},{32,80},{48,96},{64,112},{80,0},{96,16},{112,32},{1... | collective-permute-start | bytes 393224 | tf_op jit(solution)/shard_map/ppermute | solution.py:79
  232.7 11.9 %collective-permute-start.12 = (f32[64,512]{1,0:T(8,128)S(1)}, f32[64,512]{1,0:T(8,128)S(1)}, u32[]{:S(2)}, u32[]{:S(2)}) collective-permute-start(f32[64,512]{1,0:T(8,128)S(1)} %get-tuple-element.7), channel_id=1, source_target_pairs={{0,32},{16,48},{32,64},{48,80},{64,96},{80,112},{96,0},{112,16},{1... | collective-permute-start | bytes 393224 | tf_op jit(solution)/shard_map/ppermute | solution.py:79
  232.7 11.9 %collective-permute-start.13 = (f32[64,512]{1,0:T(8,128)S(1)}, f32[64,512]{1,0:T(8,128)S(1)}, u32[]{:S(2)}, u32[]{:S(2)}) collective-permute-start(f32[64,512]{1,0:T(8,128)S(1)} %get-tuple-element.6), channel_id=1, source_target_pairs={{0,16},{16,32},{32,48},{48,64},{64,80},{80,96},{96,112},{112,0},{1... | collective-permute-start | bytes 393224 | tf_op jit(solution)/shard_map/ppermute | solution.py:79
  234.8 9.8 %collective-permute-start.7 = (f32[64,512]{1,0:T(8,128)S(1)}, f32[64,512]{1,0:T(8,128)S(1)}, u32[]{:S(2)}, u32[]{:S(2)}) collective-permute-start(f32[64,512]{1,0:T(8,128)S(1)} %get-tuple-element.5), channel_id=1, source_target_pairs={{0,112},{16,0},{32,16},{48,32},{64,48},{80,64},{96,80},{112,96},{1... | collective-permute-start | bytes 393224 | tf_op jit(solution)/shard_map/ppermute | solution.py:79
  238.4 6.3 %collective-permute-start.8 = (f32[64,512]{1,0:T(8,128)S(1)}, f32[64,512]{1,0:T(8,128)S(1)}, u32[]{:S(2)}, u32[]{:S(2)}) collective-permute-start(f32[64,512]{1,0:T(8,128)S(1)} %get-tuple-element.11), channel_id=1, source_target_pairs={{0,96},{16,112},{32,0},{48,16},{64,32},{80,48},{96,64},{112,80},{1... | collective-permute-start | bytes 393224 | tf_op jit(solution)/shard_map/ppermute | solution.py:79
  240.4 7.4 %collective-permute-start.9 = (f32[64,512]{1,0:T(8,128)S(1)}, f32[64,512]{1,0:T(8,128)S(1)}, u32[]{:S(2)}, u32[]{:S(2)}) collective-permute-start(f32[64,512]{1,0:T(8,128)S(1)} %get-tuple-element.10), channel_id=1, source_target_pairs={{0,80},{16,96},{32,112},{48,0},{64,16},{80,32},{96,48},{112,64},{1... | collective-permute-start | bytes 393224 | tf_op jit(solution)/shard_map/ppermute | solution.py:79
Sparse Core Ops, SparseCore 0:
  37.9 71.6 reduce-scatter.4
  112.0 71.4 reduce-scatter.2
  185.5 34.8 all-gather.1

commit v8 on v5

--- a/solution.py
+++ b/solution.py
@@ -76,14 +76,27 @@
     return masked.reshape(rows, cols)
 
 
-def shift(x, k, n):
-    return lax.ppermute(x, ROW, [(i, (i + k) % n) for i in range(n)])
+def permute(x, dest):
+    return lax.ppermute(x, ROW, [(i, dest(i)) for i in range(lax.axis_size(ROW))])
+
+
+def z_shift(x, s, n_hi):
+    n_z = lax.axis_size(ROW) // n_hi
+    return permute(x, lambda i: ((i // n_hi + s) % n_z) * n_hi + i % n_hi)
+
+
+def hi_swap(x):
+    return permute(x, lambda i: i ^ 1)
 
 
 def on_device(tokens, gate_weight, up_weight, down_weight, gate_keep, up_keep, down_keep):
-    n = lax.axis_size(ROW)
+    n_hi = lax.axis_size("x_hi")
+    n_z = lax.axis_size("z")
     hidden_cols = gate_weight.shape[1]
-    features = jnp.concatenate([tokens] + [shift(tokens, k, n) for k in range(1, n)], axis=0)
+    pair_rows = jnp.concatenate([tokens, hi_swap(tokens)], axis=0)
+    features = jnp.concatenate(
+        [pair_rows] + [z_shift(pair_rows, s, n_hi) for s in range(1, n_z)], axis=0
+    )
     pair = gate_up(features, gate_weight, up_weight, gate_keep, up_keep)
     summed = lax.psum_scatter(pair, COL, scatter_dimension=0, tiled=True)
     hidden = (jax.nn.silu(summed[:, :hidden_cols]) * summed[:, hidden_cols:]).astype(jnp.bfloat16)
@@ -91,11 +104,12 @@
     partial_out = jnp.dot(
         hidden_all, expand(down_weight, down_keep), preferred_element_type=jnp.float32
     )
+    t2 = 2 * tokens.shape[0]
+    pair_sum = partial_out[:t2]
+    for s in range(1, n_z):
+        pair_sum = pair_sum + z_shift(partial_out[s * t2:(s + 1) * t2], -s, n_hi)
     t = tokens.shape[0]
-    total = partial_out[:t]
-    for k in range(1, n):
-        total = total + shift(partial_out[k * t:(k + 1) * t], -k, n)
-    return total.astype(jnp.bfloat16)
+    return (pair_sum[:t] + hi_swap(pair_sum[t:])).astype(jnp.bfloat16)
 
 
 def solution(mesh):

time: 204 us -> 204 us (level)
  waiting for transfers between devices: 135 us -> 150 us
  starting transfers between devices: 31.6 us -> 17.3 us
    ppermute x14 -> x8, starting transfers between devices: 31.5 us -> 17.2 us  [permute(): lax.ppermute(x, ROW, [(i, dest(i)) for i in range(lax.axis_size(ROW))])]
    ppermute x14 -> x8, waiting for transfers between devices: 11.1 us -> 23.8 us  [permute(): lax.ppermute(x, ROW, [(i, dest(i)) for i in range(lax.axis_size(ROW))])]
    reduce_scatter x1, waiting for transfers between devices: 87.5 us -> 89.9 us  [on_device(): summed = lax.psum_scatter(pair, COL, scatter_dimension=0, tiled=True)]
  transfers between devices with their start and end apart: 16 -> 10, of which waited for: 7 -> 9; matrix products, arithmetic and copies ran while one was open for 1% -> 0% of each run, Pallas kernels for 0% -> 0%
where the time goes in v8:
time: 204 us
  waiting for transfers between devices  150 us (74%)
  starting transfers between devices  17.3 us (8%)
  between operations  13.5 us (7%)
  Pallas kernels  12.5 us (6%)
  matrix products  4.16 us (2%)
  local copies, waits for them, and re-layouts  3.92 us (2%)
  other arithmetic  2.73 us (1%)
    reduce_scatter x1, waiting for transfers between devices, on_device(): summed = lax.psum_scatter(pair, COL, scatter_dimension=0, tiled=True)  89.9 us
    all_gather x1, waiting for transfers between devices, on_device(): hidden_all = lax.all_gather(hidden, COL, axis=0, tiled=True)  35.9 us
    ppermute x8, waiting for transfers between devices, permute(): lax.ppermute(x, ROW, [(i, dest(i)) for i in range(lax.axis_size(ROW))])  23.8 us
    ppermute x8, starting transfers between devices, permute(): lax.ppermute(x, ROW, [(i, dest(i)) for i in range(lax.axis_size(ROW))])  17.2 us
    pallas_call x1, Pallas kernels, gate_up(): pl.pallas_call(functools.partial(_gate_up_kernel, n_half, n_feat), grid_s...  12.5 us
    dot_general x1, matrix products, on_device(): jnp.dot(hidden_all, expand(down_weight, down_keep), preferred_element_typ...  4.16 us
  transfers between devices with their start and end apart: 10, of which 9 were waited for; matrix products, arithmetic and copies ran while one was open for 0% of the time, Pallas kernels for 0%

profile of v8, /device:TPU:0, one launch (start us, length us, event | category | flops | bytes accessed | tf_op | source)
XLA Modules:
  0.0 203.7 jit_solution(10386732258052937040)
XLA Ops:
  6.5 0.0 reduce-scatter.2.cloned.1.call-start
  6.5 3.1 %collective-permute-start = (bf16[64,512]{1,0:T(8,128)(2,1)}, bf16[64,512]{1,0:T(8,128)(2,1)S(1)}, u32[]{:S(2)}, u32[]{:S(2)}) collective-permute-start(bf16[64,512]{1,0:T(8,128)(2,1)} %param.7), channel_id=1, source_target_pairs={{0,16},{16,0},{32,48},{48,32},{64,80},{80,64},{96,112},{112,96},{1... | collective-permute-start | bytes 196616 | tf_op jit(solution)/shard_map/ppermute | solution.py:80
  9.7 0.9 constant_dynamic-update-slice_fusion.1
  10.6 2.0 collective-permute-done
  12.5 2.1 %collective-permute-start.1 = (bf16[128,512]{1,0:T(8,128)(2,1)S(1)}, bf16[128,512]{1,0:T(8,128)(2,1)S(1)}, u32[]{:S(2)}, u32[]{:S(2)}) collective-permute-start(bf16[128,512]{1,0:T(8,128)(2,1)S(1)} %get-tuple-element.8), channel_id=1, source_target_pairs={{0,32},{16,48},{32,64},{48,80},{64,96},{80,112},{96,0},{112,16},{1... | collective-permute-start | bytes 393224 | tf_op jit(solution)/shard_map/ppermute | solution.py:80
  14.6 3.6 %collective-permute-start.2 = (bf16[128,512]{1,0:T(8,128)(2,1)S(1)}, bf16[128,512]{1,0:T(8,128)(2,1)S(1)}, u32[]{:S(2)}, u32[]{:S(2)}) collective-permute-start(bf16[128,512]{1,0:T(8,128)(2,1)S(1)} %get-tuple-element.8), channel_id=1, source_target_pairs={{0,64},{16,80},{32,96},{48,112},{64,0},{80,16},{96,32},{112,48},{1... | collective-permute-start | bytes 393224 | tf_op jit(solution)/shard_map/ppermute | solution.py:80
  18.2 1.0 collective-permute-start.3
  19.2 1.9 collective-permute-done.1
  21.1 2.0 collective-permute-done.2
  23.1 0.1 collective-permute-done.3
  23.2 0.0 copy-start
  23.2 0.8 copy-done
  24.0 12.5 %shard_map.73 = f32[512,7168]{1,0:T(8,128)} custom-call(s32[4,28]{1,0:T(4,128)} %gk_ref.1, s32[4,28]{1,0:T(4,128)} %uk_ref.1, bf16[512,512]{1,0:T(8,128)(2,1)} %copy-done, bf16[512,3584]{1,0:T(8,128)(2,1)} %gw_ref.1, bf16[512,3584]{1,0:T(8,128)(2,1)} %uw_ref.1), custom_call_target="tpu_custom_call" | custom-call | flops 3758096384 | bytes 22544384 | tf_op jit(solution)/shard_map/pallas_call | solution.py:54
  36.5 0.0 copy-start.1
  36.5 0.0 reduce-scatter.2.cloned.1.call-update
  36.6 0.0 all-gather.2.cloned.1.call-start
  36.6 89.9 %reduce-scatter.2.cloned.1.call-done = f32[32,7168]{1,0:T(8,128)} async-done(((f32[512,7168]{1,0:T(8,128)}), f32[32,7168]{1,0:T(8,128)}) %reduce-scatter.2.cloned.1.call-update) | async-done | bytes 917520 | tf_op jit(solution)/shard_map/reduce_scatter | solution.py:101
  126.5 2.0 fusion.2
  128.5 0.0 all-gather.2.cloned.1.call-update
  128.5 0.0 copy-done.1
  128.5 0.1 copy.8
  128.6 35.9 %all-gather.2.cloned.1.call-done = bf16[512,3584]{1,0:T(8,128)(2,1)} async-done(((bf16[32,3584]{1,0:T(8,128)(2,1)}), bf16[512,3584]{1,0:T(8,128)(2,1)}) %all-gather.2.cloned.1.call-update) | async-done | bytes 3670032 | tf_op jit(solution)/shard_map/all_gather | solution.py:103
  164.5 0.0 copy-start.2
  164.5 1.0 mul.20
  165.6 1.0 copy-done.2
  166.6 4.2 %fusion = f32[512,512]{1,0:T(8,128)S(1)} fusion(bf16[512,3584]{1,0:T(8,128)(2,1)} %all-gather.2.cloned.1.call-done, bf16[3584,512]{1,0:T(8,128)(2,1)S(1)} %copy-done.2, bf16[448,8,4,128]{3,2,1,0:T(4,128)(2,1)S(1)} %bitcast.6), kind=kOutput, calls=%fused_computation.1 | convolution fusion | flops 1880883200 | bytes 12058624 | tf_op jit(solution)/shard_map/dot_general | solution.py:104
  170.7 0.1 fusion.6
  170.8 3.0 %collective-permute-start.4 = (f32[128,512]{1,0:T(8,128)S(1)}, f32[128,512]{1,0:T(8,128)S(1)}, u32[]{:S(2)}, u32[]{:S(2)}) collective-permute-start(f32[128,512]{1,0:T(8,128)S(1)} %get-tuple-element.5), channel_id=1, source_target_pairs={{0,96},{16,112},{32,0},{48,16},{64,32},{80,48},{96,64},{112,80},{1... | collective-permute-start | bytes 786440 | tf_op jit(solution)/shard_map/ppermute | solution.py:80
  173.8 0.7 collective-permute-start.5
  174.5 1.0 collective-permute-start.6
  175.4 9.9 %collective-permute-done.4 = f32[128,512]{1,0:T(8,128)S(1)} collective-permute-done((f32[128,512]{1,0:T(8,128)S(1)}, f32[128,512]{1,0:T(8,128)S(1)}, u32[]{:S(2)}, u32[]{:S(2)}) %collective-permute-start.4) | collective-permute-done | bytes 262176 | tf_op jit(solution)/shard_map/ppermute | solution.py:80
  185.4 0.0 collective-permute-done.5
  185.4 3.7 %collective-permute-done.6 = f32[128,512]{1,0:T(8,128)S(1)} collective-permute-done((f32[128,512]{1,0:T(8,128)S(1)}, f32[128,512]{1,0:T(8,128)S(1)}, u32[]{:S(2)}, u32[]{:S(2)}) %collective-permute-start.6) | collective-permute-done | bytes 262176 | tf_op jit(solution)/shard_map/ppermute | solution.py:80
  189.1 0.1 fusion.4
  189.2 2.8 %collective-permute-start.7 = (f32[64,512]{1,0:T(8,128)S(1)}, f32[64,512]{1,0:T(8,128)S(1)}, u32[]{:S(2)}, u32[]{:S(2)}) collective-permute-start(f32[64,512]{1,0:T(8,128)S(1)} %slice.39), channel_id=1, source_target_pairs={{0,16},{16,0},{32,48},{48,32},{64,80},{80,64},{96,112},{112,96},{1... | collective-permute-start | bytes 393224 | tf_op jit(solution)/shard_map/ppermute | solution.py:80
  192.0 4.2 %collective-permute-done.7 = f32[64,512]{1,0:T(8,128)S(1)} collective-permute-done((f32[64,512]{1,0:T(8,128)S(1)}, f32[64,512]{1,0:T(8,128)S(1)}, u32[]{:S(2)}, u32[]{:S(2)}) %collective-permute-start.7) | collective-permute-done | bytes 131104 | tf_op jit(solution)/shard_map/ppermute | solution.py:80
  196.2 0.6 fusion.5
  (6 shorter events, 0.1 us)
Async XLA Ops:
  6.5 120.0 %reduce-scatter.2.cloned.1.call-start = ((), (), s32[]{:S(2)}) async-start(), calls=%async_computation.1 | async-start | bytes 15597568 | tf_op jit(solution)/shard_map/reduce_scatter | solution.py:101
  6.5 6.0 %collective-permute-start = (bf16[64,512]{1,0:T(8,128)(2,1)}, bf16[64,512]{1,0:T(8,128)(2,1)S(1)}, u32[]{:S(2)}, u32[]{:S(2)}) collective-permute-start(bf16[64,512]{1,0:T(8,128)(2,1)} %param.7), channel_id=1, source_target_pairs={{0,16},{16,0},{32,48},{48,32},{64,80},{80,64},{96,112},{112,96},{1... | collective-permute-start | bytes 196616 | tf_op jit(solution)/shard_map/ppermute | solution.py:80
  12.5 8.6 %collective-permute-start.1 = (bf16[128,512]{1,0:T(8,128)(2,1)S(1)}, bf16[128,512]{1,0:T(8,128)(2,1)S(1)}, u32[]{:S(2)}, u32[]{:S(2)}) collective-permute-start(bf16[128,512]{1,0:T(8,128)(2,1)S(1)} %get-tuple-element.8), channel_id=1, source_target_pairs={{0,32},{16,48},{32,64},{48,80},{64,96},{80,112},{96,0},{112,16},{1... | collective-permute-start | bytes 393224 | tf_op jit(solution)/shard_map/ppermute | solution.py:80
  14.6 8.5 %collective-permute-start.2 = (bf16[128,512]{1,0:T(8,128)(2,1)S(1)}, bf16[128,512]{1,0:T(8,128)(2,1)S(1)}, u32[]{:S(2)}, u32[]{:S(2)}) collective-permute-start(bf16[128,512]{1,0:T(8,128)(2,1)S(1)} %get-tuple-element.8), channel_id=1, source_target_pairs={{0,64},{16,80},{32,96},{48,112},{64,0},{80,16},{96,32},{112,48},{1... | collective-permute-start | bytes 393224 | tf_op jit(solution)/shard_map/ppermute | solution.py:80
  18.2 5.0 %collective-permute-start.3 = (bf16[128,512]{1,0:T(8,128)(2,1)S(1)}, bf16[128,512]{1,0:T(8,128)(2,1)S(1)}, u32[]{:S(2)}, u32[]{:S(2)}) collective-permute-start(bf16[128,512]{1,0:T(8,128)(2,1)S(1)} %get-tuple-element.8), channel_id=1, source_target_pairs={{0,96},{16,112},{32,0},{48,16},{64,32},{80,48},{96,64},{112,80},{1... | collective-permute-start | bytes 393224 | tf_op jit(solution)/shard_map/ppermute | solution.py:80
  23.2 0.8 copy-start
  36.5 92.0 %copy-start.1 = (s32[28,4]{0,1:T(4,128)S(1)}, s32[28,4]{0,1:T(4,128)}, u32[]{:S(2)}) copy-start(s32[28,4]{0,1:T(4,128)} %param.13) | copy-start | bytes 1348
  36.6 128.0 %all-gather.2.cloned.1.call-start = ((), (), s32[]{:S(2)}) async-start(), calls=%async_computation.2 | async-start | bytes 3899392 | tf_op jit(solution)/shard_map/all_gather | solution.py:103
  164.5 2.0 %copy-start.2 = (bf16[3584,512]{1,0:T(8,128)(2,1)S(1)}, bf16[3584,512]{1,0:T(8,128)(2,1)}, u32[]{:S(2)}) copy-start(bf16[3584,512]{1,0:T(8,128)(2,1)} %param.10) | copy-start | bytes 11010052
  170.8 14.6 %collective-permute-start.4 = (f32[128,512]{1,0:T(8,128)S(1)}, f32[128,512]{1,0:T(8,128)S(1)}, u32[]{:S(2)}, u32[]{:S(2)}) collective-permute-start(f32[128,512]{1,0:T(8,128)S(1)} %get-tuple-element.5), channel_id=1, source_target_pairs={{0,96},{16,112},{32,0},{48,16},{64,32},{80,48},{96,64},{112,80},{1... | collective-permute-start | bytes 786440 | tf_op jit(solution)/shard_map/ppermute | solution.py:80
  173.8 11.6 %collective-permute-start.5 = (f32[128,512]{1,0:T(8,128)S(1)}, f32[128,512]{1,0:T(8,128)S(1)}, u32[]{:S(2)}, u32[]{:S(2)}) collective-permute-start(f32[128,512]{1,0:T(8,128)S(1)} %get-tuple-element.7), channel_id=1, source_target_pairs={{0,64},{16,80},{32,96},{48,112},{64,0},{80,16},{96,32},{112,48},{1... | collective-permute-start | bytes 786440 | tf_op jit(solution)/shard_map/ppermute | solution.py:80
  174.5 14.6 %collective-permute-start.6 = (f32[128,512]{1,0:T(8,128)S(1)}, f32[128,512]{1,0:T(8,128)S(1)}, u32[]{:S(2)}, u32[]{:S(2)}) collective-permute-start(f32[128,512]{1,0:T(8,128)S(1)} %get-tuple-element.6), channel_id=1, source_target_pairs={{0,32},{16,48},{32,64},{48,80},{64,96},{80,112},{96,0},{112,16},{1... | collective-permute-start | bytes 786440 | tf_op jit(solution)/shard_map/ppermute | solution.py:80
  189.2 7.0 %collective-permute-start.7 = (f32[64,512]{1,0:T(8,128)S(1)}, f32[64,512]{1,0:T(8,128)S(1)}, u32[]{:S(2)}, u32[]{:S(2)}) collective-permute-start(f32[64,512]{1,0:T(8,128)S(1)} %slice.39), channel_id=1, source_target_pairs={{0,16},{16,0},{32,48},{48,32},{64,80},{80,64},{96,112},{112,96},{1... | collective-permute-start | bytes 393224 | tf_op jit(solution)/shard_map/ppermute | solution.py:80
Sparse Core Ops, SparseCore 0:
  36.7 89.7 reduce-scatter.1
  128.6 35.8 all-gather.1

commit v9 on v8

--- a/solution.py
+++ b/solution.py
@@ -104,12 +104,18 @@
     partial_out = jnp.dot(
         hidden_all, expand(down_weight, down_keep), preferred_element_type=jnp.float32
     )
-    t2 = 2 * tokens.shape[0]
-    pair_sum = partial_out[:t2]
-    for s in range(1, n_z):
-        pair_sum = pair_sum + z_shift(partial_out[s * t2:(s + 1) * t2], -s, n_hi)
     t = tokens.shape[0]
-    return (pair_sum[:t] + hi_swap(pair_sum[t:])).astype(jnp.bfloat16)
+    total = partial_out[:t]
+    for s in range(n_z):
+        for i in range(n_hi):
+            if s == 0 and i == 0:
+                continue
+            b = s * n_hi + i
+            total = total + permute(
+                partial_out[b * t:(b + 1) * t],
+                lambda L, s=s, i=i: ((L // n_hi - s) % n_z) * n_hi + ((L % n_hi) ^ i),
+            )
+    return total.astype(jnp.bfloat16)
 
 
 def solution(mesh):

time: 204 us -> 202 us (level)
  waiting for transfers between devices: 150 us -> 139 us
  starting transfers between devices: 17.3 us -> 24.6 us
    ppermute x8 -> x11, waiting for transfers between devices: 23.8 us -> 13.7 us  [permute(): lax.ppermute(x, ROW, [(i, dest(i)) for i in range(lax.axis_size(ROW))])]
    ppermute x8 -> x11, starting transfers between devices: 17.2 us -> 24.6 us  [permute(): lax.ppermute(x, ROW, [(i, dest(i)) for i in range(lax.axis_size(ROW))])]
  transfers between devices with their start and end apart: 10 -> 13, of which waited for: 9 -> 9; matrix products, arithmetic and copies ran while one was open for 0% -> 1% of each run, Pallas kernels for 0% -> 0%
where the time goes in v9:
time: 202 us; the launch traced here: 201 us
  waiting for transfers between devices  139 us (69%)
  starting transfers between devices  24.6 us (12%)
  between operations  13.5 us (7%)
  Pallas kernels  12.3 us (6%)
  matrix products  4.16 us (2%)
  local copies, waits for them, and re-layouts  3.93 us (2%)
  other arithmetic  2.69 us (1%)
    reduce_scatter x1, waiting for transfers between devices, on_device(): summed = lax.psum_scatter(pair, COL, scatter_dimension=0, tiled=True)  89.9 us
    all_gather x1, waiting for transfers between devices, on_device(): hidden_all = lax.all_gather(hidden, COL, axis=0, tiled=True)  35.9 us
    ppermute x11, starting transfers between devices, permute(): lax.ppermute(x, ROW, [(i, dest(i)) for i in range(lax.axis_size(ROW))])  24.6 us
    ppermute x11, waiting for transfers between devices, permute(): lax.ppermute(x, ROW, [(i, dest(i)) for i in range(lax.axis_size(ROW))])  13.7 us
    pallas_call x1, Pallas kernels, gate_up(): pl.pallas_call(functools.partial(_gate_up_kernel, n_half, n_feat), grid_s...  12.3 us
    dot_general x1, matrix products, on_device(): jnp.dot(hidden_all, expand(down_weight, down_keep), preferred_element_typ...  4.16 us
  transfers between devices with their start and end apart: 13, of which 9 were waited for; matrix products, arithmetic and copies ran while one was open for 1% of the time, Pallas kernels for 0%

profile of v9, /device:TPU:0, one launch (start us, length us, event | category | flops | bytes accessed | tf_op | source)
XLA Modules:
  0.0 200.7 jit_solution(15048467248838312873)
XLA Ops:
  6.5 0.0 reduce-scatter.2.cloned.1.call-start
  6.5 3.1 %collective-permute-start = (bf16[64,512]{1,0:T(8,128)(2,1)}, bf16[64,512]{1,0:T(8,128)(2,1)S(1)}, u32[]{:S(2)}, u32[]{:S(2)}) collective-permute-start(bf16[64,512]{1,0:T(8,128)(2,1)} %param.7), channel_id=1, source_target_pairs={{0,16},{16,0},{32,48},{48,32},{64,80},{80,64},{96,112},{112,96},{1... | collective-permute-start | bytes 196616 | tf_op jit(solution)/shard_map/ppermute | solution.py:80
  9.7 0.9 constant_dynamic-update-slice_fusion.1
  10.6 2.0 collective-permute-done
  12.5 2.1 %collective-permute-start.1 = (bf16[128,512]{1,0:T(8,128)(2,1)S(1)}, bf16[128,512]{1,0:T(8,128)(2,1)S(1)}, u32[]{:S(2)}, u32[]{:S(2)}) collective-permute-start(bf16[128,512]{1,0:T(8,128)(2,1)S(1)} %get-tuple-element.12), channel_id=1, source_target_pairs={{0,32},{16,48},{32,64},{48,80},{64,96},{80,112},{96,0},{112,16},{1... | collective-permute-start | bytes 393224 | tf_op jit(solution)/shard_map/ppermute | solution.py:80
  14.6 3.6 %collective-permute-start.2 = (bf16[128,512]{1,0:T(8,128)(2,1)S(1)}, bf16[128,512]{1,0:T(8,128)(2,1)S(1)}, u32[]{:S(2)}, u32[]{:S(2)}) collective-permute-start(bf16[128,512]{1,0:T(8,128)(2,1)S(1)} %get-tuple-element.12), channel_id=1, source_target_pairs={{0,64},{16,80},{32,96},{48,112},{64,0},{80,16},{96,32},{112,48},{1... | collective-permute-start | bytes 393224 | tf_op jit(solution)/shard_map/ppermute | solution.py:80
  18.2 1.0 collective-permute-start.3
  19.2 1.9 collective-permute-done.1
  21.1 2.0 collective-permute-done.2
  23.1 0.1 collective-permute-done.3
  23.2 0.0 copy-start
  23.2 0.8 copy-done
  24.0 12.3 %shard_map.73 = f32[512,7168]{1,0:T(8,128)} custom-call(s32[4,28]{1,0:T(4,128)} %gk_ref.1, s32[4,28]{1,0:T(4,128)} %uk_ref.1, bf16[512,512]{1,0:T(8,128)(2,1)} %copy-done, bf16[512,3584]{1,0:T(8,128)(2,1)} %gw_ref.1, bf16[512,3584]{1,0:T(8,128)(2,1)} %uw_ref.1), custom_call_target="tpu_custom_call" | custom-call | flops 3758096384 | bytes 22544384 | tf_op jit(solution)/shard_map/pallas_call | solution.py:54
  36.3 0.0 copy-start.1
  36.3 0.0 reduce-scatter.2.cloned.1.call-update
  36.3 0.0 all-gather.2.cloned.1.call-start
  36.4 89.9 %reduce-scatter.2.cloned.1.call-done = f32[32,7168]{1,0:T(8,128)} async-done(((f32[512,7168]{1,0:T(8,128)}), f32[32,7168]{1,0:T(8,128)}) %reduce-scatter.2.cloned.1.call-update) | async-done | bytes 917520 | tf_op jit(solution)/shard_map/reduce_scatter | solution.py:101
  126.3 2.0 fusion.2
  128.2 0.0 all-gather.2.cloned.1.call-update
  128.3 0.0 copy-done.1
  128.3 0.1 copy.8
  128.4 35.9 %all-gather.2.cloned.1.call-done = bf16[512,3584]{1,0:T(8,128)(2,1)} async-done(((bf16[32,3584]{1,0:T(8,128)(2,1)}), bf16[512,3584]{1,0:T(8,128)(2,1)}) %all-gather.2.cloned.1.call-update) | async-done | bytes 3670032 | tf_op jit(solution)/shard_map/all_gather | solution.py:103
  164.3 0.0 copy-start.2
  164.3 1.0 mul.20
  165.3 1.0 copy-done.2
  166.3 4.2 %fusion = f32[512,512]{1,0:T(8,128)S(1)} fusion(bf16[512,3584]{1,0:T(8,128)(2,1)} %all-gather.2.cloned.1.call-done, bf16[3584,512]{1,0:T(8,128)(2,1)S(1)} %copy-done.2, bf16[448,8,4,128]{3,2,1,0:T(4,128)(2,1)S(1)} %bitcast.6), kind=kOutput, calls=%fused_computation.1 | convolution fusion | flops 1880883200 | bytes 12058624 | tf_op jit(solution)/shard_map/dot_general | solution.py:104
  170.5 0.1 fusion.10
  170.6 3.8 %collective-permute-start.10 = (f32[64,512]{1,0:T(8,128)S(1)}, f32[64,512]{1,0:T(8,128)S(1)}, u32[]{:S(2)}, u32[]{:S(2)}) collective-permute-start(f32[64,512]{1,0:T(8,128)S(1)} %get-tuple-element.6), channel_id=1, source_target_pairs={{0,48},{16,32},{32,80},{48,64},{64,112},{80,96},{96,16},{112,0},{1... | collective-permute-start | bytes 393224 | tf_op jit(solution)/shard_map/ppermute | solution.py:80
  174.3 0.8 collective-permute-start.4
  175.2 1.7 collective-permute-start.5
  176.8 3.9 %collective-permute-start.6 = (f32[64,512]{1,0:T(8,128)S(1)}, f32[64,512]{1,0:T(8,128)S(1)}, u32[]{:S(2)}, u32[]{:S(2)}) collective-permute-start(f32[64,512]{1,0:T(8,128)S(1)} %get-tuple-element.10), channel_id=1, source_target_pairs={{0,112},{16,96},{32,16},{48,0},{64,48},{80,32},{96,80},{112,64},{1... | collective-permute-start | bytes 393224 | tf_op jit(solution)/shard_map/ppermute | solution.py:80
  180.7 0.7 collective-permute-start.7
  181.4 0.0 collective-permute-done.10
  181.4 3.3 %collective-permute-start.8 = (f32[64,512]{1,0:T(8,128)S(1)}, f32[64,512]{1,0:T(8,128)S(1)}, u32[]{:S(2)}, u32[]{:S(2)}) collective-permute-start(f32[64,512]{1,0:T(8,128)S(1)} %get-tuple-element.8), channel_id=1, source_target_pairs={{0,80},{16,64},{32,112},{48,96},{64,16},{80,0},{96,48},{112,32},{1... | collective-permute-start | bytes 393224 | tf_op jit(solution)/shard_map/ppermute | solution.py:80
  184.7 0.0 collective-permute-done.4
  184.7 0.7 collective-permute-start.9
  185.3 0.0 collective-permute-done.5
  185.4 0.1 collective-permute-done.6
  185.5 5.6 %collective-permute-done.7 = f32[64,512]{1,0:T(8,128)S(1)} collective-permute-done((f32[64,512]{1,0:T(8,128)S(1)}, f32[64,512]{1,0:T(8,128)S(1)}, u32[]{:S(2)}, u32[]{:S(2)}) %collective-permute-start.7) | collective-permute-done | bytes 131104 | tf_op jit(solution)/shard_map/ppermute | solution.py:80
  191.0 0.0 collective-permute-done.8
  191.0 2.1 %collective-permute-done.9 = f32[64,512]{1,0:T(8,128)S(1)} collective-permute-done((f32[64,512]{1,0:T(8,128)S(1)}, f32[64,512]{1,0:T(8,128)S(1)}, u32[]{:S(2)}, u32[]{:S(2)}) %collective-permute-start.9) | collective-permute-done | bytes 131104 | tf_op jit(solution)/shard_map/ppermute | solution.py:80
  193.1 0.7 fusion.9
  (5 shorter events, 0.0 us)
Async XLA Ops:
  6.5 119.7 %reduce-scatter.2.cloned.1.call-start = ((), (), s32[]{:S(2)}) async-start(), calls=%async_computation.1 | async-start | bytes 15597568 | tf_op jit(solution)/shard_map/reduce_scatter | solution.py:101
  6.5 6.0 %collective-permute-start = (bf16[64,512]{1,0:T(8,128)(2,1)}, bf16[64,512]{1,0:T(8,128)(2,1)S(1)}, u32[]{:S(2)}, u32[]{:S(2)}) collective-permute-start(bf16[64,512]{1,0:T(8,128)(2,1)} %param.7), channel_id=1, source_target_pairs={{0,16},{16,0},{32,48},{48,32},{64,80},{80,64},{96,112},{112,96},{1... | collective-permute-start | bytes 196616 | tf_op jit(solution)/shard_map/ppermute | solution.py:80
  12.5 8.6 %collective-permute-start.1 = (bf16[128,512]{1,0:T(8,128)(2,1)S(1)}, bf16[128,512]{1,0:T(8,128)(2,1)S(1)}, u32[]{:S(2)}, u32[]{:S(2)}) collective-permute-start(bf16[128,512]{1,0:T(8,128)(2,1)S(1)} %get-tuple-element.12), channel_id=1, source_target_pairs={{0,32},{16,48},{32,64},{48,80},{64,96},{80,112},{96,0},{112,16},{1... | collective-permute-start | bytes 393224 | tf_op jit(solution)/shard_map/ppermute | solution.py:80
  14.6 8.5 %collective-permute-start.2 = (bf16[128,512]{1,0:T(8,128)(2,1)S(1)}, bf16[128,512]{1,0:T(8,128)(2,1)S(1)}, u32[]{:S(2)}, u32[]{:S(2)}) collective-permute-start(bf16[128,512]{1,0:T(8,128)(2,1)S(1)} %get-tuple-element.12), channel_id=1, source_target_pairs={{0,64},{16,80},{32,96},{48,112},{64,0},{80,16},{96,32},{112,48},{1... | collective-permute-start | bytes 393224 | tf_op jit(solution)/shard_map/ppermute | solution.py:80
  18.2 5.0 %collective-permute-start.3 = (bf16[128,512]{1,0:T(8,128)(2,1)S(1)}, bf16[128,512]{1,0:T(8,128)(2,1)S(1)}, u32[]{:S(2)}, u32[]{:S(2)}) collective-permute-start(bf16[128,512]{1,0:T(8,128)(2,1)S(1)} %get-tuple-element.12), channel_id=1, source_target_pairs={{0,96},{16,112},{32,0},{48,16},{64,32},{80,48},{96,64},{112,80},{1... | collective-permute-start | bytes 393224 | tf_op jit(solution)/shard_map/ppermute | solution.py:80
  23.2 0.8 copy-start
  36.3 92.0 %copy-start.1 = (s32[28,4]{0,1:T(4,128)S(1)}, s32[28,4]{0,1:T(4,128)}, u32[]{:S(2)}) copy-start(s32[28,4]{0,1:T(4,128)} %param.13) | copy-start | bytes 1348
  36.3 128.0 %all-gather.2.cloned.1.call-start = ((), (), s32[]{:S(2)}) async-start(), calls=%async_computation.2 | async-start | bytes 3899392 | tf_op jit(solution)/shard_map/all_gather | solution.py:103
  164.3 2.0 %copy-start.2 = (bf16[3584,512]{1,0:T(8,128)(2,1)S(1)}, bf16[3584,512]{1,0:T(8,128)(2,1)}, u32[]{:S(2)}) copy-start(bf16[3584,512]{1,0:T(8,128)(2,1)} %param.10) | copy-start | bytes 11010052
  170.6 10.8 %collective-permute-start.10 = (f32[64,512]{1,0:T(8,128)S(1)}, f32[64,512]{1,0:T(8,128)S(1)}, u32[]{:S(2)}, u32[]{:S(2)}) collective-permute-start(f32[64,512]{1,0:T(8,128)S(1)} %get-tuple-element.6), channel_id=1, source_target_pairs={{0,48},{16,32},{32,80},{48,64},{64,112},{80,96},{96,16},{112,0},{1... | collective-permute-start | bytes 393224 | tf_op jit(solution)/shard_map/ppermute | solution.py:80
  174.3 10.4 %collective-permute-start.4 = (f32[64,512]{1,0:T(8,128)S(1)}, f32[64,512]{1,0:T(8,128)S(1)}, u32[]{:S(2)}, u32[]{:S(2)}) collective-permute-start(f32[64,512]{1,0:T(8,128)S(1)} %get-tuple-element.5), channel_id=1, source_target_pairs={{0,16},{16,0},{32,48},{48,32},{64,80},{80,64},{96,112},{112,96},{1... | collective-permute-start | bytes 393224 | tf_op jit(solution)/shard_map/ppermute | solution.py:80
  175.2 10.2 %collective-permute-start.5 = (f32[64,512]{1,0:T(8,128)S(1)}, f32[64,512]{1,0:T(8,128)S(1)}, u32[]{:S(2)}, u32[]{:S(2)}) collective-permute-start(f32[64,512]{1,0:T(8,128)S(1)} %get-tuple-element.11), channel_id=1, source_target_pairs={{0,96},{16,112},{32,0},{48,16},{64,32},{80,48},{96,64},{112,80},{1... | collective-permute-start | bytes 393224 | tf_op jit(solution)/shard_map/ppermute | solution.py:80
  176.8 8.6 %collective-permute-start.6 = (f32[64,512]{1,0:T(8,128)S(1)}, f32[64,512]{1,0:T(8,128)S(1)}, u32[]{:S(2)}, u32[]{:S(2)}) collective-permute-start(f32[64,512]{1,0:T(8,128)S(1)} %get-tuple-element.10), channel_id=1, source_target_pairs={{0,112},{16,96},{32,16},{48,0},{64,48},{80,32},{96,80},{112,64},{1... | collective-permute-start | bytes 393224 | tf_op jit(solution)/shard_map/ppermute | solution.py:80
  180.7 10.3 %collective-permute-start.7 = (f32[64,512]{1,0:T(8,128)S(1)}, f32[64,512]{1,0:T(8,128)S(1)}, u32[]{:S(2)}, u32[]{:S(2)}) collective-permute-start(f32[64,512]{1,0:T(8,128)S(1)} %get-tuple-element.9), channel_id=1, source_target_pairs={{0,64},{16,80},{32,96},{48,112},{64,0},{80,16},{96,32},{112,48},{1... | collective-permute-start | bytes 393224 | tf_op jit(solution)/shard_map/ppermute | solution.py:80
  181.4 9.6 %collective-permute-start.8 = (f32[64,512]{1,0:T(8,128)S(1)}, f32[64,512]{1,0:T(8,128)S(1)}, u32[]{:S(2)}, u32[]{:S(2)}) collective-permute-start(f32[64,512]{1,0:T(8,128)S(1)} %get-tuple-element.8), channel_id=1, source_target_pairs={{0,80},{16,64},{32,112},{48,96},{64,16},{80,0},{96,48},{112,32},{1... | collective-permute-start | bytes 393224 | tf_op jit(solution)/shard_map/ppermute | solution.py:80
  184.7 8.4 %collective-permute-start.9 = (f32[64,512]{1,0:T(8,128)S(1)}, f32[64,512]{1,0:T(8,128)S(1)}, u32[]{:S(2)}, u32[]{:S(2)}) collective-permute-start(f32[64,512]{1,0:T(8,128)S(1)} %get-tuple-element.7), channel_id=1, source_target_pairs={{0,32},{16,48},{32,64},{48,80},{64,96},{80,112},{96,0},{112,16},{1... | collective-permute-start | bytes 393224 | tf_op jit(solution)/shard_map/ppermute | solution.py:80
Sparse Core Ops, SparseCore 0:
  36.4 89.7 reduce-scatter.1
  128.4 35.8 all-gather.1

commit v10 on v9

--- a/solution.py
+++ b/solution.py
@@ -99,10 +99,12 @@
     )
     pair = gate_up(features, gate_weight, up_weight, gate_keep, up_keep)
     summed = lax.psum_scatter(pair, COL, scatter_dimension=0, tiled=True)
+    down_mat = expand(down_weight, down_keep)
+    summed, down_mat = lax.optimization_barrier((summed, down_mat))
     hidden = (jax.nn.silu(summed[:, :hidden_cols]) * summed[:, hidden_cols:]).astype(jnp.bfloat16)
     hidden_all = lax.all_gather(hidden, COL, axis=0, tiled=True)
     partial_out = jnp.dot(
-        hidden_all, expand(down_weight, down_keep), preferred_element_type=jnp.float32
+        hidden_all, down_mat, preferred_element_type=jnp.float32
     )
     t = tokens.shape[0]
     total = partial_out[:t]

time: 202 us -> 201 us (level)
  waiting for transfers between devices: 139 us -> 135 us
  other arithmetic: 2.69 us -> 4.97 us
    reduce_scatter x1, waiting for transfers between devices: 89.9 us -> 85 us  [on_device(): summed = lax.psum_scatter(pair, COL, scatter_dimension=0, tiled=True)]
    mul x0 -> x1, other arithmetic: none -> 2.29 us  [expand(): weight.reshape(nrow, rows // nrow, ncol, cols // ncol)]
  transfers between devices with their start and end apart: 13 -> 13, of which waited for: 9 -> 9; matrix products, arithmetic and copies ran while one was open for 1% -> 2% of each run, Pallas kernels for 0% -> 0%
where the time goes in v10:
time: 201 us; the launch traced here: 200 us
  waiting for transfers between devices  135 us (67%)
  starting transfers between devices  24.6 us (12%)
  between operations  13.5 us (7%)
  Pallas kernels  12.3 us (6%)
  matrix products  5.21 us (3%)
  other arithmetic  4.97 us (2%)
  local copies, waits for them, and re-layouts  4.53 us (2%)
    reduce_scatter x1, waiting for transfers between devices, on_device(): summed = lax.psum_scatter(pair, COL, scatter_dimension=0, tiled=True)  85 us
    all_gather x1, waiting for transfers between devices, on_device(): hidden_all = lax.all_gather(hidden, COL, axis=0, tiled=True)  35.9 us
    ppermute x11, starting transfers between devices, permute(): lax.ppermute(x, ROW, [(i, dest(i)) for i in range(lax.axis_size(ROW))])  24.6 us
    ppermute x11, waiting for transfers between devices, permute(): lax.ppermute(x, ROW, [(i, dest(i)) for i in range(lax.axis_size(ROW))])  13.7 us
    pallas_call x1, Pallas kernels, gate_up(): pl.pallas_call(functools.partial(_gate_up_kernel, n_half, n_feat), grid_s...  12.3 us
    dot_general x1, matrix products, on_device(): jnp.dot(hidden_all, down_mat, preferred_element_type=jnp.float32)  5.21 us
  transfers between devices with their start and end apart: 13, of which 9 were waited for; matrix products, arithmetic and copies ran while one was open for 2% of the time, Pallas kernels for 0%

profile of v10, /device:TPU:0, one launch (start us, length us, event | category | flops | bytes accessed | tf_op | source)
XLA Modules:
  0.0 199.7 jit_solution(10628371060121446688)
XLA Ops:
  6.5 0.0 reduce-scatter.2.cloned.1.call-start
  6.5 3.1 %collective-permute-start = (bf16[64,512]{1,0:T(8,128)(2,1)}, bf16[64,512]{1,0:T(8,128)(2,1)S(1)}, u32[]{:S(2)}, u32[]{:S(2)}) collective-permute-start(bf16[64,512]{1,0:T(8,128)(2,1)} %param.7), channel_id=1, source_target_pairs={{0,16},{16,0},{32,48},{48,32},{64,80},{80,64},{96,112},{112,96},{1... | collective-permute-start | bytes 196616 | tf_op jit(solution)/shard_map/ppermute | solution.py:80
  9.7 0.9 constant_dynamic-update-slice_fusion.1
  10.6 2.0 collective-permute-done
  12.5 2.1 %collective-permute-start.1 = (bf16[128,512]{1,0:T(8,128)(2,1)S(1)}, bf16[128,512]{1,0:T(8,128)(2,1)S(1)}, u32[]{:S(2)}, u32[]{:S(2)}) collective-permute-start(bf16[128,512]{1,0:T(8,128)(2,1)S(1)} %get-tuple-element.16), channel_id=1, source_target_pairs={{0,32},{16,48},{32,64},{48,80},{64,96},{80,112},{96,0},{112,16},{1... | collective-permute-start | bytes 393224 | tf_op jit(solution)/shard_map/ppermute | solution.py:80
  14.6 3.6 %collective-permute-start.2 = (bf16[128,512]{1,0:T(8,128)(2,1)S(1)}, bf16[128,512]{1,0:T(8,128)(2,1)S(1)}, u32[]{:S(2)}, u32[]{:S(2)}) collective-permute-start(bf16[128,512]{1,0:T(8,128)(2,1)S(1)} %get-tuple-element.16), channel_id=1, source_target_pairs={{0,64},{16,80},{32,96},{48,112},{64,0},{80,16},{96,32},{112,48},{1... | collective-permute-start | bytes 393224 | tf_op jit(solution)/shard_map/ppermute | solution.py:80
  18.2 1.0 collective-permute-start.3
  19.2 1.9 collective-permute-done.1
  21.1 2.0 collective-permute-done.2
  23.1 0.1 collective-permute-done.3
  23.2 0.0 copy-start.1
  23.2 0.8 copy-done.1
  24.0 12.3 %shard_map.73 = f32[512,7168]{1,0:T(8,128)} custom-call(s32[4,28]{1,0:T(4,128)} %gk_ref.1, s32[4,28]{1,0:T(4,128)} %uk_ref.1, bf16[512,512]{1,0:T(8,128)(2,1)} %copy-done.1, bf16[512,3584]{1,0:T(8,128)(2,1)} %gw_ref.1, bf16[512,3584]{1,0:T(8,128)(2,1)} %uw_ref.1), custom_call_target="tpu_custom_call" | custom-call | flops 3758096384 | bytes 22544384 | tf_op jit(solution)/shard_map/pallas_call | solution.py:54
  36.3 0.0 copy-start.2
  36.3 0.0 reduce-scatter.2.cloned.1.call-update
  36.3 0.0 all-gather.2.cloned.1.call-start
  36.4 0.6 copy-done.2
  37.0 0.1 copy.8
  37.1 0.0 copy-start
  37.1 1.0 mul.18
  38.1 1.0 copy-done
  39.1 2.3 %bitcast_multiply_fusion = bf16[3584,512]{1,0:T(8,128)(2,1)} fusion(bf16[3584,512]{1,0:T(8,128)(2,1)S(1)} %copy-done, bf16[448,8,4,128]{3,2,1,0:T(4,128)(2,1)S(1)} %bitcast.6), kind=kLoop, calls=%fused_computation | loop fusion | flops 1835008 | bytes 11010048 | tf_op jit(solution)/shard_map/mul | solution.py:73
  41.4 85.0 %reduce-scatter.2.cloned.1.call-done = f32[32,7168]{1,0:T(8,128)} async-done(((f32[512,7168]{1,0:T(8,128)}), f32[32,7168]{1,0:T(8,128)}) %reduce-scatter.2.cloned.1.call-update) | async-done | bytes 917520 | tf_op jit(solution)/shard_map/reduce_scatter | solution.py:101
  126.4 2.0 multiply_convert_fusion
  128.4 0.0 all-gather.2.cloned.1.call-update
  128.4 35.9 %all-gather.2.cloned.1.call-done = bf16[512,3584]{1,0:T(8,128)(2,1)} async-done(((bf16[32,3584]{1,0:T(8,128)(2,1)}), bf16[512,3584]{1,0:T(8,128)(2,1)}) %all-gather.2.cloned.1.call-update) | async-done | bytes 3670032 | tf_op jit(solution)/shard_map/all_gather | solution.py:105
  164.3 5.2 %fusion.8 = f32[512,512]{1,0:T(8,128)S(1)} fusion(bf16[512,3584]{1,0:T(8,128)(2,1)} %all-gather.2.cloned.1.call-done, bf16[3584,512]{1,0:T(8,128)(2,1)} %bitcast_multiply_fusion), kind=kOutput, calls=%fused_computation.18 | convolution fusion | flops 1879048192 | bytes 8388608 | tf_op jit(solution)/shard_map/dot_general | solution.py:106
  169.5 0.1 fusion.7
  169.6 3.8 %collective-permute-start.10 = (f32[64,512]{1,0:T(8,128)S(1)}, f32[64,512]{1,0:T(8,128)S(1)}, u32[]{:S(2)}, u32[]{:S(2)}) collective-permute-start(f32[64,512]{1,0:T(8,128)S(1)} %get-tuple-element.10), channel_id=1, source_target_pairs={{0,48},{16,32},{32,80},{48,64},{64,112},{80,96},{96,16},{112,0},{1... | collective-permute-start | bytes 393224 | tf_op jit(solution)/shard_map/ppermute | solution.py:80
  173.3 0.8 collective-permute-start.4
  174.2 1.7 collective-permute-start.5
  175.8 3.9 %collective-permute-start.6 = (f32[64,512]{1,0:T(8,128)S(1)}, f32[64,512]{1,0:T(8,128)S(1)}, u32[]{:S(2)}, u32[]{:S(2)}) collective-permute-start(f32[64,512]{1,0:T(8,128)S(1)} %get-tuple-element.14), channel_id=1, source_target_pairs={{0,112},{16,96},{32,16},{48,0},{64,48},{80,32},{96,80},{112,64},{1... | collective-permute-start | bytes 393224 | tf_op jit(solution)/shard_map/ppermute | solution.py:80
  179.7 0.7 collective-permute-start.7
  180.4 0.0 collective-permute-done.10
  180.4 3.3 %collective-permute-start.8 = (f32[64,512]{1,0:T(8,128)S(1)}, f32[64,512]{1,0:T(8,128)S(1)}, u32[]{:S(2)}, u32[]{:S(2)}) collective-permute-start(f32[64,512]{1,0:T(8,128)S(1)} %get-tuple-element.12), channel_id=1, source_target_pairs={{0,80},{16,64},{32,112},{48,96},{64,16},{80,0},{96,48},{112,32},{1... | collective-permute-start | bytes 393224 | tf_op jit(solution)/shard_map/ppermute | solution.py:80
  183.7 0.0 collective-permute-done.4
  183.7 0.7 collective-permute-start.9
  184.4 0.0 collective-permute-done.5
  184.4 0.1 collective-permute-done.6
  184.5 5.6 %collective-permute-done.7 = f32[64,512]{1,0:T(8,128)S(1)} collective-permute-done((f32[64,512]{1,0:T(8,128)S(1)}, f32[64,512]{1,0:T(8,128)S(1)}, u32[]{:S(2)}, u32[]{:S(2)}) %collective-permute-start.7) | collective-permute-done | bytes 131104 | tf_op jit(solution)/shard_map/ppermute | solution.py:80
  190.0 0.0 collective-permute-done.8
  190.0 2.1 %collective-permute-done.9 = f32[64,512]{1,0:T(8,128)S(1)} collective-permute-done((f32[64,512]{1,0:T(8,128)S(1)}, f32[64,512]{1,0:T(8,128)S(1)}, u32[]{:S(2)}, u32[]{:S(2)}) %collective-permute-start.9) | collective-permute-done | bytes 131104 | tf_op jit(solution)/shard_map/ppermute | solution.py:80
  192.1 0.7 fusion.6
  (5 shorter events, 0.0 us)
Async XLA Ops:
  6.5 119.9 %reduce-scatter.2.cloned.1.call-start = ((), (), s32[]{:S(2)}) async-start(), calls=%async_computation.1 | async-start | bytes 15597568 | tf_op jit(solution)/shard_map/reduce_scatter | solution.py:101
  6.5 6.0 %collective-permute-start = (bf16[64,512]{1,0:T(8,128)(2,1)}, bf16[64,512]{1,0:T(8,128)(2,1)S(1)}, u32[]{:S(2)}, u32[]{:S(2)}) collective-permute-start(bf16[64,512]{1,0:T(8,128)(2,1)} %param.7), channel_id=1, source_target_pairs={{0,16},{16,0},{32,48},{48,32},{64,80},{80,64},{96,112},{112,96},{1... | collective-permute-start | bytes 196616 | tf_op jit(solution)/shard_map/ppermute | solution.py:80
  12.5 8.6 %collective-permute-start.1 = (bf16[128,512]{1,0:T(8,128)(2,1)S(1)}, bf16[128,512]{1,0:T(8,128)(2,1)S(1)}, u32[]{:S(2)}, u32[]{:S(2)}) collective-permute-start(bf16[128,512]{1,0:T(8,128)(2,1)S(1)} %get-tuple-element.16), channel_id=1, source_target_pairs={{0,32},{16,48},{32,64},{48,80},{64,96},{80,112},{96,0},{112,16},{1... | collective-permute-start | bytes 393224 | tf_op jit(solution)/shard_map/ppermute | solution.py:80
  14.6 8.5 %collective-permute-start.2 = (bf16[128,512]{1,0:T(8,128)(2,1)S(1)}, bf16[128,512]{1,0:T(8,128)(2,1)S(1)}, u32[]{:S(2)}, u32[]{:S(2)}) collective-permute-start(bf16[128,512]{1,0:T(8,128)(2,1)S(1)} %get-tuple-element.16), channel_id=1, source_target_pairs={{0,64},{16,80},{32,96},{48,112},{64,0},{80,16},{96,32},{112,48},{1... | collective-permute-start | bytes 393224 | tf_op jit(solution)/shard_map/ppermute | solution.py:80
  18.2 5.0 %collective-permute-start.3 = (bf16[128,512]{1,0:T(8,128)(2,1)S(1)}, bf16[128,512]{1,0:T(8,128)(2,1)S(1)}, u32[]{:S(2)}, u32[]{:S(2)}) collective-permute-start(bf16[128,512]{1,0:T(8,128)(2,1)S(1)} %get-tuple-element.16), channel_id=1, source_target_pairs={{0,96},{16,112},{32,0},{48,16},{64,32},{80,48},{96,64},{112,80},{1... | collective-permute-start | bytes 393224 | tf_op jit(solution)/shard_map/ppermute | solution.py:80
  23.2 0.8 copy-start.1
  36.3 0.7 copy-start.2
  36.3 128.0 %all-gather.2.cloned.1.call-start = ((), (), s32[]{:S(2)}) async-start(), calls=%async_computation.2 | async-start | bytes 3899392 | tf_op jit(solution)/shard_map/all_gather | solution.py:105
  37.1 2.0 %copy-start = (bf16[3584,512]{1,0:T(8,128)(2,1)S(1)}, bf16[3584,512]{1,0:T(8,128)(2,1)}, u32[]{:S(2)}) copy-start(bf16[3584,512]{1,0:T(8,128)(2,1)} %param.10) | copy-start | bytes 11010052
  169.6 10.8 %collective-permute-start.10 = (f32[64,512]{1,0:T(8,128)S(1)}, f32[64,512]{1,0:T(8,128)S(1)}, u32[]{:S(2)}, u32[]{:S(2)}) collective-permute-start(f32[64,512]{1,0:T(8,128)S(1)} %get-tuple-element.10), channel_id=1, source_target_pairs={{0,48},{16,32},{32,80},{48,64},{64,112},{80,96},{96,16},{112,0},{1... | collective-permute-start | bytes 393224 | tf_op jit(solution)/shard_map/ppermute | solution.py:80
  173.3 10.4 %collective-permute-start.4 = (f32[64,512]{1,0:T(8,128)S(1)}, f32[64,512]{1,0:T(8,128)S(1)}, u32[]{:S(2)}, u32[]{:S(2)}) collective-permute-start(f32[64,512]{1,0:T(8,128)S(1)} %get-tuple-element.9), channel_id=1, source_target_pairs={{0,16},{16,0},{32,48},{48,32},{64,80},{80,64},{96,112},{112,96},{1... | collective-permute-start | bytes 393224 | tf_op jit(solution)/shard_map/ppermute | solution.py:80
  174.2 10.2 %collective-permute-start.5 = (f32[64,512]{1,0:T(8,128)S(1)}, f32[64,512]{1,0:T(8,128)S(1)}, u32[]{:S(2)}, u32[]{:S(2)}) collective-permute-start(f32[64,512]{1,0:T(8,128)S(1)} %get-tuple-element.15), channel_id=1, source_target_pairs={{0,96},{16,112},{32,0},{48,16},{64,32},{80,48},{96,64},{112,80},{1... | collective-permute-start | bytes 393224 | tf_op jit(solution)/shard_map/ppermute | solution.py:80
  175.8 8.6 %collective-permute-start.6 = (f32[64,512]{1,0:T(8,128)S(1)}, f32[64,512]{1,0:T(8,128)S(1)}, u32[]{:S(2)}, u32[]{:S(2)}) collective-permute-start(f32[64,512]{1,0:T(8,128)S(1)} %get-tuple-element.14), channel_id=1, source_target_pairs={{0,112},{16,96},{32,16},{48,0},{64,48},{80,32},{96,80},{112,64},{1... | collective-permute-start | bytes 393224 | tf_op jit(solution)/shard_map/ppermute | solution.py:80
  179.7 10.3 %collective-permute-start.7 = (f32[64,512]{1,0:T(8,128)S(1)}, f32[64,512]{1,0:T(8,128)S(1)}, u32[]{:S(2)}, u32[]{:S(2)}) collective-permute-start(f32[64,512]{1,0:T(8,128)S(1)} %get-tuple-element.13), channel_id=1, source_target_pairs={{0,64},{16,80},{32,96},{48,112},{64,0},{80,16},{96,32},{112,48},{1... | collective-permute-start | bytes 393224 | tf_op jit(solution)/shard_map/ppermute | solution.py:80
  180.4 9.6 %collective-permute-start.8 = (f32[64,512]{1,0:T(8,128)S(1)}, f32[64,512]{1,0:T(8,128)S(1)}, u32[]{:S(2)}, u32[]{:S(2)}) collective-permute-start(f32[64,512]{1,0:T(8,128)S(1)} %get-tuple-element.12), channel_id=1, source_target_pairs={{0,80},{16,64},{32,112},{48,96},{64,16},{80,0},{96,48},{112,32},{1... | collective-permute-start | bytes 393224 | tf_op jit(solution)/shard_map/ppermute | solution.py:80
  183.7 8.4 %collective-permute-start.9 = (f32[64,512]{1,0:T(8,128)S(1)}, f32[64,512]{1,0:T(8,128)S(1)}, u32[]{:S(2)}, u32[]{:S(2)}) collective-permute-start(f32[64,512]{1,0:T(8,128)S(1)} %get-tuple-element.11), channel_id=1, source_target_pairs={{0,32},{16,48},{32,64},{48,80},{64,96},{80,112},{96,0},{112,16},{1... | collective-permute-start | bytes 393224 | tf_op jit(solution)/shard_map/ppermute | solution.py:80
Sparse Core Ops, SparseCore 0:
  36.4 89.9 reduce-scatter.1
  128.6 35.6 all-gather.1

commit v11 on v10

--- a/solution.py
+++ b/solution.py
@@ -103,20 +103,25 @@
     summed, down_mat = lax.optimization_barrier((summed, down_mat))
     hidden = (jax.nn.silu(summed[:, :hidden_cols]) * summed[:, hidden_cols:]).astype(jnp.bfloat16)
     hidden_all = lax.all_gather(hidden, COL, axis=0, tiled=True)
-    partial_out = jnp.dot(
-        hidden_all, down_mat, preferred_element_type=jnp.float32
-    )
     t = tokens.shape[0]
-    total = partial_out[:t]
+
+    def block(b):
+        return jnp.dot(
+            hidden_all[b * t:(b + 1) * t], down_mat, preferred_element_type=jnp.float32
+        )
+
+    total = None
     for s in range(n_z):
         for i in range(n_hi):
             if s == 0 and i == 0:
                 continue
             b = s * n_hi + i
-            total = total + permute(
-                partial_out[b * t:(b + 1) * t],
+            sent = permute(
+                block(b),
                 lambda L, s=s, i=i: ((L // n_hi - s) % n_z) * n_hi + ((L % n_hi) ^ i),
             )
+            total = sent if total is None else total + sent
+    total = block(0) + total
     return total.astype(jnp.bfloat16)
 
 

time: 201 us -> 204 us (1.015)
  matrix products: 5.21 us -> 9.87 us
    dot_general x1 -> x8, matrix products: 5.21 us -> 9.87 us  [block(): jnp.dot(hidden_all[b * t:(b + 1) * t], down_mat, preferred_element_type=j...]
  transfers between devices with their start and end apart: 13 -> 13, of which waited for: 9 -> 9; matrix products, arithmetic and copies ran while one was open for 2% -> 5% of each run, Pallas kernels for 0% -> 0%
where the time goes in v11:
time: 204 us
  waiting for transfers between devices  135 us (66%)
  starting transfers between devices  24.3 us (12%)
  between operations  13.5 us (7%)
  Pallas kernels  12.3 us (6%)
  matrix products  9.87 us (5%)
  local copies, waits for them, and re-layouts  4.47 us (2%)
  other arithmetic  4.26 us (2%)
    reduce_scatter x1, waiting for transfers between devices, on_device(): summed = lax.psum_scatter(pair, COL, scatter_dimension=0, tiled=True)  85 us
    all_gather x1, waiting for transfers between devices, on_device(): hidden_all = lax.all_gather(hidden, COL, axis=0, tiled=True)  35.8 us
    ppermute x11, starting transfers between devices, permute(): lax.ppermute(x, ROW, [(i, dest(i)) for i in range(lax.axis_size(ROW))])  24.2 us
    ppermute x11, waiting for transfers between devices, permute(): lax.ppermute(x, ROW, [(i, dest(i)) for i in range(lax.axis_size(ROW))])  14.1 us
    pallas_call x1, Pallas kernels, gate_up(): pl.pallas_call(functools.partial(_gate_up_kernel, n_half, n_feat), grid_s...  12.3 us
    dot_general x8, matrix products, block(): jnp.dot(hidden_all[b * t:(b + 1) * t], down_mat, preferred_element_type=j...  9.87 us
  transfers between devices with their start and end apart: 13, of which 9 were waited for; matrix products, arithmetic and copies ran while one was open for 5% of the time, Pallas kernels for 0%

profile of v11, /device:TPU:0, one launch (start us, length us, event | category | flops | bytes accessed | tf_op | source)
XLA Modules:
  0.0 203.7 jit_solution(16893318859954701834)
XLA Ops:
  6.5 0.0 reduce-scatter.2.cloned.1.call-start
  6.5 3.1 %collective-permute-start = (bf16[64,512]{1,0:T(8,128)(2,1)}, bf16[64,512]{1,0:T(8,128)(2,1)S(1)}, u32[]{:S(2)}, u32[]{:S(2)}) collective-permute-start(bf16[64,512]{1,0:T(8,128)(2,1)} %param.7), channel_id=1, source_target_pairs={{0,16},{16,0},{32,48},{48,32},{64,80},{80,64},{96,112},{112,96},{1... | collective-permute-start | bytes 196616 | tf_op jit(solution)/shard_map/ppermute | solution.py:80
  9.7 0.9 constant_dynamic-update-slice_fusion.1
  10.6 2.0 collective-permute-done
  12.5 2.1 %collective-permute-start.1 = (bf16[128,512]{1,0:T(8,128)(2,1)S(1)}, bf16[128,512]{1,0:T(8,128)(2,1)S(1)}, u32[]{:S(2)}, u32[]{:S(2)}) collective-permute-start(bf16[128,512]{1,0:T(8,128)(2,1)S(1)} %get-tuple-element.9), channel_id=1, source_target_pairs={{0,32},{16,48},{32,64},{48,80},{64,96},{80,112},{96,0},{112,16},{1... | collective-permute-start | bytes 393224 | tf_op jit(solution)/shard_map/ppermute | solution.py:80
  14.6 3.6 %collective-permute-start.2 = (bf16[128,512]{1,0:T(8,128)(2,1)S(1)}, bf16[128,512]{1,0:T(8,128)(2,1)S(1)}, u32[]{:S(2)}, u32[]{:S(2)}) collective-permute-start(bf16[128,512]{1,0:T(8,128)(2,1)S(1)} %get-tuple-element.9), channel_id=1, source_target_pairs={{0,64},{16,80},{32,96},{48,112},{64,0},{80,16},{96,32},{112,48},{1... | collective-permute-start | bytes 393224 | tf_op jit(solution)/shard_map/ppermute | solution.py:80
  18.2 1.0 collective-permute-start.3
  19.2 1.9 collective-permute-done.1
  21.1 2.0 collective-permute-done.2
  23.1 0.1 collective-permute-done.3
  23.2 0.0 copy-start.3
  23.2 0.8 copy-done.3
  24.0 12.3 %shard_map.73 = f32[512,7168]{1,0:T(8,128)} custom-call(s32[4,28]{1,0:T(4,128)} %gk_ref.1, s32[4,28]{1,0:T(4,128)} %uk_ref.1, bf16[512,512]{1,0:T(8,128)(2,1)} %copy-done.3, bf16[512,3584]{1,0:T(8,128)(2,1)} %gw_ref.1, bf16[512,3584]{1,0:T(8,128)(2,1)} %uw_ref.1), custom_call_target="tpu_custom_call" | custom-call | flops 3758096384 | bytes 22544384 | tf_op jit(solution)/shard_map/pallas_call | solution.py:54
  36.3 0.0 copy-start.4
  36.3 0.0 reduce-scatter.2.cloned.1.call-update
  36.4 0.0 all-gather.2.cloned.1.call-start
  36.4 0.6 copy-done.4
  37.0 0.1 copy.8
  37.1 0.0 copy-start.2
  37.1 1.0 mul.18
  38.2 1.0 copy-done.2
  39.2 2.3 %bitcast_multiply_fusion = bf16[3584,512]{1,0:T(8,128)(2,1)} fusion(bf16[3584,512]{1,0:T(8,128)(2,1)S(1)} %copy-done.2, bf16[448,8,4,128]{3,2,1,0:T(4,128)(2,1)S(1)} %bitcast.12), kind=kLoop, calls=%fused_computation | loop fusion | flops 1835008 | bytes 11010048 | tf_op jit(solution)/shard_map/mul | solution.py:73
  41.5 85.0 %reduce-scatter.2.cloned.1.call-done = f32[32,7168]{1,0:T(8,128)} async-done(((f32[512,7168]{1,0:T(8,128)}), f32[32,7168]{1,0:T(8,128)}) %reduce-scatter.2.cloned.1.call-update) | async-done | bytes 917520 | tf_op jit(solution)/shard_map/reduce_scatter | solution.py:101
  126.5 2.0 multiply_convert_fusion
  128.5 0.0 all-gather.2.cloned.1.call-update
  128.5 35.8 %all-gather.2.cloned.1.call-done = bf16[512,3584]{1,0:T(8,128)(2,1)} async-done(((bf16[32,3584]{1,0:T(8,128)(2,1)}), bf16[512,3584]{1,0:T(8,128)(2,1)}) %all-gather.2.cloned.1.call-update) | async-done | bytes 3670032 | tf_op jit(solution)/shard_map/all_gather | solution.py:105
  164.3 0.0 copy-start
  164.3 0.0 copy-start.1
  164.3 3.1 %fusion.10 = f32[64,512]{1,0:T(8,128)S(1)} fusion(bf16[3584,512]{1,0:T(8,128)(2,1)} %bitcast_multiply_fusion, bf16[512,3584]{1,0:T(8,128)(2,1)} %all-gather.2.cloned.1.call-done), kind=kOutput, calls=%fused_computation.11 | convolution fusion | flops 234881024 | bytes 4259840 | tf_op jit(solution)/shard_map/dot_general | solution.py:109
  167.4 3.0 %collective-permute-start.5 = (f32[64,512]{1,0:T(8,128)S(1)}, f32[64,512]{1,0:T(8,128)S(1)}, u32[]{:S(2)}, u32[]{:S(2)}) collective-permute-start(f32[64,512]{1,0:T(8,128)S(1)} %fusion.10), channel_id=1, source_target_pairs={{0,96},{16,112},{32,0},{48,16},{64,32},{80,48},{96,64},{112,80},{1... | collective-permute-start | bytes 393224 | tf_op jit(solution)/shard_map/ppermute | solution.py:80
  170.4 0.0 copy-done
  170.4 1.8 fusion.12
  172.2 2.8 %collective-permute-start.4 = (f32[64,512]{1,0:T(8,128)S(1)}, f32[64,512]{1,0:T(8,128)S(1)}, u32[]{:S(2)}, u32[]{:S(2)}) collective-permute-start(f32[64,512]{1,0:T(8,128)S(1)} %fusion.12), channel_id=1, source_target_pairs={{0,16},{16,0},{32,48},{48,32},{64,80},{80,64},{96,112},{112,96},{1... | collective-permute-start | bytes 393224 | tf_op jit(solution)/shard_map/ppermute | solution.py:80
  175.0 0.0 copy-done.1
  175.0 0.7 fusion.8
  175.7 1.1 collective-permute-start.6
  176.8 0.7 fusion.6
  177.6 0.5 collective-permute-start.7
  178.0 0.7 fusion.4
  178.8 5.4 %collective-permute-start.8 = (f32[64,512]{1,0:T(8,128)S(1)}, f32[64,512]{1,0:T(8,128)S(1)}, u32[]{:S(2)}, u32[]{:S(2)}) collective-permute-start(f32[64,512]{1,0:T(8,128)S(1)} %fusion.4), channel_id=1, source_target_pairs={{0,80},{16,64},{32,112},{48,96},{64,16},{80,0},{96,48},{112,32},{1... | collective-permute-start | bytes 393224 | tf_op jit(solution)/shard_map/ppermute | solution.py:80
  184.1 0.7 fusion.2
  184.9 0.7 fusion
  185.6 0.0 collective-permute-done.5
  185.6 1.3 collective-permute-start.9
  186.9 0.0 collective-permute-done.4
  187.0 0.4 collective-permute-start.10
  187.3 0.0 collective-permute-done.6
  187.3 0.0 collective-permute-done.7
  187.3 0.4 collective-permute-done.8
  187.8 5.5 %collective-permute-done.9 = f32[64,512]{1,0:T(8,128)S(1)} collective-permute-done((f32[64,512]{1,0:T(8,128)S(1)}, f32[64,512]{1,0:T(8,128)S(1)}, u32[]{:S(2)}, u32[]{:S(2)}) %collective-permute-start.9) | collective-permute-done | bytes 131104 | tf_op jit(solution)/shard_map/ppermute | solution.py:80
  193.3 2.3 %collective-permute-done.10 = f32[64,512]{1,0:T(8,128)S(1)} collective-permute-done((f32[64,512]{1,0:T(8,128)S(1)}, f32[64,512]{1,0:T(8,128)S(1)}, u32[]{:S(2)}, u32[]{:S(2)}) %collective-permute-start.10) | collective-permute-done | bytes 131104 | tf_op jit(solution)/shard_map/ppermute | solution.py:80
  195.5 1.4 add_convert_fusion
  (5 shorter events, 0.0 us)
Async XLA Ops:
  6.5 120.0 %reduce-scatter.2.cloned.1.call-start = ((), (), s32[]{:S(2)}) async-start(), calls=%async_computation.1 | async-start | bytes 15597568 | tf_op jit(solution)/shard_map/reduce_scatter | solution.py:101
  6.5 6.0 %collective-permute-start = (bf16[64,512]{1,0:T(8,128)(2,1)}, bf16[64,512]{1,0:T(8,128)(2,1)S(1)}, u32[]{:S(2)}, u32[]{:S(2)}) collective-permute-start(bf16[64,512]{1,0:T(8,128)(2,1)} %param.7), channel_id=1, source_target_pairs={{0,16},{16,0},{32,48},{48,32},{64,80},{80,64},{96,112},{112,96},{1... | collective-permute-start | bytes 196616 | tf_op jit(solution)/shard_map/ppermute | solution.py:80
  12.5 8.6 %collective-permute-start.1 = (bf16[128,512]{1,0:T(8,128)(2,1)S(1)}, bf16[128,512]{1,0:T(8,128)(2,1)S(1)}, u32[]{:S(2)}, u32[]{:S(2)}) collective-permute-start(bf16[128,512]{1,0:T(8,128)(2,1)S(1)} %get-tuple-element.9), channel_id=1, source_target_pairs={{0,32},{16,48},{32,64},{48,80},{64,96},{80,112},{96,0},{112,16},{1... | collective-permute-start | bytes 393224 | tf_op jit(solution)/shard_map/ppermute | solution.py:80
  14.6 8.5 %collective-permute-start.2 = (bf16[128,512]{1,0:T(8,128)(2,1)S(1)}, bf16[128,512]{1,0:T(8,128)(2,1)S(1)}, u32[]{:S(2)}, u32[]{:S(2)}) collective-permute-start(bf16[128,512]{1,0:T(8,128)(2,1)S(1)} %get-tuple-element.9), channel_id=1, source_target_pairs={{0,64},{16,80},{32,96},{48,112},{64,0},{80,16},{96,32},{112,48},{1... | collective-permute-start | bytes 393224 | tf_op jit(solution)/shard_map/ppermute | solution.py:80
  18.2 5.0 %collective-permute-start.3 = (bf16[128,512]{1,0:T(8,128)(2,1)S(1)}, bf16[128,512]{1,0:T(8,128)(2,1)S(1)}, u32[]{:S(2)}, u32[]{:S(2)}) collective-permute-start(bf16[128,512]{1,0:T(8,128)(2,1)S(1)} %get-tuple-element.9), channel_id=1, source_target_pairs={{0,96},{16,112},{32,0},{48,16},{64,32},{80,48},{96,64},{112,80},{1... | collective-permute-start | bytes 393224 | tf_op jit(solution)/shard_map/ppermute | solution.py:80
  23.2 0.8 copy-start.3
  36.3 0.7 copy-start.4
  36.4 128.0 %all-gather.2.cloned.1.call-start = ((), (), s32[]{:S(2)}) async-start(), calls=%async_computation.2 | async-start | bytes 3899392 | tf_op jit(solution)/shard_map/all_gather | solution.py:105
  37.1 2.0 %copy-start.2 = (bf16[3584,512]{1,0:T(8,128)(2,1)S(1)}, bf16[3584,512]{1,0:T(8,128)(2,1)}, u32[]{:S(2)}) copy-start(bf16[3584,512]{1,0:T(8,128)(2,1)} %param.10) | copy-start | bytes 11010052
  164.3 6.1 %copy-start = (bf16[3584,512]{1,0:T(8,128)(2,1)S(1)}, bf16[3584,512]{1,0:T(8,128)(2,1)}, u32[]{:S(2)}) copy-start(bf16[3584,512]{1,0:T(8,128)(2,1)} %bitcast_multiply_fusion) | copy-start | bytes 11010052
  164.3 10.6 %copy-start.1 = (bf16[512,3584]{1,0:T(8,128)(2,1)S(1)}, bf16[512,3584]{1,0:T(8,128)(2,1)}, u32[]{:S(2)}) copy-start(bf16[512,3584]{1,0:T(8,128)(2,1)} %all-gather.2.cloned.1.call-done) | copy-start | bytes 11010052
  167.4 18.2 %collective-permute-start.5 = (f32[64,512]{1,0:T(8,128)S(1)}, f32[64,512]{1,0:T(8,128)S(1)}, u32[]{:S(2)}, u32[]{:S(2)}) collective-permute-start(f32[64,512]{1,0:T(8,128)S(1)} %fusion.10), channel_id=1, source_target_pairs={{0,96},{16,112},{32,0},{48,16},{64,32},{80,48},{96,64},{112,80},{1... | collective-permute-start | bytes 393224 | tf_op jit(solution)/shard_map/ppermute | solution.py:80
  172.2 14.8 %collective-permute-start.4 = (f32[64,512]{1,0:T(8,128)S(1)}, f32[64,512]{1,0:T(8,128)S(1)}, u32[]{:S(2)}, u32[]{:S(2)}) collective-permute-start(f32[64,512]{1,0:T(8,128)S(1)} %fusion.12), channel_id=1, source_target_pairs={{0,16},{16,0},{32,48},{48,32},{64,80},{80,64},{96,112},{112,96},{1... | collective-permute-start | bytes 393224 | tf_op jit(solution)/shard_map/ppermute | solution.py:80
  175.7 11.6 %collective-permute-start.6 = (f32[64,512]{1,0:T(8,128)S(1)}, f32[64,512]{1,0:T(8,128)S(1)}, u32[]{:S(2)}, u32[]{:S(2)}) collective-permute-start(f32[64,512]{1,0:T(8,128)S(1)} %fusion.8), channel_id=1, source_target_pairs={{0,112},{16,96},{32,16},{48,0},{64,48},{80,32},{96,80},{112,64},{1... | collective-permute-start | bytes 393224 | tf_op jit(solution)/shard_map/ppermute | solution.py:80
  177.6 9.8 %collective-permute-start.7 = (f32[64,512]{1,0:T(8,128)S(1)}, f32[64,512]{1,0:T(8,128)S(1)}, u32[]{:S(2)}, u32[]{:S(2)}) collective-permute-start(f32[64,512]{1,0:T(8,128)S(1)} %fusion.6), channel_id=1, source_target_pairs={{0,64},{16,80},{32,96},{48,112},{64,0},{80,16},{96,32},{112,48},{1... | collective-permute-start | bytes 393224 | tf_op jit(solution)/shard_map/ppermute | solution.py:80
  178.8 9.0 %collective-permute-start.8 = (f32[64,512]{1,0:T(8,128)S(1)}, f32[64,512]{1,0:T(8,128)S(1)}, u32[]{:S(2)}, u32[]{:S(2)}) collective-permute-start(f32[64,512]{1,0:T(8,128)S(1)} %fusion.4), channel_id=1, source_target_pairs={{0,80},{16,64},{32,112},{48,96},{64,16},{80,0},{96,48},{112,32},{1... | collective-permute-start | bytes 393224 | tf_op jit(solution)/shard_map/ppermute | solution.py:80
  185.6 7.7 %collective-permute-start.9 = (f32[64,512]{1,0:T(8,128)S(1)}, f32[64,512]{1,0:T(8,128)S(1)}, u32[]{:S(2)}, u32[]{:S(2)}) collective-permute-start(f32[64,512]{1,0:T(8,128)S(1)} %fusion.2), channel_id=1, source_target_pairs={{0,32},{16,48},{32,64},{48,80},{64,96},{80,112},{96,0},{112,16},{1... | collective-permute-start | bytes 393224 | tf_op jit(solution)/shard_map/ppermute | solution.py:80
  187.0 8.6 %collective-permute-start.10 = (f32[64,512]{1,0:T(8,128)S(1)}, f32[64,512]{1,0:T(8,128)S(1)}, u32[]{:S(2)}, u32[]{:S(2)}) collective-permute-start(f32[64,512]{1,0:T(8,128)S(1)} %fusion), channel_id=1, source_target_pairs={{0,48},{16,32},{32,80},{48,64},{64,112},{80,96},{96,16},{112,0},{1... | collective-permute-start | bytes 393224 | tf_op jit(solution)/shard_map/ppermute | solution.py:80
Sparse Core Ops, SparseCore 0:
  36.5 89.9 reduce-scatter.1
  128.6 35.6 all-gather.1

commit v12 on v10

--- a/solution.py
+++ b/solution.py
@@ -12,7 +12,8 @@
 TILE = 1792
 
 
-def _gate_up_kernel(n_half, n_feat, gk_ref, uk_ref, x_ref, gw_ref, uw_ref, o_ref, w_scr):
+def _gate_up_kernel(n_half, n_feat, gk_ref, uk_ref, x_ref, gw_ref, uw_ref, *refs):
+    o_ref, w_scr = refs[-2:]
     j = pl.program_id(0)
 
     def build(w_ref, k_ref, jj):
@@ -35,32 +36,41 @@
     o_ref[...] = jnp.dot(x_ref[...], w_scr[...], preferred_element_type=jnp.float32)
 
 
-def gate_up(x, gw, uw, gk, uk):
+def gate_up(x, gw, uw, gk, uk, rows, row_block, into=None):
     t, f = x.shape
     h = gw.shape[1]
     n_half = h // TILE
     n_feat = f // BLOCK
+    in_specs = [
+        pl.BlockSpec((t, f), lambda j, gk, uk: (0, 0)),
+        pl.BlockSpec((f, TILE), lambda j, gk, uk: (0, jnp.minimum(j, n_half - 1))),
+        pl.BlockSpec((f, TILE), lambda j, gk, uk: (0, jnp.maximum(j - n_half, 0))),
+    ]
+    operands = [gk, uk, x, gw, uw]
+    aliases = {}
+    if into is not None:
+        in_specs.append(pl.BlockSpec(memory_space=pl.ANY))
+        aliases = {len(operands): 0}
+        operands.append(into)
     grid_spec = pltpu.PrefetchScalarGridSpec(
         num_scalar_prefetch=2,
         grid=(2 * n_half,),
-        in_specs=[
-            pl.BlockSpec((t, f), lambda j, gk, uk: (0, 0)),
-            pl.BlockSpec((f, TILE), lambda j, gk, uk: (0, jnp.minimum(j, n_half - 1))),
-            pl.BlockSpec((f, TILE), lambda j, gk, uk: (0, jnp.maximum(j - n_half, 0))),
-        ],
-        out_specs=pl.BlockSpec((t, TILE), lambda j, gk, uk: (0, j)),
+        in_specs=in_specs,
+        out_specs=pl.BlockSpec((t, TILE), lambda j, gk, uk: (row_block, j)),
         scratch_shapes=[pltpu.VMEM((f, TILE), x.dtype)],
     )
     return pl.pallas_call(
         functools.partial(_gate_up_kernel, n_half, n_feat),
         grid_spec=grid_spec,
-        out_shape=jax.ShapeDtypeStruct((t, 2 * h), jnp.float32),
+        out_shape=jax.ShapeDtypeStruct((rows, 2 * h), jnp.float32),
+        input_output_aliases=aliases,
         compiler_params=pltpu.CompilerParams(dimension_semantics=("arbitrary",)),
         cost_estimate=pl.CostEstimate(
             flops=2 * t * f * 2 * h, transcendentals=0,
             bytes_accessed=2 * (t * f + 2 * f * h) + 4 * t * 2 * h,
         ),
-    )(gk, uk, x, gw, uw)
+    )(*operands)
+
 
 ROW = ("z", "x_hi")
 COL = ("x_lo", "y", "core")
@@ -94,10 +104,14 @@
     n_z = lax.axis_size("z")
     hidden_cols = gate_weight.shape[1]
     pair_rows = jnp.concatenate([tokens, hi_swap(tokens)], axis=0)
-    features = jnp.concatenate(
-        [pair_rows] + [z_shift(pair_rows, s, n_hi) for s in range(1, n_z)], axis=0
+    shifted = [z_shift(pair_rows, s, n_hi) for s in range(1, n_z)]
+    features = jnp.concatenate([pair_rows] + shifted, axis=0)
+    rows = features.shape[0]
+    half = rows // 2
+    pair = gate_up(features[:half], gate_weight, up_weight, gate_keep, up_keep, rows, 0)
+    pair = gate_up(
+        features[half:], gate_weight, up_weight, gate_keep, up_keep, rows, 1, into=pair
     )
-    pair = gate_up(features, gate_weight, up_weight, gate_keep, up_keep)
     summed = lax.psum_scatter(pair, COL, scatter_dimension=0, tiled=True)
     down_mat = expand(down_weight, down_keep)
     summed, down_mat = lax.optimization_barrier((summed, down_mat))

time: 201 us -> 206 us (1.025)
  Pallas kernels: 12.3 us -> 19.2 us
  waiting for transfers between devices: 135 us -> 132 us
  other arithmetic: 4.97 us -> 7.3 us
    pallas_call x1 -> x2, Pallas kernels: 12.3 us -> 19.2 us  [gate_up(): pl.pallas_call(functools.partial(_gate_up_kernel, n_half, n_feat), grid_s...]
    concatenate x0 -> x2, other arithmetic: none -> 2.31 us  [on_device(): features = jnp.concatenate([pair_rows] + shifted, axis=0)]
  transfers between devices with their start and end apart: 13 -> 13, of which waited for: 9 -> 7; matrix products, arithmetic and copies ran while one was open for 2% -> 3% of each run, Pallas kernels for 0% -> 5%
where the time goes in v12:
time: 206 us; the launch traced here: 205 us
  waiting for transfers between devices  132 us (64%)
  starting transfers between devices  24.6 us (12%)
  Pallas kernels  19.2 us (9%)
  between operations  13.4 us (7%)
  other arithmetic  7.3 us (4%)
  matrix products  5.21 us (3%)
  local copies, waits for them, and re-layouts  3.7 us (2%)
    reduce_scatter x1, waiting for transfers between devices, on_device(): summed = lax.psum_scatter(pair, COL, scatter_dimension=0, tiled=True)  84.1 us
    all_gather x1, waiting for transfers between devices, on_device(): hidden_all = lax.all_gather(hidden, COL, axis=0, tiled=True)  36.1 us
    ppermute x11, starting transfers between devices, permute(): lax.ppermute(x, ROW, [(i, dest(i)) for i in range(lax.axis_size(ROW))])  24.5 us
    pallas_call x2, Pallas kernels, gate_up(): pl.pallas_call(functools.partial(_gate_up_kernel, n_half, n_feat), grid_s...  19.2 us
    ppermute x11, waiting for transfers between devices, permute(): lax.ppermute(x, ROW, [(i, dest(i)) for i in range(lax.axis_size(ROW))])  11.6 us
    dot_general x1, matrix products, on_device(): jnp.dot(hidden_all, down_mat, preferred_element_type=jnp.float32)  5.21 us
  transfers between devices with their start and end apart: 13, of which 7 were waited for; matrix products, arithmetic and copies ran while one was open for 3% of the time, Pallas kernels for 5%

profile of v12, /device:TPU:0, one launch (start us, length us, event | category | flops | bytes accessed | tf_op | source)
XLA Modules:
  0.0 205.3 jit_solution(17180924004076464073)
XLA Ops:
  6.5 0.0 reduce-scatter.2.cloned.1.call-start
  6.5 3.1 %collective-permute-start = (bf16[64,512]{1,0:T(8,128)(2,1)}, bf16[64,512]{1,0:T(8,128)(2,1)S(1)}, u32[]{:S(2)}, u32[]{:S(2)}) collective-permute-start(bf16[64,512]{1,0:T(8,128)(2,1)} %param.7), channel_id=1, source_target_pairs={{0,16},{16,0},{32,48},{48,32},{64,80},{80,64},{96,112},{112,96},{1... | collective-permute-start | bytes 196616 | tf_op jit(solution)/shard_map/ppermute | solution.py:90
  9.7 0.9 constant_dynamic-update-slice_fusion.1
  10.6 2.0 collective-permute-done
  12.5 2.0 collective-permute-start.3
  14.6 3.6 %collective-permute-start.1 = (bf16[128,512]{1,0:T(8,128)(2,1)S(1)}, bf16[128,512]{1,0:T(8,128)(2,1)S(1)}, u32[]{:S(2)}, u32[]{:S(2)}) collective-permute-start(bf16[128,512]{1,0:T(8,128)(2,1)S(1)} %constant_dynamic-update-slice_fusion), channel_id=1, source_target_pairs={{0,64},{16,80},{32,96},{48,112},{64,0},{80,16},{96,32},{112,48},{1... | collective-permute-start | bytes 393224 | tf_op jit(solution)/shard_map/ppermute | solution.py:90
  18.1 1.0 collective-permute-start.2
  19.1 1.9 collective-permute-done.3
  21.0 1.6 pad_maximum_fusion.1.x_ref
  22.6 9.6 %shard_map.73.refs_0_ = f32[512,7168]{1,0:T(8,128)} custom-call(s32[4,28]{1,0:T(4,128)} %gk_ref.3, s32[4,28]{1,0:T(4,128)} %uk_ref.3, bf16[256,512]{1,0:T(8,128)(2,1)} %pad_maximum_fusion.1.x_ref, bf16[512,3584]{1,0:T(8,128)(2,1)} %gw_ref.3, bf16[512,3584]{1,0:T(8,128)(2,1)} %uw_ref.3), custom_call_target="tpu_custom_call" | custom-call | flops 1879048192 | bytes 14942208 | tf_op jit(solution)/shard_map/pallas_call | solution.py:62
  32.2 0.0 collective-permute-done.1
  32.2 0.0 collective-permute-done.2
  32.2 0.7 pad_maximum_fusion.x_ref
  32.9 9.6 %shard_map.74 = f32[512,7168]{1,0:T(8,128)} custom-call(s32[4,28]{1,0:T(4,128)} %gk_ref.3, s32[4,28]{1,0:T(4,128)} %uk_ref.3, bf16[256,512]{1,0:T(8,128)(2,1)} %pad_maximum_fusion.x_ref, bf16[512,3584]{1,0:T(8,128)(2,1)} %gw_ref.3, bf16[512,3584]{1,0:T(8,128)(2,1)} %uw_ref.3, f32[512,7168]{1,0:T(8,128)} %shard_map.73.refs_0_), custom_call_target="tpu_custom_call", output_to_operand_aliasing={{}: (5, {})} | custom-call | flops 1879048192 | bytes 14942208 | tf_op jit(solution)/shard_map/pallas_call | solution.py:62
  42.6 0.0 copy-start.1
  42.6 0.0 reduce-scatter.2.cloned.1.call-update
  42.6 0.0 all-gather.2.cloned.1.call-start
  42.7 0.6 copy-done.1
  43.3 0.1 copy.9
  43.4 0.0 copy-start
  43.4 1.0 mul.18
  44.4 1.0 copy-done
  45.4 2.3 %bitcast_multiply_fusion = bf16[3584,512]{1,0:T(8,128)(2,1)} fusion(bf16[3584,512]{1,0:T(8,128)(2,1)S(1)} %copy-done, bf16[448,8,4,128]{3,2,1,0:T(4,128)(2,1)S(1)} %bitcast.6), kind=kLoop, calls=%fused_computation | loop fusion | flops 1835008 | bytes 11010048 | tf_op jit(solution)/shard_map/mul | solution.py:83
  47.7 84.1 %reduce-scatter.2.cloned.1.call-done = f32[32,7168]{1,0:T(8,128)} async-done(((f32[512,7168]{1,0:T(8,128)}), f32[32,7168]{1,0:T(8,128)}) %reduce-scatter.2.cloned.1.call-update) | async-done | bytes 917520 | tf_op jit(solution)/shard_map/reduce_scatter | solution.py:115
  131.8 2.0 multiply_convert_fusion
  133.8 0.0 all-gather.2.cloned.1.call-update
  133.8 36.1 %all-gather.2.cloned.1.call-done = bf16[512,3584]{1,0:T(8,128)(2,1)} async-done(((bf16[32,3584]{1,0:T(8,128)(2,1)}), bf16[512,3584]{1,0:T(8,128)(2,1)}) %all-gather.2.cloned.1.call-update) | async-done | bytes 3670032 | tf_op jit(solution)/shard_map/all_gather | solution.py:119
  169.9 5.2 %fusion.8 = f32[512,512]{1,0:T(8,128)S(1)} fusion(bf16[512,3584]{1,0:T(8,128)(2,1)} %all-gather.2.cloned.1.call-done, bf16[3584,512]{1,0:T(8,128)(2,1)} %bitcast_multiply_fusion), kind=kOutput, calls=%fused_computation.15 | convolution fusion | flops 1879048192 | bytes 8388608 | tf_op jit(solution)/shard_map/dot_general | solution.py:120
  175.1 0.1 fusion.7
  175.2 3.8 %collective-permute-start.10 = (f32[64,512]{1,0:T(8,128)S(1)}, f32[64,512]{1,0:T(8,128)S(1)}, u32[]{:S(2)}, u32[]{:S(2)}) collective-permute-start(f32[64,512]{1,0:T(8,128)S(1)} %get-tuple-element.10), channel_id=1, source_target_pairs={{0,48},{16,32},{32,80},{48,64},{64,112},{80,96},{96,16},{112,0},{1... | collective-permute-start | bytes 393224 | tf_op jit(solution)/shard_map/ppermute | solution.py:90
  178.9 0.8 collective-permute-start.4
  179.8 1.7 collective-permute-start.5
  181.5 3.9 %collective-permute-start.6 = (f32[64,512]{1,0:T(8,128)S(1)}, f32[64,512]{1,0:T(8,128)S(1)}, u32[]{:S(2)}, u32[]{:S(2)}) collective-permute-start(f32[64,512]{1,0:T(8,128)S(1)} %get-tuple-element.14), channel_id=1, source_target_pairs={{0,112},{16,96},{32,16},{48,0},{64,48},{80,32},{96,80},{112,64},{1... | collective-permute-start | bytes 393224 | tf_op jit(solution)/shard_map/ppermute | solution.py:90
  185.3 0.7 collective-permute-start.7
  186.0 0.0 collective-permute-done.10
  186.0 3.3 %collective-permute-start.8 = (f32[64,512]{1,0:T(8,128)S(1)}, f32[64,512]{1,0:T(8,128)S(1)}, u32[]{:S(2)}, u32[]{:S(2)}) collective-permute-start(f32[64,512]{1,0:T(8,128)S(1)} %get-tuple-element.12), channel_id=1, source_target_pairs={{0,80},{16,64},{32,112},{48,96},{64,16},{80,0},{96,48},{112,32},{1... | collective-permute-start | bytes 393224 | tf_op jit(solution)/shard_map/ppermute | solution.py:90
  189.3 0.0 collective-permute-done.4
  189.3 0.7 collective-permute-start.9
  190.0 0.0 collective-permute-done.5
  190.0 0.1 collective-permute-done.6
  190.1 5.6 %collective-permute-done.7 = f32[64,512]{1,0:T(8,128)S(1)} collective-permute-done((f32[64,512]{1,0:T(8,128)S(1)}, f32[64,512]{1,0:T(8,128)S(1)}, u32[]{:S(2)}, u32[]{:S(2)}) %collective-permute-start.7) | collective-permute-done | bytes 131104 | tf_op jit(solution)/shard_map/ppermute | solution.py:90
  195.7 0.0 collective-permute-done.8
  195.7 2.1 %collective-permute-done.9 = f32[64,512]{1,0:T(8,128)S(1)} collective-permute-done((f32[64,512]{1,0:T(8,128)S(1)}, f32[64,512]{1,0:T(8,128)S(1)}, u32[]{:S(2)}, u32[]{:S(2)}) %collective-permute-start.9) | collective-permute-done | bytes 131104 | tf_op jit(solution)/shard_map/ppermute | solution.py:90
  197.8 0.7 fusion.6
  (2 shorter events, 0.0 us)
Async XLA Ops:
  6.5 125.3 %reduce-scatter.2.cloned.1.call-start = ((), (), s32[]{:S(2)}) async-start(), calls=%async_computation.1 | async-start | bytes 15597568 | tf_op jit(solution)/shard_map/reduce_scatter | solution.py:115
  6.5 6.0 %collective-permute-start = (bf16[64,512]{1,0:T(8,128)(2,1)}, bf16[64,512]{1,0:T(8,128)(2,1)S(1)}, u32[]{:S(2)}, u32[]{:S(2)}) collective-permute-start(bf16[64,512]{1,0:T(8,128)(2,1)} %param.7), channel_id=1, source_target_pairs={{0,16},{16,0},{32,48},{48,32},{64,80},{80,64},{96,112},{112,96},{1... | collective-permute-start | bytes 196616 | tf_op jit(solution)/shard_map/ppermute | solution.py:90
  12.5 8.5 %collective-permute-start.3 = (bf16[128,512]{1,0:T(8,128)(2,1)S(1)}, bf16[128,512]{1,0:T(8,128)(2,1)S(1)}, u32[]{:S(2)}, u32[]{:S(2)}) collective-permute-start(bf16[128,512]{1,0:T(8,128)(2,1)S(1)} %constant_dynamic-update-slice_fusion), channel_id=1, source_target_pairs={{0,32},{16,48},{32,64},{48,80},{64,96},{80,112},{96,0},{112,16},{1... | collective-permute-start | bytes 393224 | tf_op jit(solution)/shard_map/ppermute | solution.py:90
  14.6 17.6 %collective-permute-start.1 = (bf16[128,512]{1,0:T(8,128)(2,1)S(1)}, bf16[128,512]{1,0:T(8,128)(2,1)S(1)}, u32[]{:S(2)}, u32[]{:S(2)}) collective-permute-start(bf16[128,512]{1,0:T(8,128)(2,1)S(1)} %constant_dynamic-update-slice_fusion), channel_id=1, source_target_pairs={{0,64},{16,80},{32,96},{48,112},{64,0},{80,16},{96,32},{112,48},{1... | collective-permute-start | bytes 393224 | tf_op jit(solution)/shard_map/ppermute | solution.py:90
  18.1 14.1 %collective-permute-start.2 = (bf16[128,512]{1,0:T(8,128)(2,1)S(1)}, bf16[128,512]{1,0:T(8,128)(2,1)S(1)}, u32[]{:S(2)}, u32[]{:S(2)}) collective-permute-start(bf16[128,512]{1,0:T(8,128)(2,1)S(1)} %constant_dynamic-update-slice_fusion), channel_id=1, source_target_pairs={{0,96},{16,112},{32,0},{48,16},{64,32},{80,48},{96,64},{112,80},{1... | collective-permute-start | bytes 393224 | tf_op jit(solution)/shard_map/ppermute | solution.py:90
  42.6 0.7 copy-start.1
  42.6 127.3 %all-gather.2.cloned.1.call-start = ((), (), s32[]{:S(2)}) async-start(), calls=%async_computation.2 | async-start | bytes 3899392 | tf_op jit(solution)/shard_map/all_gather | solution.py:119
  43.4 2.0 copy-start
  175.2 10.8 %collective-permute-start.10 = (f32[64,512]{1,0:T(8,128)S(1)}, f32[64,512]{1,0:T(8,128)S(1)}, u32[]{:S(2)}, u32[]{:S(2)}) collective-permute-start(f32[64,512]{1,0:T(8,128)S(1)} %get-tuple-element.10), channel_id=1, source_target_pairs={{0,48},{16,32},{32,80},{48,64},{64,112},{80,96},{96,16},{112,0},{1... | collective-permute-start | bytes 393224 | tf_op jit(solution)/shard_map/ppermute | solution.py:90
  178.9 10.4 %collective-permute-start.4 = (f32[64,512]{1,0:T(8,128)S(1)}, f32[64,512]{1,0:T(8,128)S(1)}, u32[]{:S(2)}, u32[]{:S(2)}) collective-permute-start(f32[64,512]{1,0:T(8,128)S(1)} %get-tuple-element.9), channel_id=1, source_target_pairs={{0,16},{16,0},{32,48},{48,32},{64,80},{80,64},{96,112},{112,96},{1... | collective-permute-start | bytes 393224 | tf_op jit(solution)/shard_map/ppermute | solution.py:90
  179.8 10.2 %collective-permute-start.5 = (f32[64,512]{1,0:T(8,128)S(1)}, f32[64,512]{1,0:T(8,128)S(1)}, u32[]{:S(2)}, u32[]{:S(2)}) collective-permute-start(f32[64,512]{1,0:T(8,128)S(1)} %get-tuple-element.15), channel_id=1, source_target_pairs={{0,96},{16,112},{32,0},{48,16},{64,32},{80,48},{96,64},{112,80},{1... | collective-permute-start | bytes 393224 | tf_op jit(solution)/shard_map/ppermute | solution.py:90
  181.5 8.6 %collective-permute-start.6 = (f32[64,512]{1,0:T(8,128)S(1)}, f32[64,512]{1,0:T(8,128)S(1)}, u32[]{:S(2)}, u32[]{:S(2)}) collective-permute-start(f32[64,512]{1,0:T(8,128)S(1)} %get-tuple-element.14), channel_id=1, source_target_pairs={{0,112},{16,96},{32,16},{48,0},{64,48},{80,32},{96,80},{112,64},{1... | collective-permute-start | bytes 393224 | tf_op jit(solution)/shard_map/ppermute | solution.py:90
  185.3 10.3 %collective-permute-start.7 = (f32[64,512]{1,0:T(8,128)S(1)}, f32[64,512]{1,0:T(8,128)S(1)}, u32[]{:S(2)}, u32[]{:S(2)}) collective-permute-start(f32[64,512]{1,0:T(8,128)S(1)} %get-tuple-element.13), channel_id=1, source_target_pairs={{0,64},{16,80},{32,96},{48,112},{64,0},{80,16},{96,32},{112,48},{1... | collective-permute-start | bytes 393224 | tf_op jit(solution)/shard_map/ppermute | solution.py:90
  186.0 9.6 %collective-permute-start.8 = (f32[64,512]{1,0:T(8,128)S(1)}, f32[64,512]{1,0:T(8,128)S(1)}, u32[]{:S(2)}, u32[]{:S(2)}) collective-permute-start(f32[64,512]{1,0:T(8,128)S(1)} %get-tuple-element.12), channel_id=1, source_target_pairs={{0,80},{16,64},{32,112},{48,96},{64,16},{80,0},{96,48},{112,32},{1... | collective-permute-start | bytes 393224 | tf_op jit(solution)/shard_map/ppermute | solution.py:90
  189.3 8.4 %collective-permute-start.9 = (f32[64,512]{1,0:T(8,128)S(1)}, f32[64,512]{1,0:T(8,128)S(1)}, u32[]{:S(2)}, u32[]{:S(2)}) collective-permute-start(f32[64,512]{1,0:T(8,128)S(1)} %get-tuple-element.11), channel_id=1, source_target_pairs={{0,32},{16,48},{32,64},{48,80},{64,96},{80,112},{96,0},{112,16},{1... | collective-permute-start | bytes 393224 | tf_op jit(solution)/shard_map/ppermute | solution.py:90
Sparse Core Ops, SparseCore 0:
  42.7 89.0 reduce-scatter.1
  134.0 35.9 all-gather.1

commit v13 on v10

--- a/solution.py
+++ b/solution.py
@@ -93,10 +93,10 @@
     n_hi = lax.axis_size("x_hi")
     n_z = lax.axis_size("z")
     hidden_cols = gate_weight.shape[1]
-    pair_rows = jnp.concatenate([tokens, hi_swap(tokens)], axis=0)
-    features = jnp.concatenate(
-        [pair_rows] + [z_shift(pair_rows, s, n_hi) for s in range(1, n_z)], axis=0
+    z_rows = jnp.concatenate(
+        [tokens] + [z_shift(tokens, s, n_hi) for s in range(1, n_z)], axis=0
     )
+    features = jnp.concatenate([z_rows, hi_swap(z_rows)], axis=0)
     pair = gate_up(features, gate_weight, up_weight, gate_keep, up_keep)
     summed = lax.psum_scatter(pair, COL, scatter_dimension=0, tiled=True)
     down_mat = expand(down_weight, down_keep)
@@ -112,7 +112,7 @@
         for i in range(n_hi):
             if s == 0 and i == 0:
                 continue
-            b = s * n_hi + i
+            b = i * n_z + s
             total = total + permute(
                 partial_out[b * t:(b + 1) * t],
                 lambda L, s=s, i=i: ((L // n_hi - s) % n_z) * n_hi + ((L % n_hi) ^ i),

time: 201 us -> 203 us (level)
  transfers between devices with their start and end apart: 13 -> 13, of which waited for: 9 -> 8; matrix products, arithmetic and copies ran while one was open for 2% -> 2% of each run, Pallas kernels for 0% -> 0%
where the time goes in v13:
time: 203 us; the launch traced here: 202 us
  waiting for transfers between devices  136 us (67%)
  starting transfers between devices  24.5 us (12%)
  between operations  13.5 us (7%)
  Pallas kernels  12.4 us (6%)
  other arithmetic  5.84 us (3%)
  matrix products  5.21 us (3%)
  local copies, waits for them, and re-layouts  4.52 us (2%)
    reduce_scatter x1, waiting for transfers between devices, on_device(): summed = lax.psum_scatter(pair, COL, scatter_dimension=0, tiled=True)  84.4 us
    all_gather x1, waiting for transfers between devices, on_device(): hidden_all = lax.all_gather(hidden, COL, axis=0, tiled=True)  36.1 us
    ppermute x11, starting transfers between devices, permute(): lax.ppermute(x, ROW, [(i, dest(i)) for i in range(lax.axis_size(ROW))])  24.5 us
    ppermute x11, waiting for transfers between devices, permute(): lax.ppermute(x, ROW, [(i, dest(i)) for i in range(lax.axis_size(ROW))])  15.5 us
    pallas_call x1, Pallas kernels, gate_up(): pl.pallas_call(functools.partial(_gate_up_kernel, n_half, n_feat), grid_s...  12.4 us
    dot_general x1, matrix products, on_device(): jnp.dot(hidden_all, down_mat, preferred_element_type=jnp.float32)  5.21 us
  transfers between devices with their start and end apart: 13, of which 8 were waited for; matrix products, arithmetic and copies ran while one was open for 2% of the time, Pallas kernels for 0%

profile of v13, /device:TPU:0, one launch (start us, length us, event | category | flops | bytes accessed | tf_op | source)
XLA Modules:
  0.0 202.0 jit_solution(5390265978604976182)
XLA Ops:
  6.5 0.0 reduce-scatter.2.cloned.1.call-start
  6.5 2.0 %collective-permute-start = (bf16[64,512]{1,0:T(8,128)(2,1)}, bf16[64,512]{1,0:T(8,128)(2,1)S(1)}, u32[]{:S(2)}, u32[]{:S(2)}) collective-permute-start(bf16[64,512]{1,0:T(8,128)(2,1)} %param.7), channel_id=1, source_target_pairs={{0,32},{16,48},{32,64},{48,80},{64,96},{80,112},{96,0},{112,16},{1... | collective-permute-start | bytes 196616 | tf_op jit(solution)/shard_map/ppermute | solution.py:80
  8.6 3.6 %collective-permute-start.1 = (bf16[64,512]{1,0:T(8,128)(2,1)}, bf16[64,512]{1,0:T(8,128)(2,1)S(1)}, u32[]{:S(2)}, u32[]{:S(2)}) collective-permute-start(bf16[64,512]{1,0:T(8,128)(2,1)} %param.7), channel_id=1, source_target_pairs={{0,64},{16,80},{32,96},{48,112},{64,0},{80,16},{96,32},{112,48},{1... | collective-permute-start | bytes 196616 | tf_op jit(solution)/shard_map/ppermute | solution.py:80
  12.2 1.0 collective-permute-start.2
  13.2 0.9 constant_dynamic-update-slice_fusion.4
  14.0 0.0 collective-permute-done
  14.0 1.5 collective-permute-done.1
  15.6 1.1 collective-permute-done.2
  16.6 0.9 pad_maximum_fusion
  17.5 3.1 %collective-permute-start.3 = (bf16[256,512]{1,0:T(8,128)(2,1)S(1)}, bf16[256,512]{1,0:T(8,128)(2,1)S(1)}, u32[]{:S(2)}, u32[]{:S(2)}) collective-permute-start(bf16[256,512]{1,0:T(8,128)(2,1)S(1)} %pad_maximum_fusion), channel_id=1, source_target_pairs={{0,16},{16,0},{32,48},{48,32},{64,80},{80,64},{96,112},{112,96},{1... | collective-permute-start | bytes 786440 | tf_op jit(solution)/shard_map/ppermute | solution.py:80
  20.6 5.1 %collective-permute-done.3 = bf16[256,512]{1,0:T(8,128)(2,1)S(1)} collective-permute-done((bf16[256,512]{1,0:T(8,128)(2,1)S(1)}, bf16[256,512]{1,0:T(8,128)(2,1)S(1)}, u32[]{:S(2)}, u32[]{:S(2)}) %collective-permute-start.3) | collective-permute-done | bytes 262176 | tf_op jit(solution)/shard_map/ppermute | solution.py:80
  25.7 0.0 copy-start.1
  25.7 0.8 copy-done.1
  26.5 12.4 %shard_map.73 = f32[512,7168]{1,0:T(8,128)} custom-call(s32[4,28]{1,0:T(4,128)} %gk_ref.1, s32[4,28]{1,0:T(4,128)} %uk_ref.1, bf16[512,512]{1,0:T(8,128)(2,1)} %copy-done.1, bf16[512,3584]{1,0:T(8,128)(2,1)} %gw_ref.1, bf16[512,3584]{1,0:T(8,128)(2,1)} %uw_ref.1), custom_call_target="tpu_custom_call" | custom-call | flops 3758096384 | bytes 22544384 | tf_op jit(solution)/shard_map/pallas_call | solution.py:54
  38.9 0.0 copy-start.2
  38.9 0.0 reduce-scatter.2.cloned.1.call-update
  39.0 0.0 all-gather.2.cloned.1.call-start
  39.0 0.6 copy-done.2
  39.6 0.1 copy.8
  39.7 0.0 copy-start
  39.7 1.0 mul.18
  40.8 1.0 copy-done
  41.8 2.3 %bitcast_multiply_fusion = bf16[3584,512]{1,0:T(8,128)(2,1)} fusion(bf16[3584,512]{1,0:T(8,128)(2,1)S(1)} %copy-done, bf16[448,8,4,128]{3,2,1,0:T(4,128)(2,1)S(1)} %bitcast.6), kind=kLoop, calls=%fused_computation | loop fusion | flops 1835008 | bytes 11010048 | tf_op jit(solution)/shard_map/mul | solution.py:73
  44.1 84.4 %reduce-scatter.2.cloned.1.call-done = f32[32,7168]{1,0:T(8,128)} async-done(((f32[512,7168]{1,0:T(8,128)}), f32[32,7168]{1,0:T(8,128)}) %reduce-scatter.2.cloned.1.call-update) | async-done | bytes 917520 | tf_op jit(solution)/shard_map/reduce_scatter | solution.py:101
  128.5 2.0 multiply_convert_fusion
  130.5 0.0 all-gather.2.cloned.1.call-update
  130.5 36.1 %all-gather.2.cloned.1.call-done = bf16[512,3584]{1,0:T(8,128)(2,1)} async-done(((bf16[32,3584]{1,0:T(8,128)(2,1)}), bf16[512,3584]{1,0:T(8,128)(2,1)}) %all-gather.2.cloned.1.call-update) | async-done | bytes 3670032 | tf_op jit(solution)/shard_map/all_gather | solution.py:105
  166.6 5.2 %fusion.8 = f32[512,512]{1,0:T(8,128)S(1)} fusion(bf16[512,3584]{1,0:T(8,128)(2,1)} %all-gather.2.cloned.1.call-done, bf16[3584,512]{1,0:T(8,128)(2,1)} %bitcast_multiply_fusion), kind=kOutput, calls=%fused_computation.17 | convolution fusion | flops 1879048192 | bytes 8388608 | tf_op jit(solution)/shard_map/dot_general | solution.py:106
  171.8 0.1 fusion.7
  171.9 3.8 %collective-permute-start.10 = (f32[64,512]{1,0:T(8,128)S(1)}, f32[64,512]{1,0:T(8,128)S(1)}, u32[]{:S(2)}, u32[]{:S(2)}) collective-permute-start(f32[64,512]{1,0:T(8,128)S(1)} %get-tuple-element.10), channel_id=1, source_target_pairs={{0,48},{16,32},{32,80},{48,64},{64,112},{80,96},{96,16},{112,0},{1... | collective-permute-start | bytes 393224 | tf_op jit(solution)/shard_map/ppermute | solution.py:80
  175.6 0.8 collective-permute-start.4
  176.5 1.7 collective-permute-start.5
  178.2 3.9 %collective-permute-start.6 = (f32[64,512]{1,0:T(8,128)S(1)}, f32[64,512]{1,0:T(8,128)S(1)}, u32[]{:S(2)}, u32[]{:S(2)}) collective-permute-start(f32[64,512]{1,0:T(8,128)S(1)} %get-tuple-element.14), channel_id=1, source_target_pairs={{0,112},{16,96},{32,16},{48,0},{64,48},{80,32},{96,80},{112,64},{1... | collective-permute-start | bytes 393224 | tf_op jit(solution)/shard_map/ppermute | solution.py:80
  182.0 0.7 collective-permute-start.7
  182.7 0.0 collective-permute-done.10
  182.7 3.3 %collective-permute-start.8 = (f32[64,512]{1,0:T(8,128)S(1)}, f32[64,512]{1,0:T(8,128)S(1)}, u32[]{:S(2)}, u32[]{:S(2)}) collective-permute-start(f32[64,512]{1,0:T(8,128)S(1)} %get-tuple-element.12), channel_id=1, source_target_pairs={{0,80},{16,64},{32,112},{48,96},{64,16},{80,0},{96,48},{112,32},{1... | collective-permute-start | bytes 393224 | tf_op jit(solution)/shard_map/ppermute | solution.py:80
  186.0 0.0 collective-permute-done.4
  186.0 0.7 collective-permute-start.9
  186.7 0.0 collective-permute-done.5
  186.7 0.1 collective-permute-done.6
  186.8 5.6 %collective-permute-done.7 = f32[64,512]{1,0:T(8,128)S(1)} collective-permute-done((f32[64,512]{1,0:T(8,128)S(1)}, f32[64,512]{1,0:T(8,128)S(1)}, u32[]{:S(2)}, u32[]{:S(2)}) %collective-permute-start.7) | collective-permute-done | bytes 131104 | tf_op jit(solution)/shard_map/ppermute | solution.py:80
  192.3 0.0 collective-permute-done.8
  192.4 2.1 %collective-permute-done.9 = f32[64,512]{1,0:T(8,128)S(1)} collective-permute-done((f32[64,512]{1,0:T(8,128)S(1)}, f32[64,512]{1,0:T(8,128)S(1)}, u32[]{:S(2)}, u32[]{:S(2)}) %collective-permute-start.9) | collective-permute-done | bytes 131104 | tf_op jit(solution)/shard_map/ppermute | solution.py:80
  194.5 0.7 fusion.6
  (5 shorter events, 0.0 us)
Async XLA Ops:
  6.5 121.9 %reduce-scatter.2.cloned.1.call-start = ((), (), s32[]{:S(2)}) async-start(), calls=%async_computation.1 | async-start | bytes 15597568 | tf_op jit(solution)/shard_map/reduce_scatter | solution.py:101
  6.5 7.5 %collective-permute-start = (bf16[64,512]{1,0:T(8,128)(2,1)}, bf16[64,512]{1,0:T(8,128)(2,1)S(1)}, u32[]{:S(2)}, u32[]{:S(2)}) collective-permute-start(bf16[64,512]{1,0:T(8,128)(2,1)} %param.7), channel_id=1, source_target_pairs={{0,32},{16,48},{32,64},{48,80},{64,96},{80,112},{96,0},{112,16},{1... | collective-permute-start | bytes 196616 | tf_op jit(solution)/shard_map/ppermute | solution.py:80
  8.6 7.0 %collective-permute-start.1 = (bf16[64,512]{1,0:T(8,128)(2,1)}, bf16[64,512]{1,0:T(8,128)(2,1)S(1)}, u32[]{:S(2)}, u32[]{:S(2)}) collective-permute-start(bf16[64,512]{1,0:T(8,128)(2,1)} %param.7), channel_id=1, source_target_pairs={{0,64},{16,80},{32,96},{48,112},{64,0},{80,16},{96,32},{112,48},{1... | collective-permute-start | bytes 196616 | tf_op jit(solution)/shard_map/ppermute | solution.py:80
  12.2 4.5 %collective-permute-start.2 = (bf16[64,512]{1,0:T(8,128)(2,1)}, bf16[64,512]{1,0:T(8,128)(2,1)S(1)}, u32[]{:S(2)}, u32[]{:S(2)}) collective-permute-start(bf16[64,512]{1,0:T(8,128)(2,1)} %param.7), channel_id=1, source_target_pairs={{0,96},{16,112},{32,0},{48,16},{64,32},{80,48},{96,64},{112,80},{1... | collective-permute-start | bytes 196616 | tf_op jit(solution)/shard_map/ppermute | solution.py:80
  17.5 8.2 %collective-permute-start.3 = (bf16[256,512]{1,0:T(8,128)(2,1)S(1)}, bf16[256,512]{1,0:T(8,128)(2,1)S(1)}, u32[]{:S(2)}, u32[]{:S(2)}) collective-permute-start(bf16[256,512]{1,0:T(8,128)(2,1)S(1)} %pad_maximum_fusion), channel_id=1, source_target_pairs={{0,16},{16,0},{32,48},{48,32},{64,80},{80,64},{96,112},{112,96},{1... | collective-permute-start | bytes 786440 | tf_op jit(solution)/shard_map/ppermute | solution.py:80
  25.7 0.8 copy-start.1
  38.9 0.7 copy-start.2
  39.0 127.6 %all-gather.2.cloned.1.call-start = ((), (), s32[]{:S(2)}) async-start(), calls=%async_computation.2 | async-start | bytes 3899392 | tf_op jit(solution)/shard_map/all_gather | solution.py:105
  39.7 2.0 %copy-start = (bf16[3584,512]{1,0:T(8,128)(2,1)S(1)}, bf16[3584,512]{1,0:T(8,128)(2,1)}, u32[]{:S(2)}) copy-start(bf16[3584,512]{1,0:T(8,128)(2,1)} %param.10) | copy-start | bytes 11010052
  171.9 10.8 %collective-permute-start.10 = (f32[64,512]{1,0:T(8,128)S(1)}, f32[64,512]{1,0:T(8,128)S(1)}, u32[]{:S(2)}, u32[]{:S(2)}) collective-permute-start(f32[64,512]{1,0:T(8,128)S(1)} %get-tuple-element.10), channel_id=1, source_target_pairs={{0,48},{16,32},{32,80},{48,64},{64,112},{80,96},{96,16},{112,0},{1... | collective-permute-start | bytes 393224 | tf_op jit(solution)/shard_map/ppermute | solution.py:80
  175.6 10.4 %collective-permute-start.4 = (f32[64,512]{1,0:T(8,128)S(1)}, f32[64,512]{1,0:T(8,128)S(1)}, u32[]{:S(2)}, u32[]{:S(2)}) collective-permute-start(f32[64,512]{1,0:T(8,128)S(1)} %get-tuple-element.9), channel_id=1, source_target_pairs={{0,16},{16,0},{32,48},{48,32},{64,80},{80,64},{96,112},{112,96},{1... | collective-permute-start | bytes 393224 | tf_op jit(solution)/shard_map/ppermute | solution.py:80
  176.5 10.2 %collective-permute-start.5 = (f32[64,512]{1,0:T(8,128)S(1)}, f32[64,512]{1,0:T(8,128)S(1)}, u32[]{:S(2)}, u32[]{:S(2)}) collective-permute-start(f32[64,512]{1,0:T(8,128)S(1)} %get-tuple-element.15), channel_id=1, source_target_pairs={{0,96},{16,112},{32,0},{48,16},{64,32},{80,48},{96,64},{112,80},{1... | collective-permute-start | bytes 393224 | tf_op jit(solution)/shard_map/ppermute | solution.py:80
  178.2 8.6 %collective-permute-start.6 = (f32[64,512]{1,0:T(8,128)S(1)}, f32[64,512]{1,0:T(8,128)S(1)}, u32[]{:S(2)}, u32[]{:S(2)}) collective-permute-start(f32[64,512]{1,0:T(8,128)S(1)} %get-tuple-element.14), channel_id=1, source_target_pairs={{0,112},{16,96},{32,16},{48,0},{64,48},{80,32},{96,80},{112,64},{1... | collective-permute-start | bytes 393224 | tf_op jit(solution)/shard_map/ppermute | solution.py:80
  182.0 10.3 %collective-permute-start.7 = (f32[64,512]{1,0:T(8,128)S(1)}, f32[64,512]{1,0:T(8,128)S(1)}, u32[]{:S(2)}, u32[]{:S(2)}) collective-permute-start(f32[64,512]{1,0:T(8,128)S(1)} %get-tuple-element.13), channel_id=1, source_target_pairs={{0,64},{16,80},{32,96},{48,112},{64,0},{80,16},{96,32},{112,48},{1... | collective-permute-start | bytes 393224 | tf_op jit(solution)/shard_map/ppermute | solution.py:80
  182.7 9.6 %collective-permute-start.8 = (f32[64,512]{1,0:T(8,128)S(1)}, f32[64,512]{1,0:T(8,128)S(1)}, u32[]{:S(2)}, u32[]{:S(2)}) collective-permute-start(f32[64,512]{1,0:T(8,128)S(1)} %get-tuple-element.12), channel_id=1, source_target_pairs={{0,80},{16,64},{32,112},{48,96},{64,16},{80,0},{96,48},{112,32},{1... | collective-permute-start | bytes 393224 | tf_op jit(solution)/shard_map/ppermute | solution.py:80
  186.0 8.4 %collective-permute-start.9 = (f32[64,512]{1,0:T(8,128)S(1)}, f32[64,512]{1,0:T(8,128)S(1)}, u32[]{:S(2)}, u32[]{:S(2)}) collective-permute-start(f32[64,512]{1,0:T(8,128)S(1)} %get-tuple-element.11), channel_id=1, source_target_pairs={{0,32},{16,48},{32,64},{48,80},{64,96},{80,112},{96,0},{112,16},{1... | collective-permute-start | bytes 393224 | tf_op jit(solution)/shard_map/ppermute | solution.py:80
Sparse Core Ops, SparseCore 0:
  39.1 89.3 reduce-scatter.1
  130.6 35.9 all-gather.1
